TPU v7x, 256 devices: a whole 4x4x8 slice. The times are simulated.
256 devices in a mesh: grp: 2 (over core), req: 128 (over y, z, x).
Axes of the slice: x: 4, y: 4, z: 8, core: 2. Of those that a mesh axis runs over, the one named last changes fastest.
Arguments:
- new_qkv: bfloat16 [1024, 32, 3840], P(('grp', 'req')), parts along dimension 0, may hold values from -5 to 5
- cache_kv: bfloat16 [1024, 32, 2560], P(('grp', 'req')), parts along dimension 0, may hold values from -5 to 5
- resid: bfloat16 [1024, 32, 1280], P(('grp', 'req')), parts along dimension 0, may hold values from -6 to 6
- span_len: int32 [1024], P(('grp', 'req')), parts along dimension 0, may hold values from 1 to 32
- cache_len: int32 [1024], P(('grp', 'req')), parts along dimension 0, may hold values from 0 to 32
- series_perm: int32 [1024], P(('grp', 'req')), parts along dimension 0, may hold values from 0 to 511, each once
- ff_gain: float32 [1280], replicated, may hold values from 0.5 to 1.5
- w_up: bfloat16 [1280, 1280], replicated, may hold values from -0.15625 to 0.15625
- w_down: bfloat16 [1280, 1280], replicated, may hold values from -0.15625 to 0.15625
Outputs:
- packed_out: bfloat16 [32768, 1280], P(('grp', 'req')), parts along dimension 0
There are 2 independent parts, one for each index of `grp`. A program takes and returns all parts, laid end to end along the dimension named above; an argument that names none is the same for every part. Nothing has to cross between parts.
Inputs may be any that keep to these rules, and one draw needn't show every extreme that they name: `series_perm`: each series id appears once.
All inputs are finite; a program needn't handle non-finite values.
Results may differ from a plain program's by a relative error of at most 0.0055.
Values may be sent and summed in bfloat16 or wider, within the bound.
No kernel may reach another device: no remote copies, remote signals or barrier semaphores. Data moves between devices by JAX's collectives and lax.ppermute only.
A program may use at most 64 MiB of HBM per device.

v0:
```python
import jax
import jax.numpy as jnp
from jax import lax
from jax.sharding import PartitionSpec as P

H = 16


def attend_block(new_qkv, cache_kv, cache_len):
    series_here, span_slots, triple = new_qkv.shape
    width = triple // 3
    head_size = width // H
    cache_slots = cache_kv.shape[1]
    queries = new_qkv[:, :, :width].reshape(series_here, span_slots, H, head_size)
    key_rows = jnp.concatenate([cache_kv[:, :, :width], new_qkv[:, :, width : 2 * width]], axis=1)
    key_rows = key_rows.reshape(series_here, cache_slots + span_slots, H, head_size)
    value_rows = jnp.concatenate([cache_kv[:, :, width:], new_qkv[:, :, 2 * width :]], axis=1)
    value_rows = value_rows.reshape(series_here, cache_slots + span_slots, H, head_size)
    scores = jnp.einsum(
        "sthd,skhd->shtk", queries, key_rows, preferred_element_type=jnp.float32
    ) * head_size ** (-0.5)
    key_pos = jnp.arange(cache_slots + span_slots, dtype=jnp.int32)[None, None, None, :]
    row_pos = jnp.arange(span_slots, dtype=jnp.int32)[None, None, :, None]
    visible = jnp.where(
        key_pos < cache_slots,
        key_pos < cache_len[:, None, None, None],
        key_pos - cache_slots <= row_pos,
    )
    scores = jnp.where(visible, scores, -1e30)
    row_top = jnp.max(scores, axis=-1, keepdims=True)
    expo_terms = jnp.exp(scores - row_top)
    weights = (expo_terms / jnp.sum(expo_terms, axis=-1, keepdims=True)).astype(jnp.bfloat16)
    attended = jnp.einsum(
        "shtk,skhd->sthd", weights, value_rows, preferred_element_type=jnp.float32
    )
    return attended.reshape(series_here, span_slots, width)


def feed_forward(hidden, ff_gain, w_up, w_down):
    wide_rows = hidden.astype(jnp.float32)
    normed = (
        wide_rows
        * lax.rsqrt(jnp.mean(wide_rows * wide_rows, axis=-1, keepdims=True) + 1e-06)
        * ff_gain
    ).astype(jnp.bfloat16)
    activated = jax.nn.silu(jnp.dot(normed, w_up, preferred_element_type=jnp.float32)).astype(
        jnp.bfloat16
    )
    return (wide_rows + jnp.dot(activated, w_down, preferred_element_type=jnp.float32)).astype(
        jnp.bfloat16
    )


def local(new_qkv, cache_kv, resid, span_len, cache_len, series_perm, ff_gain, w_up, w_down):
    group_size = lax.axis_size("req")
    series_here, span_slots, triple = new_qkv.shape
    width = resid.shape[2]
    rows_here = series_here * span_slots
    gathered_len, gathered_perm = (
        lax.all_gather(span_len, "req", axis=0, tiled=True),
        lax.all_gather(series_perm, "req", axis=0, tiled=True),
    )
    series_total = gathered_len.shape[0]
    count_by_id = jnp.zeros((series_total,), jnp.int32).at[gathered_perm].set(gathered_len)
    start_by_id = jnp.cumsum(count_by_id) - count_by_id
    slot_index = jnp.arange(span_slots, dtype=jnp.int32)
    packed_index = start_by_id[series_perm][:, None] + slot_index[None, :]
    live_slot = slot_index[None, :] < span_len[:, None]
    per_series = (span_slots + group_size - 1) // group_size
    slot_depth = series_here * per_series
    target_dev = packed_index % group_size
    send_place = (
        target_dev * slot_depth
        + jnp.arange(series_here, dtype=jnp.int32)[:, None] * per_series
        + slot_index[None, :] // group_size
    )
    send_place = jnp.where(live_slot, send_place, group_size * slot_depth).reshape(-1)
    token_tags = (
        jnp.full((group_size * slot_depth,), -1, jnp.int32)
        .at[send_place]
        .set(jnp.where(live_slot, packed_index, -1).reshape(-1), mode="drop")
        .reshape(group_size, slot_depth)
    )
    attended = attend_block(new_qkv, cache_kv, cache_len)
    hidden = (resid.astype(jnp.float32) + attended).astype(jnp.bfloat16).reshape(rows_here, width)
    placed = (
        jnp.zeros((group_size * slot_depth, width), hidden.dtype)
        .at[send_place]
        .set(hidden, mode="drop")
    )
    arrived = lax.all_to_all(
        placed.reshape(group_size, slot_depth, width),
        "req",
        split_axis=0,
        concat_axis=0,
        tiled=True,
    )
    arrived_tags = lax.all_to_all(token_tags, "req", split_axis=0, concat_axis=0, tiled=True)
    local_row = jnp.where(arrived_tags >= 0, arrived_tags // group_size, rows_here).reshape(-1)
    return feed_forward(
        jnp.zeros((rows_here, width), jnp.bfloat16)
        .at[local_row]
        .set(arrived.reshape(-1, width), mode="drop"),
        ff_gain,
        w_up,
        w_down,
    )


def solution(mesh):
    in_specs = (
        P(("grp", "req"), None, None),
        P(("grp", "req"), None, None),
        P(("grp", "req"), None, None),
        P(("grp", "req")),
        P(("grp", "req")),
        P(("grp", "req")),
        P(),
        P(),
        P(),
    )
    out_specs = P(("grp", "req"), None)
    return jax.shard_map(local, mesh=mesh, in_specs=in_specs, out_specs=out_specs, check_vma=False)
```

profile of v0, /device:TPU:8, one launch (start us, length us, event | category | flops | bytes accessed | tf_op | source)
XLA Modules:
  0.0 140.6 jit_solution(3549287398630842972)
XLA Ops:
  0.0 0.0 copy-start
  0.0 0.8 compare_select_fusion.7
  0.8 0.9 iota_compare_fusion.2
  1.7 1.3 dynamic-slice
  3.6 0.9 dynamic-update-slice
  4.5 0.8 dynamic-update-slice.1
  5.3 29.6 %all-reduce.2 = (s32[512]{0:T(512)S(1)}, s32[512]{0:T(512)S(1)}) all-reduce(s32[512]{0:T(512)S(1)} %dynamic-update-slice, s32[512]{0:T(512)S(1)} %dynamic-update-slice.1), channel_id=1, replica_groups=mesh['grp'=2,'req'=128] {'req'}, use_global_device_ids=true, to_apply=%add | all-reduce | flops 1024 | bytes 8192
  35.0 2.4 %scatter_custom_fusion = s32[512]{0:T(512)S(1)} fusion(s32[512]{0:T(512)S(1)} %compare_select_fusion.2, s32[512]{0:T(512)S(1)} %get-tuple-element.6, s32[]{:T(128)} %constant.63.clone.1), kind=kCustom, calls=%fused_computation.61 | custom fusion | bytes 2052 | tf_op jit(solution)/shard_map/scatter | solution.py:64
  37.4 0.3 reduce-window.9
  37.7 0.1 slice.22
  37.8 0.1 slice_reduce_fusion
  38.0 0.1 bitcast_subtract_fusion
  38.0 0.6 gather_fusion
  38.7 0.7 broadcast_select_fusion.1
  39.4 0.1 add.152
  39.5 0.1 add.158
  39.6 0.1 add.155
  39.7 0.1 lt.90
  39.8 0.1 reshape.394
  39.9 1.0 scatter_custom_fusion.1
  40.8 0.7 all_to_all.11
  41.6 7.2 %all-to-all-start = ((s32[128,1,4]{2,1,0:T(1,128)}), s32[128,1,4]{2,1,0:T(1,128)S(1)}, u32[]{:S(2)}, u32[]{:S(2)}) async-start(s32[128,1,4]{2,1,0:T(1,128)} %bitcast.4), calls=%async_computation | async-start | bytes 131072 | tf_op jit(solution)/shard_map/all_to_all | solution.py:98
  48.7 0.0 copy-start.2
  48.8 2.0 %fusion.39 = (bf16[4,32,1280]{2,1,0:T(8,128)(2,1)}, bf16[4,32,1280]{2,1,0:T(8,128)(2,1)S(1)}, bf16[4,32,1280]{2,1,0:T(8,128)(2,1)S(1)}) fusion(bf16[4,32,3840]{2,1,0:T(8,128)(2,1)} %param.9), kind=kLoop, calls=%fused_computation.75 | loop fusion | bytes 1966080 | tf_op jit(solution)/shard_map/slice | solution.py:14
  50.8 0.0 copy-done.2
  50.9 1.2 pad_maximum_fusion
  52.0 0.0 copy-start.4
  52.0 3.3 %reshape.368 = bf16[4,64,16,80]{3,2,1,0:T(8,128)(2,1)} reshape(bf16[4,64,1280]{2,1,0:T(8,128)(2,1)} %get-tuple-element.14) | data formatting | bytes 1310720 | tf_op jit(solution)/shard_map/reshape | solution.py:16
  55.3 2.6 %reshape.369 = bf16[4,32,16,80]{3,2,1,0:T(8,128)(2,1)} reshape(bf16[4,32,1280]{2,1,0:T(8,128)(2,1)} %get-tuple-element.7) | data formatting | bytes 655360 | tf_op jit(solution)/shard_map/reshape | solution.py:14
  57.9 0.0 copy-done.4
  57.9 0.1 iota_compare_fusion.1
  58.0 2.0 %fusion.5 = f32[4,16,32,64]{3,2,1,0:T(8,128)S(1)} fusion(bf16[4,64,16,80]{3,2,1,0:T(8,128)(2,1)} %reshape.368, bf16[4,32,16,80]{3,2,1,0:T(8,128)(2,1)} %reshape.369, pred[4,32,64]{2,1,0:T(8,128)(4,1)S(1)} %broadcast_select_fusion), kind=kOutput, calls=%fused_computation.12 | convolution fusion | flops 21233664 | bytes 1515520 | tf_op jit(solution)/shard_map/sthd,skhd->shtk/dot_general | solution.py:19
  60.0 0.0 copy-start.1
  60.0 1.0 copy-done.1
  61.1 0.7 fusion.41
  61.7 3.3 %reshape.367 = bf16[4,64,16,80]{3,2,1,0:T(8,128)(2,1)} reshape(bf16[4,64,1280]{2,1,0:T(8,128)(2,1)} %get-tuple-element.15) | data formatting | bytes 1310720 | tf_op jit(solution)/shard_map/reshape | solution.py:18
  65.0 6.6 %convolution_bitcast_fusion = f32[4,32,16,80]{3,1,2,0:T(8,128)} fusion(bf16[4,64,16,80]{3,2,1,0:T(8,128)(2,1)} %reshape.367, f32[4,16,32]{2,1,0:T(8,128)S(1)} %fusion.41, f32[4,16,32,64]{3,2,1,0:T(8,128)} %copy-done.1), kind=kOutput, calls=%fused_computation.13 | convolution fusion | flops 21366848 | bytes 1843200 | tf_op jit(solution)/shard_map/shtk,skhd->sthd/dot_general | solution.py:33
  71.6 2.8 %copy.18 = f32[4,32,16,80]{3,2,1,0:T(8,128)} copy(f32[4,32,16,80]{3,1,2,0:T(8,128)} %convolution_bitcast_fusion) | data formatting | bytes 1310720 | tf_op jit(solution)/shard_map/shtk,skhd->sthd/transpose | solution.py:33
  74.4 2.5 %reshape.370 = f32[4,32,1280]{2,1,0:T(8,128)} reshape(f32[4,32,16,80]{3,2,1,0:T(8,128)} %copy.18) | data formatting | bytes 1310720 | tf_op jit(solution)/shard_map/reshape | solution.py:36
  76.9 1.9 %add_convert_fusion = bf16[4,32,1280]{2,1,0:T(8,128)(2,1)} fusion(f32[4,32,1280]{2,1,0:T(8,128)} %reshape.370, bf16[4,32,1280]{2,1,0:T(8,128)(2,1)} %param.11), kind=kLoop, calls=%fused_computation.25 | loop fusion | flops 491520 | bytes 1310720 | tf_op jit(solution)/shard_map/convert_element_type | solution.py:85
  78.9 2.9 %scatter_custom_fusion.2 = bf16[512,1280]{1,0:T(8,128)(2,1)} fusion(s32[128]{0:T(128)S(1)} %fusion.36, bf16[128,1280]{1,0:T(8,128)(2,1)} %bitcast.21, bf16[]{:T(256)} %constant.38.clone.1), kind=kCustom, calls=%fused_computation.26 | custom fusion | bytes 1311232 | tf_op jit(solution)/shard_map/scatter | solution.py:89
  81.8 3.5 %reshape.372 = bf16[128,4,1280]{2,1,0:T(4,128)(2,1)} reshape(bf16[512,1280]{1,0:T(8,128)(2,1)} %scatter_custom_fusion.2) | data formatting | bytes 2621440 | tf_op jit(solution)/shard_map/reshape | solution.py:92
  85.3 0.0 all-to-all-done
  85.3 14.2 %all-to-all-start.1 = ((bf16[128,4,1280]{2,1,0:T(4,128)(2,1)}), bf16[128,4,1280]{2,1,0:T(4,128)(2,1)}, u32[]{:S(2)}, u32[]{:S(2)}) async-start(bf16[128,4,1280]{2,1,0:T(4,128)(2,1)} %reshape.372), calls=%async_computation.1 | async-start | bytes 2621440 | tf_op jit(solution)/shard_map/all_to_all | solution.py:91
  99.5 0.5 broadcast.333
  100.0 0.8 reduce.5
  100.8 0.1 all_to_all.13
  100.9 0.0 copy-start.3
  100.9 27.0 %all-to-all-done.1 = bf16[128,4,1280]{2,1,0:T(4,128)(2,1)} async-done(((bf16[128,4,1280]{2,1,0:T(4,128)(2,1)}), bf16[128,4,1280]{2,1,0:T(4,128)(2,1)}, u32[]{:S(2)}, u32[]{:S(2)}) %all-to-all-start.1) | async-done | bytes 1310752 | tf_op jit(solution)/shard_map/all_to_all | solution.py:91
  127.9 3.4 %reshape.410 = bf16[512,1280]{1,0:T(8,128)(2,1)} reshape(bf16[128,4,1280]{2,1,0:T(4,128)(2,1)} %all-to-all-done.1) | data formatting | bytes 2621440 | tf_op jit(solution)/shard_map/reshape | solution.py:103
  131.3 4.1 %scatter_custom_fusion.3 = bf16[128,1280]{1,0:T(8,128)(2,1)} fusion(s32[512]{0:T(512)S(1)} %bitcast.23, bf16[512,1280]{1,0:T(8,128)(2,1)} %reshape.410, bf16[]{:T(256)} %constant.38.clone.1), kind=kCustom, calls=%fused_computation.34 | custom fusion | bytes 328192 | tf_op jit(solution)/shard_map/scatter | solution.py:103
  135.4 1.1 fusion.8
  136.6 0.0 copy-done
  136.6 0.0 copy-done.3
  136.6 4.0 %fusion.1 = bf16[128,1280]{1,0:T(8,128)(2,1)} fusion(bf16[1280,1280]{1,0:T(8,128)(2,1)S(1)} %copy-done, bf16[128,1280]{1,0:T(8,128)(2,1)} %scatter_custom_fusion.3, bf16[1280,1280]{1,0:T(8,128)(2,1)} %param.16, f32[1280]{0:T(1024)S(1)} %copy-done.3, f32[128]{0:T(128)S(1)} %add_rsqrt_fusion), kind=kOutput, calls=%fused_computation.7 | convolution fusion | flops 840826880 | bytes 7214592 | tf_op jit(solution)/shard_map/dot_general | solution.py:49
  (16 shorter events, 0.2 us)
Async XLA Ops:
  0.0 136.6 %copy-start = (bf16[1280,1280]{1,0:T(8,128)(2,1)S(1)}, bf16[1280,1280]{1,0:T(8,128)(2,1)}, u32[]{:S(2)}) copy-start(bf16[1280,1280]{1,0:T(8,128)(2,1)} %param.17) | copy-start | bytes 9830404
  41.6 43.7 %all-to-all-start = ((s32[128,1,4]{2,1,0:T(1,128)}), s32[128,1,4]{2,1,0:T(1,128)S(1)}, u32[]{:S(2)}, u32[]{:S(2)}) async-start(s32[128,1,4]{2,1,0:T(1,128)} %bitcast.4), calls=%async_computation | async-start | bytes 131072 | tf_op jit(solution)/shard_map/all_to_all | solution.py:98
  48.7 2.1 %copy-start.2 = (bf16[4,32,2560]{2,1,0:T(8,128)(2,1)S(1)}, bf16[4,32,2560]{2,1,0:T(8,128)(2,1)}, u32[]{:S(2)}) copy-start(bf16[4,32,2560]{2,1,0:T(8,128)(2,1)} %param.10) | copy-start | bytes 1966084
  52.0 5.9 %copy-start.4 = (s32[4]{0:T(128)S(1)}, s32[4]{0:T(128)}, u32[]{:S(2)}) copy-start(s32[4]{0:T(128)} %param.13) | copy-start | bytes 52
  60.0 1.0 copy-start.1
  85.3 42.7 %all-to-all-start.1 = ((bf16[128,4,1280]{2,1,0:T(4,128)(2,1)}), bf16[128,4,1280]{2,1,0:T(4,128)(2,1)}, u32[]{:S(2)}, u32[]{:S(2)}) async-start(bf16[128,4,1280]{2,1,0:T(4,128)(2,1)} %reshape.372), calls=%async_computation.1 | async-start | bytes 2621440 | tf_op jit(solution)/shard_map/all_to_all | solution.py:91
  100.9 35.6 %copy-start.3 = (f32[1280]{0:T(1024)S(1)}, f32[1280]{0:T(1024)}, u32[]{:S(2)}) copy-start(f32[1280]{0:T(1024)} %param.15) | copy-start | bytes 15364
where the time goes:
time: 142 us; the launch traced here: 141 us
  local copies, waits for them, and re-layouts  40.5 us (29%)
  blocking collectives  29.6 us (21%)
  waiting for transfers between devices  27 us (19%)
  starting transfers between devices  21.4 us (15%)
  matrix products  12.6 us (9%)
  other arithmetic  8.71 us (6%)
    unnamed x1, blocking collectives  29.6 us
    all_to_all x1, waiting for transfers between devices, local(): lax.all_to_all(placed.reshape(group_size, slot_depth, width), 'req', spli...  27 us
    all_to_all x1, starting transfers between devices, local(): lax.all_to_all(placed.reshape(group_size, slot_depth, width), 'req', spli...  14.2 us
    all_to_all x1, starting transfers between devices, local(): lax.all_to_all(token_tags, 'req', split_axis=0, concat_axis=0, tiled=True)  7.16 us
    dot_general x1, matrix products, attend_block(): jnp.einsum('shtk,skhd->sthd', weights, value_rows, preferred_element_type...  6.56 us
    scatter x1, local copies, waits for them, and re-layouts, local(): return feed_forward(jnp.zeros((rows_here, width), jnp.bfloat16).at[local_...  4.12 us
    unnamed x13, local copies, waits for them, and re-layouts  4.01 us
    dot_general x1, matrix products, feed_forward(): jnp.dot(activated, w_down, preferred_element_type=jnp.float32)  4.01 us
  transfers between devices with their start and end apart: 2, of which 1 were waited for; matrix products, arithmetic and copies ran while one was open for 26% of the time, Pallas kernels for 0%

commit v1 on v0

v1 whole, which is shorter than its diff:
```python
import jax
import jax.numpy as jnp
from jax import lax
from jax.experimental import pallas as pl
from jax.experimental.pallas import tpu as pltpu
from jax.sharding import PartitionSpec as P

H = 16


def block_kernel(cache_len_ref, qkv_ref, cache_ref, resid_ref, gain_ref, up_ref, down_ref, out_ref):
    s = pl.program_id(0)
    span_slots = qkv_ref.shape[1]
    cache_slots = cache_ref.shape[1]
    width = resid_ref.shape[2]
    head_size = width // H
    q = qkv_ref[0, :, 0:width]
    k_new = qkv_ref[0, :, width : 2 * width]
    v_new = qkv_ref[0, :, 2 * width : 3 * width]
    k_old = cache_ref[0, :, 0:width]
    v_old = cache_ref[0, :, width : 2 * width]
    col_head = lax.broadcasted_iota(jnp.int32, (H, 1, width), 2) // head_size
    head_id = lax.broadcasted_iota(jnp.int32, (H, 1, width), 0)
    head_mask = col_head == head_id
    q_heads = jnp.where(head_mask, q[None], jnp.zeros((), q.dtype)).reshape(H * span_slots, width)
    dims = (((1,), (1,)), ((), ()))
    scale = head_size ** (-0.5)
    s_old = lax.dot_general(q_heads, k_old, dims, preferred_element_type=jnp.float32) * scale
    s_new = lax.dot_general(q_heads, k_new, dims, preferred_element_type=jnp.float32) * scale
    rows = H * span_slots
    row_t = lax.broadcasted_iota(jnp.int32, (rows, span_slots), 0) % span_slots
    key_new = lax.broadcasted_iota(jnp.int32, (rows, span_slots), 1)
    key_old = lax.broadcasted_iota(jnp.int32, (rows, cache_slots), 1)
    s_old = jnp.where(key_old < cache_len_ref[s], s_old, -1e30)
    s_new = jnp.where(key_new <= row_t, s_new, -1e30)
    top = jnp.maximum(jnp.max(s_old, axis=1, keepdims=True), jnp.max(s_new, axis=1, keepdims=True))
    e_old = jnp.exp(s_old - top)
    e_new = jnp.exp(s_new - top)
    denom = jnp.sum(e_old, axis=1, keepdims=True) + jnp.sum(e_new, axis=1, keepdims=True)
    w_old = (e_old / denom).astype(jnp.bfloat16)
    w_new = (e_new / denom).astype(jnp.bfloat16)
    mixed = jnp.dot(w_old, v_old, preferred_element_type=jnp.float32) + jnp.dot(
        w_new, v_new, preferred_element_type=jnp.float32
    )
    mixed = mixed.reshape(H, span_slots, width)
    attended = jnp.sum(jnp.where(head_mask, mixed, 0.0), axis=0)
    hidden = (resid_ref[0].astype(jnp.float32) + attended).astype(jnp.bfloat16)
    wide_rows = hidden.astype(jnp.float32)
    normed = (
        wide_rows
        * lax.rsqrt(jnp.mean(wide_rows * wide_rows, axis=-1, keepdims=True) + 1e-06)
        * gain_ref[...]
    ).astype(jnp.bfloat16)
    activated = jax.nn.silu(
        jnp.dot(normed, up_ref[...], preferred_element_type=jnp.float32)
    ).astype(jnp.bfloat16)
    out_ref[0] = (
        wide_rows + jnp.dot(activated, down_ref[...], preferred_element_type=jnp.float32)
    ).astype(out_ref.dtype)


def layer_block(new_qkv, cache_kv, resid, cache_len, ff_gain, w_up, w_down):
    series_here, span_slots, triple = new_qkv.shape
    cache_slots, pair = cache_kv.shape[1], cache_kv.shape[2]
    width = resid.shape[2]
    grid_spec = pltpu.PrefetchScalarGridSpec(
        num_scalar_prefetch=1,
        grid=(series_here,),
        in_specs=[
            pl.BlockSpec((1, span_slots, triple), lambda s, cl: (s, 0, 0)),
            pl.BlockSpec((1, cache_slots, pair), lambda s, cl: (s, 0, 0)),
            pl.BlockSpec((1, span_slots, width), lambda s, cl: (s, 0, 0)),
            pl.BlockSpec((1, width), lambda s, cl: (0, 0)),
            pl.BlockSpec(w_up.shape, lambda s, cl: (0, 0)),
            pl.BlockSpec(w_down.shape, lambda s, cl: (0, 0)),
        ],
        out_specs=pl.BlockSpec((1, span_slots, width), lambda s, cl: (s, 0, 0)),
    )
    return pl.pallas_call(
        block_kernel,
        grid_spec=grid_spec,
        out_shape=jax.ShapeDtypeStruct((series_here, span_slots, width), jnp.bfloat16),
        compiler_params=pltpu.CompilerParams(dimension_semantics=("arbitrary",)),
    )(cache_len, new_qkv, cache_kv, resid, ff_gain.reshape(1, width), w_up, w_down)


def local(new_qkv, cache_kv, resid, span_len, cache_len, series_perm, ff_gain, w_up, w_down):
    group_size = lax.axis_size("req")
    me = lax.axis_index("req")
    series_here, span_slots, triple = new_qkv.shape
    width = resid.shape[2]
    gathered = lax.all_gather(jnp.stack([span_len, series_perm]), "req", axis=1, tiled=True)
    all_len, all_perm = gathered[0], gathered[1]
    series_total = all_len.shape[0]
    earlier = all_perm[None, :] < all_perm[:, None]
    all_start = jnp.sum(jnp.where(earlier, all_len[None, :], 0), axis=1)

    layer_out = layer_block(new_qkv, cache_kv, resid, cache_len, ff_gain, w_up, w_down)

    my_start = lax.dynamic_slice(all_start, (me * series_here,), (series_here,))
    target = jnp.arange(group_size, dtype=jnp.int32)[None, :, None]
    slot = jnp.arange(span_slots, dtype=jnp.int32)[None, None, :]
    my_offset = (target - my_start[:, None, None]) % group_size
    pick = (my_offset == slot) & (slot < span_len[:, None, None])
    pick = pick.astype(jnp.bfloat16)
    placed = jnp.concatenate(
        [
            jnp.dot(pick[i], layer_out[i], preferred_element_type=jnp.float32).astype(jnp.bfloat16)
            for i in range(series_here)
        ],
        axis=1,
    )
    arrived = lax.all_to_all(placed, "req", split_axis=0, concat_axis=0, tiled=True)

    src_start = all_start.reshape(group_size, series_here)
    src_len = all_len.reshape(group_size, series_here)
    src_t = (me - src_start) % group_size
    src_row = (src_start + src_t) // group_size
    src_row = jnp.where(src_t < src_len, src_row, -1)
    rows_here = series_here * span_slots
    out_row = jnp.arange(rows_here, dtype=jnp.int32)[:, None]
    result = jnp.zeros((rows_here, width), jnp.float32)
    for i in range(series_here):
        gather_i = (src_row[None, :, i] == out_row).astype(jnp.bfloat16)
        result = result + jnp.dot(
            gather_i, arrived[:, i * width : (i + 1) * width], preferred_element_type=jnp.float32
        )
    return result.astype(jnp.bfloat16)


def solution(mesh):
    in_specs = (
        P(("grp", "req"), None, None),
        P(("grp", "req"), None, None),
        P(("grp", "req"), None, None),
        P(("grp", "req")),
        P(("grp", "req")),
        P(("grp", "req")),
        P(),
        P(),
        P(),
    )
    out_specs = P(("grp", "req"), None)
    return jax.shard_map(local, mesh=mesh, in_specs=in_specs, out_specs=out_specs, check_vma=False)
```

time: 142 us -> 419 us (2.95)
  blocking collectives: 29.6 us -> 308 us
  local copies, waits for them, and re-layouts: 40.5 us -> 12.4 us
  starting transfers between devices: 21.4 us -> 48.7 us
  Pallas kernels: 0 us -> 17.9 us
  matrix products: 12.6 us -> 6.11 us
  waiting for transfers between devices: 27 us -> 21.6 us
  other arithmetic: 8.71 us -> 3.69 us
    all_gather x0 -> x1, blocking collectives: none -> 308 us  [local(): lax.all_gather(jnp.stack([span_len, series_perm]), 'req', axis=1, tiled=T...]
    unnamed x1 -> x0, blocking collectives: 29.6 us -> none
    all_to_all x2 -> x1, starting transfers between devices: 21.4 us -> 48.7 us  [local(): lax.all_to_all(placed, 'req', split_axis=0, concat_axis=0, tiled=True)]
    pallas_call x0 -> x1, Pallas kernels: none -> 17.9 us  [layer_block(): pl.pallas_call(block_kernel, grid_spec=grid_spec, out_shape=jax.ShapeDtyp...]
    reshape x6 -> x2, local copies, waits for them, and re-layouts: 18.6 us -> 1.4 us  [the longest x1 1.29 us: layer_block(): ff_gain.reshape(1, width)]
    scatter x4 -> x0, local copies, waits for them, and re-layouts: 10.4 us -> none  [the longest x1 4.12 us: local(): return feed_forward(jnp.zeros((rows_here, width), jnp.bfloat16).at[local_...]
    dot_general x3 -> x8, matrix products: 12.6 us -> 6.11 us  [the longest x4 4.45 us: local(): jnp.dot(pick[i], layer_out[i], preferred_element_type=jnp.float32)]
    unnamed x13 -> x4, local copies, waits for them, and re-layouts: 4.01 us -> 10.1 us
  transfers between devices with their start and end apart: 2 -> 1, of which waited for: 1 -> 1; matrix products, arithmetic and copies ran while one was open for 26% -> 0% of each run, Pallas kernels for 0% -> 0%
where the time goes in v1:
time: 419 us; the launch traced here: 418 us
  blocking collectives  308 us (74%)
  starting transfers between devices  48.7 us (12%)
  waiting for transfers between devices  21.6 us (5%)
  Pallas kernels  17.9 us (4%)
  local copies, waits for them, and re-layouts  12.4 us (3%)
  matrix products  6.11 us (1%)
    all_gather x1, blocking collectives, local(): lax.all_gather(jnp.stack([span_len, series_perm]), 'req', axis=1, tiled=T...  308 us
    all_to_all x1, starting transfers between devices, local(): lax.all_to_all(placed, 'req', split_axis=0, concat_axis=0, tiled=True)  48.7 us
    all_to_all x1, waiting for transfers between devices, local(): lax.all_to_all(placed, 'req', split_axis=0, concat_axis=0, tiled=True)  21.6 us
    pallas_call x1, Pallas kernels, layer_block(): pl.pallas_call(block_kernel, grid_spec=grid_spec, out_shape=jax.ShapeDtyp...  17.9 us
    unnamed x4, local copies, waits for them, and re-layouts  10.1 us
  transfers between devices with their start and end apart: 1, of which 1 were waited for; matrix products, arithmetic and copies ran while one was open for 0% of the time, Pallas kernels for 0%

profile of v1, /device:TPU:8, one launch (start us, length us, event | category | flops | bytes accessed | tf_op | source)
XLA Modules:
  0.0 418.1 jit_solution(478681273621987173)
XLA Ops:
  0.0 0.7 iota_compare_fusion.9
  0.7 1.3 reshape.74.gain_ref
  2.0 0.7 add_bitcast_fusion
  2.7 307.5 %all-gather = s32[128,4,2]{1,2,0:T(2,128)S(1)} all-gather(s32[1,4,2]{1,2,0:T(2,128)S(1)} %add_bitcast_fusion), channel_id=1, replica_groups=mesh['grp'=2,'req'=128] {'req'}, dimensions={0}, use_global_device_ids=true | all-gather | bytes 4128 | tf_op jit(solution)/shard_map/all_gather | solution.py:92
  310.2 0.1 reshape.76
  310.4 0.2 select_reduce_fusion
  310.6 0.1 dynamic_slice.3
  310.7 0.1 add_select_fusion.2
  310.8 0.1 fusion.6
  310.9 17.9 %shard_map.91 = bf16[4,32,1280]{2,1,0:T(8,128)(2,1)} custom-call(s32[4]{0:T(128)} %cache_len_ref.1, bf16[4,32,3840]{2,1,0:T(8,128)(2,1)} %qkv_ref.1, bf16[4,32,2560]{2,1,0:T(8,128)(2,1)} %cache_ref.1, bf16[4,32,1280]{2,1,0:T(8,128)(2,1)} %resid_ref.1, f32[1,1280]{1,0:T(1,128)} %reshape.74.gain_ref, bf16[1280,1280]{1,0:T(8,128)(2,1)} %up_ref.1, ...), custom_call_target="tpu_custom_call" | custom-call | tf_op jit(solution)/shard_map/pallas_call | solution.py:79
  328.8 1.1 convolution_convert_fusion
  329.9 1.1 convolution_convert_fusion.1
  331.0 1.1 convolution_convert_fusion.2
  332.2 1.1 convolution_convert_fusion.3
  333.3 0.1 maximum_bitcast_fusion
  333.4 0.5 broadcast.78
  333.9 1.6 reduce.12
  335.5 1.8 reshape.88
  337.4 48.7 %all-to-all-start = ((bf16[128,2,2560]{2,1,0:T(2,128)(2,1)}), bf16[128,2,2560]{2,1,0:T(2,128)(2,1)}, u32[]{:S(2)}, u32[]{:S(2)}) async-start(bf16[128,2,2560]{2,1,0:T(2,128)(2,1)} %reshape.88), calls=%async_computation | async-start | bytes 2621440 | tf_op jit(solution)/shard_map/all_to_all | solution.py:113
  386.1 0.1 reshape.73
  386.2 0.1 reshape_squeeze.3
  386.3 0.1 fusion.9
  386.4 0.2 slice_reduce_fusion
  386.6 21.6 %all-to-all-done = bf16[128,2,2560]{2,1,0:T(2,128)(2,1)} async-done(((bf16[128,2,2560]{2,1,0:T(2,128)(2,1)}), bf16[128,2,2560]{2,1,0:T(2,128)(2,1)}, u32[]{:S(2)}, u32[]{:S(2)}) %all-to-all-start) | async-done | bytes 1310752 | tf_op jit(solution)/shard_map/all_to_all | solution.py:113
  408.2 7.7 %reshape.89 = bf16[128,1,5120]{2,1,0:T(2,128)(2,1)S(1)} reshape(bf16[128,2,2560]{2,1,0:T(2,128)(2,1)} %all-to-all-done) | data formatting | bytes 2621440
  416.0 0.4 copy.20
  416.4 0.2 fusion.4
  416.6 0.2 convolution_add_fusion.2
  416.9 0.2 convolution_add_fusion.1
  417.1 1.0 fusion
  (2 shorter events, 0.0 us)
Async XLA Ops:
  337.4 70.9 %all-to-all-start = ((bf16[128,2,2560]{2,1,0:T(2,128)(2,1)}), bf16[128,2,2560]{2,1,0:T(2,128)(2,1)}, u32[]{:S(2)}, u32[]{:S(2)}) async-start(bf16[128,2,2560]{2,1,0:T(2,128)(2,1)} %reshape.88), calls=%async_computation | async-start | bytes 2621440 | tf_op jit(solution)/shard_map/all_to_all | solution.py:113

commit v2 on v1

--- a/solution.py
+++ b/solution.py
@@ -89,8 +89,12 @@
     me = lax.axis_index("req")
     series_here, span_slots, triple = new_qkv.shape
     width = resid.shape[2]
-    gathered = lax.all_gather(jnp.stack([span_len, series_perm]), "req", axis=1, tiled=True)
-    all_len, all_perm = gathered[0], gathered[1]
+    info = jnp.concatenate([span_len, series_perm])
+    gathered = lax.all_to_all(
+        jnp.broadcast_to(info[None], (group_size, info.shape[0])), "req", 0, 0, tiled=True
+    )
+    all_len = gathered[:, :series_here].reshape(-1)
+    all_perm = gathered[:, series_here:].reshape(-1)
     series_total = all_len.shape[0]
     earlier = all_perm[None, :] < all_perm[:, None]
     all_start = jnp.sum(jnp.where(earlier, all_len[None, :], 0), axis=1)
@@ -103,14 +107,6 @@
     my_offset = (target - my_start[:, None, None]) % group_size
     pick = (my_offset == slot) & (slot < span_len[:, None, None])
     pick = pick.astype(jnp.bfloat16)
-    placed = jnp.concatenate(
-        [
-            jnp.dot(pick[i], layer_out[i], preferred_element_type=jnp.float32).astype(jnp.bfloat16)
-            for i in range(series_here)
-        ],
-        axis=1,
-    )
-    arrived = lax.all_to_all(placed, "req", split_axis=0, concat_axis=0, tiled=True)
 
     src_start = all_start.reshape(group_size, series_here)
     src_len = all_len.reshape(group_size, series_here)
@@ -121,10 +117,10 @@
     out_row = jnp.arange(rows_here, dtype=jnp.int32)[:, None]
     result = jnp.zeros((rows_here, width), jnp.float32)
     for i in range(series_here):
+        placed = jnp.dot(pick[i], layer_out[i], preferred_element_type=jnp.float32).astype(jnp.bfloat16)
+        arrived = lax.all_to_all(placed, "req", 0, 0, tiled=True)
         gather_i = (src_row[None, :, i] == out_row).astype(jnp.bfloat16)
-        result = result + jnp.dot(
-            gather_i, arrived[:, i * width : (i + 1) * width], preferred_element_type=jnp.float32
-        )
+        result = result + jnp.dot(gather_i, arrived, preferred_element_type=jnp.float32)
     return result.astype(jnp.bfloat16)
 
 

time: 419 us -> 132 us (0.32)
  blocking collectives: 308 us -> 0 us
  waiting for transfers between devices: 21.6 us -> 45 us
  local copies, waits for them, and re-layouts: 12.4 us -> 7.49 us
    all_gather x1 -> x0, blocking collectives: 308 us -> none  [local(): lax.all_gather(jnp.stack([span_len, series_perm]), 'req', axis=1, tiled=T...]
    all_to_all x1 -> x5, waiting for transfers between devices: 21.6 us -> 45 us  [the longest x4 45 us: local(): arrived = lax.all_to_all(placed, 'req', 0, 0, tiled=True)]
    unnamed x4 -> x10, local copies, waits for them, and re-layouts: 10.1 us -> 4.31 us
    all_to_all x1 -> x5, starting transfers between devices: 48.7 us -> 51.2 us  [the longest x4 35.8 us: local(): arrived = lax.all_to_all(placed, 'req', 0, 0, tiled=True)]
  transfers between devices with their start and end apart: 1 -> 5, of which waited for: 1 -> 4; matrix products, arithmetic and copies ran while one was open for 0% -> 8% of each run, Pallas kernels for 0% -> 14%
where the time goes in v2:
time: 132 us; the launch traced here: 131 us
  starting transfers between devices  51.2 us (39%)
  waiting for transfers between devices  45 us (34%)
  Pallas kernels  17.9 us (14%)
  local copies, waits for them, and re-layouts  7.49 us (6%)
  other arithmetic  5.3 us (4%)
  matrix products  4.34 us (3%)
    all_to_all x4, waiting for transfers between devices, local(): arrived = lax.all_to_all(placed, 'req', 0, 0, tiled=True)  45 us
    all_to_all x4, starting transfers between devices, local(): arrived = lax.all_to_all(placed, 'req', 0, 0, tiled=True)  35.8 us
    pallas_call x1, Pallas kernels, layer_block(): pl.pallas_call(block_kernel, grid_spec=grid_spec, out_shape=jax.ShapeDtyp...  17.9 us
    all_to_all x1, starting transfers between devices, local(): lax.all_to_all(jnp.broadcast_to(info[None], (group_size, info.shape[0])),...  15.4 us
    unnamed x10, local copies, waits for them, and re-layouts  4.31 us
    all_to_all x4, other arithmetic, local(): arrived = lax.all_to_all(placed, 'req', 0, 0, tiled=True)  3.27 us
    dot_general x4, matrix products, local(): jnp.dot(pick[i], layer_out[i], preferred_element_type=jnp.float32)  2.68 us
  transfers between devices with their start and end apart: 5, of which 4 were waited for; matrix products, arithmetic and copies ran while one was open for 8% of the time, Pallas kernels for 14%

profile of v2, /device:TPU:8, one launch (start us, length us, event | category | flops | bytes accessed | tf_op | source)
XLA Modules:
  0.0 131.4 jit_solution(12147800484939362778)
XLA Ops:
  0.0 0.7 pad_add_fusion
  0.7 0.7 broadcast_in_dim.18
  1.4 15.4 %all-to-all-start = ((s32[128,1,8]{2,1,0:T(1,128)}), s32[128,1,8]{2,1,0:T(1,128)S(1)}, u32[]{:S(2)}, u32[]{:S(2)}) async-start(s32[128,1,8]{2,1,0:T(1,128)} %broadcast_in_dim.18), calls=%async_computation | async-start | bytes 131072 | tf_op jit(solution)/shard_map/all_to_all | solution.py:93
  16.9 0.7 iota_compare_fusion.9
  17.6 1.3 reshape.88.gain_ref
  18.9 17.9 %shard_map.91 = bf16[4,32,1280]{2,1,0:T(8,128)(2,1)} custom-call(s32[4]{0:T(128)} %cache_len_ref.1, bf16[4,32,3840]{2,1,0:T(8,128)(2,1)} %qkv_ref.1, bf16[4,32,2560]{2,1,0:T(8,128)(2,1)} %cache_ref.1, bf16[4,32,1280]{2,1,0:T(8,128)(2,1)} %resid_ref.1, f32[1,1280]{1,0:T(1,128)} %reshape.88.gain_ref, bf16[1280,1280]{1,0:T(8,128)(2,1)} %up_ref.1, ...), custom_call_target="tpu_custom_call" | custom-call | tf_op jit(solution)/shard_map/pallas_call | solution.py:79
  36.7 0.0 copy-start
  36.7 0.0 all-to-all-done
  36.7 0.1 fusion.25
  36.8 0.1 broadcast_in_dim.28
  36.9 0.1 lt.51
  37.0 0.3 select_reduce_fusion
  37.3 0.1 dynamic_slice.3
  37.4 0.1 add_select_fusion.2
  37.5 0.1 fusion.14
  37.6 1.1 fusion.1
  38.7 0.5 broadcast.78
  39.2 0.8 reduce.8
  40.1 0.8 reshape.93
  40.9 13.8 %all-to-all-start.1 = ((bf16[128,2,640]{2,1,0:T(2,128)(2,1)}), bf16[128,2,640]{2,1,0:T(2,128)(2,1)S(1)}, u32[]{:S(2)}, u32[]{:S(2)}) async-start(bf16[128,2,640]{2,1,0:T(2,128)(2,1)} %reshape.93), calls=%async_computation.1 | async-start | bytes 655360 | tf_op jit(solution)/shard_map/all_to_all | solution.py:121
  54.7 1.1 fusion.2
  55.8 0.8 reduce.9
  56.6 0.8 reshape.95
  57.4 11.5 %all-to-all-done.1 = bf16[128,2,640]{2,1,0:T(2,128)(2,1)S(1)} async-done(((bf16[128,2,640]{2,1,0:T(2,128)(2,1)}), bf16[128,2,640]{2,1,0:T(2,128)(2,1)S(1)}, u32[]{:S(2)}, u32[]{:S(2)}) %all-to-all-start.1) | async-done | bytes 327712 | tf_op jit(solution)/shard_map/all_to_all | solution.py:121
  68.9 7.4 %all-to-all-start.2 = ((bf16[128,2,640]{2,1,0:T(2,128)(2,1)}), bf16[128,2,640]{2,1,0:T(2,128)(2,1)S(1)}, u32[]{:S(2)}, u32[]{:S(2)}) async-start(bf16[128,2,640]{2,1,0:T(2,128)(2,1)} %reshape.95), calls=%async_computation.2 | async-start | bytes 655360 | tf_op jit(solution)/shard_map/all_to_all | solution.py:121
  76.3 0.0 copy-done
  76.3 0.2 fusion.3
  76.5 0.8 reduce.10
  77.4 0.8 reshape.97
  78.2 11.6 %all-to-all-done.2 = bf16[128,2,640]{2,1,0:T(2,128)(2,1)S(1)} async-done(((bf16[128,2,640]{2,1,0:T(2,128)(2,1)}), bf16[128,2,640]{2,1,0:T(2,128)(2,1)S(1)}, u32[]{:S(2)}, u32[]{:S(2)}) %all-to-all-start.2) | async-done | bytes 327712 | tf_op jit(solution)/shard_map/all_to_all | solution.py:121
  89.8 7.4 %all-to-all-start.3 = ((bf16[128,2,640]{2,1,0:T(2,128)(2,1)}), bf16[128,2,640]{2,1,0:T(2,128)(2,1)S(1)}, u32[]{:S(2)}, u32[]{:S(2)}) async-start(bf16[128,2,640]{2,1,0:T(2,128)(2,1)} %reshape.97), calls=%async_computation.3 | async-start | bytes 655360 | tf_op jit(solution)/shard_map/all_to_all | solution.py:121
  97.2 0.1 reshape.87
  97.3 0.2 fusion.4
  97.5 0.8 reduce.11
  98.4 0.8 reshape.99
  99.2 0.1 fusion.17
  99.2 0.2 slice_reduce_fusion
  99.5 0.3 reshape.94
  99.8 10.5 %all-to-all-done.3 = bf16[128,2,640]{2,1,0:T(2,128)(2,1)S(1)} async-done(((bf16[128,2,640]{2,1,0:T(2,128)(2,1)}), bf16[128,2,640]{2,1,0:T(2,128)(2,1)S(1)}, u32[]{:S(2)}, u32[]{:S(2)}) %all-to-all-start.3) | async-done | bytes 327712 | tf_op jit(solution)/shard_map/all_to_all | solution.py:121
  110.3 7.2 %all-to-all-start.4 = ((bf16[128,2,640]{2,1,0:T(2,128)(2,1)}), bf16[128,2,640]{2,1,0:T(2,128)(2,1)S(1)}, u32[]{:S(2)}, u32[]{:S(2)}) async-start(bf16[128,2,640]{2,1,0:T(2,128)(2,1)} %reshape.99), calls=%async_computation.4 | async-start | bytes 655360 | tf_op jit(solution)/shard_map/all_to_all | solution.py:121
  117.5 0.2 fusion.11
  117.7 0.3 reshape.96
  118.0 0.3 reshape.98
  118.3 0.2 convolution_add_fusion.2
  118.5 0.2 convolution_add_fusion.1
  118.8 11.4 %all-to-all-done.4 = bf16[128,2,640]{2,1,0:T(2,128)(2,1)S(1)} async-done(((bf16[128,2,640]{2,1,0:T(2,128)(2,1)}), bf16[128,2,640]{2,1,0:T(2,128)(2,1)S(1)}, u32[]{:S(2)}, u32[]{:S(2)}) %all-to-all-start.4) | async-done | bytes 327712 | tf_op jit(solution)/shard_map/all_to_all | solution.py:121
  130.2 0.3 reshape.100
  130.4 1.0 fusion
Async XLA Ops:
  1.4 35.3 %all-to-all-start = ((s32[128,1,8]{2,1,0:T(1,128)}), s32[128,1,8]{2,1,0:T(1,128)S(1)}, u32[]{:S(2)}, u32[]{:S(2)}) async-start(s32[128,1,8]{2,1,0:T(1,128)} %broadcast_in_dim.18), calls=%async_computation | async-start | bytes 131072 | tf_op jit(solution)/shard_map/all_to_all | solution.py:93
  36.7 39.6 %copy-start = (bf16[4,32,1280]{2,1,0:T(8,128)(2,1)S(1)}, bf16[4,32,1280]{2,1,0:T(8,128)(2,1)}, u32[]{:S(2)}) copy-start(bf16[4,32,1280]{2,1,0:T(8,128)(2,1)} %shard_map.91) | copy-start | bytes 983044
  40.9 28.0 %all-to-all-start.1 = ((bf16[128,2,640]{2,1,0:T(2,128)(2,1)}), bf16[128,2,640]{2,1,0:T(2,128)(2,1)S(1)}, u32[]{:S(2)}, u32[]{:S(2)}) async-start(bf16[128,2,640]{2,1,0:T(2,128)(2,1)} %reshape.93), calls=%async_computation.1 | async-start | bytes 655360 | tf_op jit(solution)/shard_map/all_to_all | solution.py:121
  68.9 20.9 %all-to-all-start.2 = ((bf16[128,2,640]{2,1,0:T(2,128)(2,1)}), bf16[128,2,640]{2,1,0:T(2,128)(2,1)S(1)}, u32[]{:S(2)}, u32[]{:S(2)}) async-start(bf16[128,2,640]{2,1,0:T(2,128)(2,1)} %reshape.95), calls=%async_computation.2 | async-start | bytes 655360 | tf_op jit(solution)/shard_map/all_to_all | solution.py:121
  89.8 20.5 %all-to-all-start.3 = ((bf16[128,2,640]{2,1,0:T(2,128)(2,1)}), bf16[128,2,640]{2,1,0:T(2,128)(2,1)S(1)}, u32[]{:S(2)}, u32[]{:S(2)}) async-start(bf16[128,2,640]{2,1,0:T(2,128)(2,1)} %reshape.97), calls=%async_computation.3 | async-start | bytes 655360 | tf_op jit(solution)/shard_map/all_to_all | solution.py:121
  110.3 19.9 %all-to-all-start.4 = ((bf16[128,2,640]{2,1,0:T(2,128)(2,1)}), bf16[128,2,640]{2,1,0:T(2,128)(2,1)S(1)}, u32[]{:S(2)}, u32[]{:S(2)}) async-start(bf16[128,2,640]{2,1,0:T(2,128)(2,1)} %reshape.99), calls=%async_computation.4 | async-start | bytes 655360 | tf_op jit(solution)/shard_map/all_to_all | solution.py:121

commit v3 on v2

--- a/solution.py
+++ b/solution.py
@@ -115,12 +115,13 @@
     src_row = jnp.where(src_t < src_len, src_row, -1)
     rows_here = series_here * span_slots
     out_row = jnp.arange(rows_here, dtype=jnp.int32)[:, None]
-    result = jnp.zeros((rows_here, width), jnp.float32)
-    for i in range(series_here):
-        placed = jnp.dot(pick[i], layer_out[i], preferred_element_type=jnp.float32).astype(jnp.bfloat16)
-        arrived = lax.all_to_all(placed, "req", 0, 0, tiled=True)
-        gather_i = (src_row[None, :, i] == out_row).astype(jnp.bfloat16)
-        result = result + jnp.dot(gather_i, arrived, preferred_element_type=jnp.float32)
+    placed = jnp.einsum(
+        "idt,itc->dic", pick, layer_out, preferred_element_type=jnp.float32
+    ).astype(jnp.bfloat16)
+    placed = placed.reshape(group_size * series_here, width)
+    arrived = lax.all_to_all(placed, "req", 0, 0, tiled=True)
+    gather = (src_row.reshape(1, -1) == out_row).astype(jnp.bfloat16)
+    result = jnp.dot(gather, arrived, preferred_element_type=jnp.float32)
     return result.astype(jnp.bfloat16)
 
 

time: 132 us -> 91.9 us (0.70)
  starting transfers between devices: 51.2 us -> 29.2 us
  waiting for transfers between devices: 45 us -> 34.4 us
  other arithmetic: 5.3 us -> 1.89 us
  local copies, waits for them, and re-layouts: 7.49 us -> 5.49 us
  matrix products: 4.34 us -> 2.7 us
    all_to_all x4 -> x1, starting transfers between devices: 35.8 us -> 13.8 us  [local(): arrived = lax.all_to_all(placed, 'req', 0, 0, tiled=True)]
    all_to_all x4 -> x1, waiting for transfers between devices: 45 us -> 34.3 us  [local(): arrived = lax.all_to_all(placed, 'req', 0, 0, tiled=True)]
    unnamed x10 -> x0, local copies, waits for them, and re-layouts: 4.31 us -> none
    all_to_all x4 -> x0, other arithmetic: 3.27 us -> none  [local(): arrived = lax.all_to_all(placed, 'req', 0, 0, tiled=True)]
    convert_element_type x0 -> x1, local copies, waits for them, and re-layouts: none -> 2.63 us  [local(): placed = jnp.einsum('idt,itc->dic', pick, layer_out, preferred_element_ty...]
    dot_general x8 -> x2, matrix products: 4.34 us -> 2.7 us  [the longest x1 1.62 us: local(): jnp.einsum('idt,itc->dic', pick, layer_out, preferred_element_type=jnp.fl...]
  transfers between devices with their start and end apart: 5 -> 2, of which waited for: 4 -> 1; matrix products, arithmetic and copies ran while one was open for 8% -> 3% of each run, Pallas kernels for 14% -> 19%
where the time goes in v3:
time: 91.9 us; the launch traced here: 91.6 us
  waiting for transfers between devices  34.4 us (37%)
  starting transfers between devices  29.2 us (32%)
  Pallas kernels  17.9 us (19%)
  local copies, waits for them, and re-layouts  5.49 us (6%)
  matrix products  2.7 us (3%)
  other arithmetic  1.89 us (2%)
    all_to_all x1, waiting for transfers between devices, local(): arrived = lax.all_to_all(placed, 'req', 0, 0, tiled=True)  34.3 us
    pallas_call x1, Pallas kernels, layer_block(): pl.pallas_call(block_kernel, grid_spec=grid_spec, out_shape=jax.ShapeDtyp...  17.9 us
    all_to_all x1, starting transfers between devices, local(): lax.all_to_all(jnp.broadcast_to(info[None], (group_size, info.shape[0])),...  15.4 us
    all_to_all x1, starting transfers between devices, local(): arrived = lax.all_to_all(placed, 'req', 0, 0, tiled=True)  13.8 us
    convert_element_type x1, local copies, waits for them, and re-layouts, local(): placed = jnp.einsum('idt,itc->dic', pick, layer_out, preferred_element_ty...  2.63 us
  transfers between devices with their start and end apart: 2, of which 1 were waited for; matrix products, arithmetic and copies ran while one was open for 3% of the time, Pallas kernels for 19%

profile of v3, /device:TPU:8, one launch (start us, length us, event | category | flops | bytes accessed | tf_op | source)
XLA Modules:
  0.0 91.6 jit_solution(14213843180677652622)
XLA Ops:
  0.0 0.7 pad_add_fusion
  0.7 0.6 broadcast_in_dim.18
  1.4 15.4 %all-to-all-start = ((s32[128,1,8]{2,1,0:T(1,128)}), s32[128,1,8]{2,1,0:T(1,128)S(1)}, u32[]{:S(2)}, u32[]{:S(2)}) async-start(s32[128,1,8]{2,1,0:T(1,128)} %broadcast_in_dim.18), calls=%async_computation | async-start | bytes 131072 | tf_op jit(solution)/shard_map/all_to_all | solution.py:93
  16.8 0.7 iota_compare_fusion.3
  17.6 1.3 %reshape.82.gain_ref = f32[1,1280]{1,0:T(1,128)} reshape(f32[1280]{0:T(1024)} %param.15) | data formatting | bytes 10240 | tf_op jit(solution)/shard_map/reshape | solution.py:84
  18.9 17.9 %shard_map.91 = bf16[4,32,1280]{2,1,0:T(8,128)(2,1)} custom-call(s32[4]{0:T(128)} %cache_len_ref.1, bf16[4,32,3840]{2,1,0:T(8,128)(2,1)} %qkv_ref.1, bf16[4,32,2560]{2,1,0:T(8,128)(2,1)} %cache_ref.1, bf16[4,32,1280]{2,1,0:T(8,128)(2,1)} %resid_ref.1, f32[1,1280]{1,0:T(1,128)} %reshape.82.gain_ref, bf16[1280,1280]{1,0:T(8,128)(2,1)} %up_ref.1, ...), custom_call_target="tpu_custom_call" | custom-call | tf_op jit(solution)/shard_map/pallas_call | solution.py:79
  36.7 0.0 all-to-all-done
  36.7 0.1 fusion.12
  36.8 0.1 lt.51
  36.9 0.1 broadcast_in_dim.28
  37.0 0.3 select_reduce_fusion
  37.3 0.1 dynamic_slice.3
  37.4 0.1 add_select_fusion.2
  37.5 1.6 %fusion = bf16[128,4,1280]{0,2,1:T(8,128)(2,1)S(1)} fusion(bf16[4,32,1280]{2,1,0:T(8,128)(2,1)} %shard_map.91, s32[4,128]{1,0:T(4,128)S(1)} %add_select_fusion.2, pred[4,32]{1,0:T(4,128)(4,1)S(1)} %iota_compare_fusion.3), kind=kOutput, calls=%fused_computation.1 | convolution fusion | flops 42631168 | bytes 1640576 | tf_op jit(solution)/shard_map/idt,itc->dic/dot_general | solution.py:118
  39.1 2.6 %copy.12 = bf16[128,4,1280]{2,1,0:T(4,128)(2,1)} copy(bf16[128,4,1280]{0,2,1:T(8,128)(2,1)S(1)} %fusion) | data formatting | bytes 2621440 | tf_op jit(solution)/shard_map/convert_element_type | solution.py:120
  41.7 13.8 %all-to-all-start.1 = ((bf16[128,4,1280]{2,1,0:T(4,128)(2,1)}), bf16[128,4,1280]{2,1,0:T(4,128)(2,1)S(1)}, u32[]{:S(2)}, u32[]{:S(2)}) async-start(bf16[128,4,1280]{2,1,0:T(4,128)(2,1)} %copy.12), calls=%async_computation.1 | async-start | bytes 2621440 | tf_op jit(solution)/shard_map/all_to_all | solution.py:122
  55.5 0.1 reshape.81
  55.6 0.1 fusion.4
  55.7 0.1 eq.32
  55.8 34.3 %all-to-all-done.1 = bf16[128,4,1280]{2,1,0:T(4,128)(2,1)S(1)} async-done(((bf16[128,4,1280]{2,1,0:T(4,128)(2,1)}), bf16[128,4,1280]{2,1,0:T(4,128)(2,1)S(1)}, u32[]{:S(2)}, u32[]{:S(2)}) %all-to-all-start.1) | async-done | bytes 1310752 | tf_op jit(solution)/shard_map/all_to_all | solution.py:122
  90.2 0.3 all_to_all.15
  90.5 1.1 %convolution_convert_fusion.1 = bf16[128,1280]{1,0:T(8,128)(2,1)} fusion(bf16[512,1280]{1,0:T(8,128)(2,1)S(1)} %all_to_all.15, s32[512]{0:T(512)S(1)} %eq.32), kind=kOutput, calls=%fused_computation.2 | convolution fusion | flops 168001536 | bytes 1640448 | tf_op jit(solution)/shard_map/dot_general | solution.py:124
Async XLA Ops:
  1.4 35.3 %all-to-all-start = ((s32[128,1,8]{2,1,0:T(1,128)}), s32[128,1,8]{2,1,0:T(1,128)S(1)}, u32[]{:S(2)}, u32[]{:S(2)}) async-start(s32[128,1,8]{2,1,0:T(1,128)} %broadcast_in_dim.18), calls=%async_computation | async-start | bytes 131072 | tf_op jit(solution)/shard_map/all_to_all | solution.py:93
  41.7 48.5 %all-to-all-start.1 = ((bf16[128,4,1280]{2,1,0:T(4,128)(2,1)}), bf16[128,4,1280]{2,1,0:T(4,128)(2,1)S(1)}, u32[]{:S(2)}, u32[]{:S(2)}) async-start(bf16[128,4,1280]{2,1,0:T(4,128)(2,1)} %copy.12), calls=%async_computation.1 | async-start | bytes 2621440 | tf_op jit(solution)/shard_map/all_to_all | solution.py:122

commit v4 on v3

v4 whole, which is shorter than its diff:
```python
import jax
import jax.numpy as jnp
from jax import lax
from jax.experimental import pallas as pl
from jax.experimental.pallas import tpu as pltpu
from jax.sharding import PartitionSpec as P

H = 16


def block_kernel(cache_len_ref, qkv_ref, cache_ref, resid_ref, gain_ref, up_ref, down_ref, pick_ref, out_ref, hid_ref):
    series_here, span_slots = qkv_ref.shape[0], qkv_ref.shape[1]
    cache_slots = cache_ref.shape[1]
    width = resid_ref.shape[2]
    head_size = width // H
    col_head = lax.broadcasted_iota(jnp.int32, (H, 1, width), 2) // head_size
    head_id = lax.broadcasted_iota(jnp.int32, (H, 1, width), 0)
    head_mask = col_head == head_id
    dims = (((1,), (1,)), ((), ()))
    scale = head_size ** (-0.5)
    rows = H * span_slots
    row_t = lax.broadcasted_iota(jnp.int32, (rows, span_slots), 0) % span_slots
    key_new = lax.broadcasted_iota(jnp.int32, (rows, span_slots), 1)
    key_old = lax.broadcasted_iota(jnp.int32, (rows, cache_slots), 1)
    for i in range(series_here):
        q = qkv_ref[i, :, 0:width]
        k_new = qkv_ref[i, :, width : 2 * width]
        v_new = qkv_ref[i, :, 2 * width : 3 * width]
        k_old = cache_ref[i, :, 0:width]
        v_old = cache_ref[i, :, width : 2 * width]
        q_heads = jnp.where(head_mask, q[None], jnp.zeros((), q.dtype)).reshape(rows, width)
        s_old = lax.dot_general(q_heads, k_old, dims, preferred_element_type=jnp.float32) * scale
        s_new = lax.dot_general(q_heads, k_new, dims, preferred_element_type=jnp.float32) * scale
        s_old = jnp.where(key_old < cache_len_ref[i], s_old, -1e30)
        s_new = jnp.where(key_new <= row_t, s_new, -1e30)
        top = jnp.maximum(jnp.max(s_old, axis=1, keepdims=True), jnp.max(s_new, axis=1, keepdims=True))
        e_old = jnp.exp(s_old - top)
        e_new = jnp.exp(s_new - top)
        denom = jnp.sum(e_old, axis=1, keepdims=True) + jnp.sum(e_new, axis=1, keepdims=True)
        w_old = (e_old / denom).astype(jnp.bfloat16)
        w_new = (e_new / denom).astype(jnp.bfloat16)
        mixed = jnp.dot(w_old, v_old, preferred_element_type=jnp.float32) + jnp.dot(
            w_new, v_new, preferred_element_type=jnp.float32
        )
        mixed = mixed.reshape(H, span_slots, width)
        attended = jnp.sum(jnp.where(head_mask, mixed, 0.0), axis=0)
        hid_ref[i * span_slots : (i + 1) * span_slots, :] = (
            resid_ref[i].astype(jnp.float32) + attended
        ).astype(hid_ref.dtype)
    wide_rows = hid_ref[...].astype(jnp.float32)
    normed = (
        wide_rows
        * lax.rsqrt(jnp.mean(wide_rows * wide_rows, axis=-1, keepdims=True) + 1e-06)
        * gain_ref[...]
    ).astype(jnp.bfloat16)
    activated = jax.nn.silu(
        jnp.dot(normed, up_ref[...], preferred_element_type=jnp.float32)
    ).astype(jnp.bfloat16)
    layer_out = (
        wide_rows + jnp.dot(activated, down_ref[...], preferred_element_type=jnp.float32)
    ).astype(jnp.bfloat16)
    out_ref[...] = jnp.dot(pick_ref[...], layer_out, preferred_element_type=jnp.float32).astype(
        out_ref.dtype
    )


def layer_block(new_qkv, cache_kv, resid, cache_len, ff_gain, w_up, w_down, pick):
    series_here, span_slots, triple = new_qkv.shape
    width = resid.shape[2]
    vmem = pltpu.MemorySpace.VMEM if hasattr(pltpu, "MemorySpace") else pltpu.VMEM
    full = pl.BlockSpec(memory_space=vmem)
    return pl.pallas_call(
        block_kernel,
        in_specs=[pl.BlockSpec(memory_space=pltpu.SMEM)] + [full] * 7,
        out_specs=full,
        out_shape=jax.ShapeDtypeStruct((pick.shape[0], width), jnp.bfloat16),
        scratch_shapes=[pltpu.VMEM((series_here * span_slots, width), jnp.bfloat16)],
    )(cache_len, new_qkv, cache_kv, resid, ff_gain.reshape(1, width), w_up, w_down, pick)


def local(new_qkv, cache_kv, resid, span_len, cache_len, series_perm, ff_gain, w_up, w_down):
    group_size = lax.axis_size("req")
    me = lax.axis_index("req")
    series_here, span_slots, triple = new_qkv.shape
    width = resid.shape[2]
    info = jnp.concatenate([span_len, series_perm])
    gathered = lax.all_to_all(
        jnp.broadcast_to(info[None], (group_size, info.shape[0])), "req", 0, 0, tiled=True
    )
    all_len = gathered[:, :series_here].reshape(-1)
    all_perm = gathered[:, series_here:].reshape(-1)
    series_total = all_len.shape[0]
    earlier = all_perm[None, :] < all_perm[:, None]
    all_start = jnp.sum(jnp.where(earlier, all_len[None, :], 0), axis=1)


    my_start = lax.dynamic_slice(all_start, (me * series_here,), (series_here,))
    target = jnp.arange(group_size, dtype=jnp.int32)[None, :, None]
    slot = jnp.arange(span_slots, dtype=jnp.int32)[None, None, :]
    my_offset = (target - my_start[:, None, None]) % group_size
    pick = (my_offset == slot) & (slot < span_len[:, None, None])
    same = jnp.arange(series_here)[:, None] == jnp.arange(series_here)[None, :]
    pick = pick.transpose(1, 0, 2)[:, :, None, :] & same[None, :, :, None]
    pick = pick.reshape(group_size * series_here, series_here * span_slots).astype(jnp.bfloat16)

    src_start = all_start.reshape(group_size, series_here)
    src_len = all_len.reshape(group_size, series_here)
    src_t = (me - src_start) % group_size
    src_row = (src_start + src_t) // group_size
    src_row = jnp.where(src_t < src_len, src_row, -1)
    rows_here = series_here * span_slots
    out_row = jnp.arange(rows_here, dtype=jnp.int32)[:, None]
    placed = layer_block(new_qkv, cache_kv, resid, cache_len, ff_gain, w_up, w_down, pick)
    arrived = lax.all_to_all(placed, "req", 0, 0, tiled=True)
    gather = (src_row.reshape(1, -1) == out_row).astype(jnp.bfloat16)
    result = jnp.dot(gather, arrived, preferred_element_type=jnp.float32)
    return result.astype(jnp.bfloat16)


def solution(mesh):
    in_specs = (
        P(("grp", "req"), None, None),
        P(("grp", "req"), None, None),
        P(("grp", "req"), None, None),
        P(("grp", "req")),
        P(("grp", "req")),
        P(("grp", "req")),
        P(),
        P(),
        P(),
    )
    out_specs = P(("grp", "req"), None)
    return jax.shard_map(local, mesh=mesh, in_specs=in_specs, out_specs=out_specs, check_vma=False)
```

time: 91.9 us -> 89.7 us (0.976)
  waiting for transfers between devices: 34.4 us -> 42.6 us
  starting transfers between devices: 29.2 us -> 22.5 us
  Pallas kernels: 17.9 us -> 13.2 us
  local copies, waits for them, and re-layouts: 5.49 us -> 7.3 us
  matrix products: 2.7 us -> 1.08 us
    all_to_all x1, waiting for transfers between devices: 0.01 us -> 8.8 us  [local(): lax.all_to_all(jnp.broadcast_to(info[None], (group_size, info.shape[0])),...]
    all_to_all x1, starting transfers between devices: 13.8 us -> 7.06 us  [local(): arrived = lax.all_to_all(placed, 'req', 0, 0, tiled=True)]
    pallas_call x1, Pallas kernels: 17.9 us -> 13.2 us  [layer_block(): pl.pallas_call(block_kernel, in_specs=[pl.BlockSpec(memory_space=pltpu.SM...]
    all_to_all x1 -> x2, local copies, waits for them, and re-layouts: 0.32 us -> 3.81 us  [local(): arrived = lax.all_to_all(placed, 'req', 0, 0, tiled=True)]
    convert_element_type x1, local copies, waits for them, and re-layouts: 2.63 us -> 0.94 us  [local(): pick.reshape(group_size * series_here, series_here * span_slots)]
    dot_general x1 -> x0, matrix products: 1.62 us -> none  [local(): jnp.einsum('idt,itc->dic', pick, layer_out, preferred_element_type=jnp.fl...]
  transfers between devices with their start and end apart: 2 -> 2, of which waited for: 1 -> 2; matrix products, arithmetic and copies ran while one was open for 3% -> 3% of each run, Pallas kernels for 19% -> 0%
where the time goes in v4:
time: 89.7 us; the launch traced here: 89.1 us
  waiting for transfers between devices  42.6 us (47%)
  starting transfers between devices  22.5 us (25%)
  Pallas kernels  13.2 us (15%)
  local copies, waits for them, and re-layouts  7.3 us (8%)
  other arithmetic  2.42 us (3%)
  matrix products  1.08 us (1%)
    all_to_all x1, waiting for transfers between devices, local(): arrived = lax.all_to_all(placed, 'req', 0, 0, tiled=True)  33.8 us
    all_to_all x1, starting transfers between devices, local(): lax.all_to_all(jnp.broadcast_to(info[None], (group_size, info.shape[0])),...  15.4 us
    pallas_call x1, Pallas kernels, layer_block(): pl.pallas_call(block_kernel, in_specs=[pl.BlockSpec(memory_space=pltpu.SM...  13.2 us
    all_to_all x1, waiting for transfers between devices, local(): lax.all_to_all(jnp.broadcast_to(info[None], (group_size, info.shape[0])),...  8.8 us
    all_to_all x1, starting transfers between devices, local(): arrived = lax.all_to_all(placed, 'req', 0, 0, tiled=True)  7.06 us
    all_to_all x2, local copies, waits for them, and re-layouts, local(): arrived = lax.all_to_all(placed, 'req', 0, 0, tiled=True)  3.81 us
  transfers between devices with their start and end apart: 2, of which 2 were waited for; matrix products, arithmetic and copies ran while one was open for 3% of the time, Pallas kernels for 0%

profile of v4, /device:TPU:8, one launch (start us, length us, event | category | flops | bytes accessed | tf_op | source)
XLA Modules:
  0.0 89.1 jit_solution(2948034717799824254)
XLA Ops:
  0.0 0.7 pad_add_fusion
  0.7 0.7 broadcast_in_dim.17
  1.4 15.4 %all-to-all-start = ((s32[128,1,8]{2,1,0:T(1,128)}), s32[128,1,8]{2,1,0:T(1,128)S(1)}, u32[]{:S(2)}, u32[]{:S(2)}) async-start(s32[128,1,8]{2,1,0:T(1,128)} %broadcast_in_dim.17), calls=%async_computation | async-start | bytes 131072 | tf_op jit(solution)/shard_map/all_to_all | solution.py:87
  16.9 0.7 iota_compare_fusion.4
  17.6 1.3 %reshape.105.gain_ref = f32[1,1280]{1,0:T(1,128)} reshape(f32[1280]{0:T(1024)} %param.15) | data formatting | bytes 10240 | tf_op jit(solution)/shard_map/reshape | solution.py:78
  18.9 8.8 %all-to-all-done = s32[128,1,8]{2,1,0:T(1,128)S(1)} async-done(((s32[128,1,8]{2,1,0:T(1,128)}), s32[128,1,8]{2,1,0:T(1,128)S(1)}, u32[]{:S(2)}, u32[]{:S(2)}) %all-to-all-start) | async-done | bytes 4128 | tf_op jit(solution)/shard_map/all_to_all | solution.py:87
  27.7 0.1 fusion.11
  27.8 0.1 lt.51
  27.9 0.1 broadcast_in_dim.18
  28.0 0.3 select_reduce_fusion
  28.3 0.1 dynamic_slice.3
  28.4 0.2 fusion
  28.6 0.4 and_convert_fusion
  29.0 0.9 %reshape.106.pick_ref = bf16[512,128]{1,0:T(8,128)(2,1)} reshape(bf16[128,4,4,32]{3,2,1,0:T(4,128)(2,1)S(1)} %and_convert_fusion) | data formatting | bytes 262144 | tf_op jit(solution)/shard_map/convert_element_type | solution.py:104
  29.9 13.2 %shard_map.91 = bf16[512,1280]{1,0:T(8,128)(2,1)} custom-call(s32[4]{0:T(128)} %cache_len_ref.1, bf16[4,32,3840]{2,1,0:T(8,128)(2,1)} %qkv_ref.1, bf16[4,32,2560]{2,1,0:T(8,128)(2,1)} %cache_ref.1, bf16[4,32,1280]{2,1,0:T(8,128)(2,1)} %resid_ref.1, f32[1,1280]{1,0:T(1,128)} %reshape.105.gain_ref, bf16[1280,1280]{1,0:T(8,128)(2,1)} %up_ref.1, ...), custom_call_target="tpu_custom_call" | custom-call | tf_op jit(solution)/shard_map/pallas_call | solution.py:72
  43.1 3.5 %all_to_all.16 = bf16[128,4,1280]{2,1,0:T(4,128)(2,1)} reshape(bf16[512,1280]{1,0:T(8,128)(2,1)} %shard_map.91) | data formatting | bytes 2621440 | tf_op jit(solution)/shard_map/all_to_all | solution.py:114
  46.6 7.1 %all-to-all-start.1 = ((bf16[128,4,1280]{2,1,0:T(4,128)(2,1)}), bf16[128,4,1280]{2,1,0:T(4,128)(2,1)S(1)}, u32[]{:S(2)}, u32[]{:S(2)}) async-start(bf16[128,4,1280]{2,1,0:T(4,128)(2,1)} %all_to_all.16), calls=%async_computation.1 | async-start | bytes 2621440 | tf_op jit(solution)/shard_map/all_to_all | solution.py:114
  53.6 0.1 reshape.104
  53.8 0.1 fusion.4
  53.8 0.1 eq.54
  53.9 33.8 %all-to-all-done.1 = bf16[128,4,1280]{2,1,0:T(4,128)(2,1)S(1)} async-done(((bf16[128,4,1280]{2,1,0:T(4,128)(2,1)}), bf16[128,4,1280]{2,1,0:T(4,128)(2,1)S(1)}, u32[]{:S(2)}, u32[]{:S(2)}) %all-to-all-start.1) | async-done | bytes 1310752 | tf_op jit(solution)/shard_map/all_to_all | solution.py:114
  87.7 0.3 all_to_all.18
  88.0 1.1 %convolution_convert_fusion = bf16[128,1280]{1,0:T(8,128)(2,1)} fusion(bf16[512,1280]{1,0:T(8,128)(2,1)S(1)} %all_to_all.18, s32[512]{0:T(512)S(1)} %eq.54), kind=kOutput, calls=%fused_computation | convolution fusion | flops 168001536 | bytes 1640448 | tf_op jit(solution)/shard_map/dot_general | solution.py:116
  (2 shorter events, 0.0 us)
Async XLA Ops:
  1.4 26.3 %all-to-all-start = ((s32[128,1,8]{2,1,0:T(1,128)}), s32[128,1,8]{2,1,0:T(1,128)S(1)}, u32[]{:S(2)}, u32[]{:S(2)}) async-start(s32[128,1,8]{2,1,0:T(1,128)} %broadcast_in_dim.17), calls=%async_computation | async-start | bytes 131072 | tf_op jit(solution)/shard_map/all_to_all | solution.py:87
  46.6 41.1 %all-to-all-start.1 = ((bf16[128,4,1280]{2,1,0:T(4,128)(2,1)}), bf16[128,4,1280]{2,1,0:T(4,128)(2,1)S(1)}, u32[]{:S(2)}, u32[]{:S(2)}) async-start(bf16[128,4,1280]{2,1,0:T(4,128)(2,1)} %all_to_all.16), calls=%async_computation.1 | async-start | bytes 2621440 | tf_op jit(solution)/shard_map/all_to_all | solution.py:114

commit v5 on v4

--- a/solution.py
+++ b/solution.py
@@ -8,7 +8,7 @@
 H = 16
 
 
-def block_kernel(cache_len_ref, qkv_ref, cache_ref, resid_ref, gain_ref, up_ref, down_ref, pick_ref, out_ref, hid_ref):
+def block_kernel(cache_len_ref, qkv_ref, cache_ref, resid_ref, gain_ref, up_ref, down_ref, out_ref, hid_ref):
     series_here, span_slots = qkv_ref.shape[0], qkv_ref.shape[1]
     cache_slots = cache_ref.shape[1]
     width = resid_ref.shape[2]
@@ -56,26 +56,23 @@
     activated = jax.nn.silu(
         jnp.dot(normed, up_ref[...], preferred_element_type=jnp.float32)
     ).astype(jnp.bfloat16)
-    layer_out = (
+    out_ref[...] = (
         wide_rows + jnp.dot(activated, down_ref[...], preferred_element_type=jnp.float32)
-    ).astype(jnp.bfloat16)
-    out_ref[...] = jnp.dot(pick_ref[...], layer_out, preferred_element_type=jnp.float32).astype(
-        out_ref.dtype
-    )
+    ).astype(out_ref.dtype)
 
 
-def layer_block(new_qkv, cache_kv, resid, cache_len, ff_gain, w_up, w_down, pick):
+def layer_block(new_qkv, cache_kv, resid, cache_len, ff_gain, w_up, w_down):
     series_here, span_slots, triple = new_qkv.shape
     width = resid.shape[2]
     vmem = pltpu.MemorySpace.VMEM if hasattr(pltpu, "MemorySpace") else pltpu.VMEM
     full = pl.BlockSpec(memory_space=vmem)
     return pl.pallas_call(
         block_kernel,
-        in_specs=[pl.BlockSpec(memory_space=pltpu.SMEM)] + [full] * 7,
+        in_specs=[pl.BlockSpec(memory_space=pltpu.SMEM)] + [full] * 6,
         out_specs=full,
-        out_shape=jax.ShapeDtypeStruct((pick.shape[0], width), jnp.bfloat16),
+        out_shape=jax.ShapeDtypeStruct((series_here * span_slots, width), jnp.bfloat16),
         scratch_shapes=[pltpu.VMEM((series_here * span_slots, width), jnp.bfloat16)],
-    )(cache_len, new_qkv, cache_kv, resid, ff_gain.reshape(1, width), w_up, w_down, pick)
+    )(cache_len, new_qkv, cache_kv, resid, ff_gain.reshape(1, width), w_up, w_down)
 
 
 def local(new_qkv, cache_kv, resid, span_len, cache_len, series_perm, ff_gain, w_up, w_down):
@@ -83,6 +80,7 @@
     me = lax.axis_index("req")
     series_here, span_slots, triple = new_qkv.shape
     width = resid.shape[2]
+    layer_out = layer_block(new_qkv, cache_kv, resid, cache_len, ff_gain, w_up, w_down)
     info = jnp.concatenate([span_len, series_perm])
     gathered = lax.all_to_all(
         jnp.broadcast_to(info[None], (group_size, info.shape[0])), "req", 0, 0, tiled=True
@@ -110,10 +108,15 @@
     src_row = jnp.where(src_t < src_len, src_row, -1)
     rows_here = series_here * span_slots
     out_row = jnp.arange(rows_here, dtype=jnp.int32)[:, None]
-    placed = layer_block(new_qkv, cache_kv, resid, cache_len, ff_gain, w_up, w_down, pick)
+    placed = lax.dot_general(
+        pick.reshape(group_size, series_here, -1),
+        layer_out,
+        (((2,), (0,)), ((), ())),
+        preferred_element_type=jnp.float32,
+    ).astype(jnp.bfloat16)
     arrived = lax.all_to_all(placed, "req", 0, 0, tiled=True)
     gather = (src_row.reshape(1, -1) == out_row).astype(jnp.bfloat16)
-    result = jnp.dot(gather, arrived, preferred_element_type=jnp.float32)
+    result = jnp.dot(gather, arrived.reshape(-1, width), preferred_element_type=jnp.float32)
     return result.astype(jnp.bfloat16)
 
 

time: 89.7 us -> 86.4 us (0.963)
  waiting for transfers between devices: 42.6 us -> 34.4 us
  starting transfers between devices: 22.5 us -> 29.2 us
  local copies, waits for them, and re-layouts: 7.3 us -> 5.16 us
  matrix products: 1.08 us -> 2.6 us
    all_to_all x1, waiting for transfers between devices: 8.8 us -> 0.01 us  [local(): lax.all_to_all(jnp.broadcast_to(info[None], (group_size, info.shape[0])),...]
    all_to_all x1, starting transfers between devices: 7.06 us -> 13.8 us  [local(): arrived = lax.all_to_all(placed, 'req', 0, 0, tiled=True)]
    all_to_all x2 -> x0, local copies, waits for them, and re-layouts: 3.81 us -> none  [local(): arrived = lax.all_to_all(placed, 'req', 0, 0, tiled=True)]
    dot_general x1 -> x2, matrix products: 1.08 us -> 2.6 us  [the longest x1 1.52 us: local(): lax.dot_general(pick.reshape(group_size, series_here, -1), layer_out, (((...]
    convert_element_type x1, local copies, waits for them, and re-layouts: 0.94 us -> 2.08 us  [local(): placed = lax.dot_general(pick.reshape(group_size, series_here, -1), layer...]
  transfers between devices with their start and end apart: 2 -> 2, of which waited for: 2 -> 1; matrix products, arithmetic and copies ran while one was open for 3% -> 3% of each run, Pallas kernels for 0% -> 15%
where the time goes in v5:
time: 86.4 us; the launch traced here: 86 us
  waiting for transfers between devices  34.4 us (40%)
  starting transfers between devices  29.2 us (34%)
  Pallas kernels  12.5 us (14%)
  local copies, waits for them, and re-layouts  5.16 us (6%)
  matrix products  2.6 us (3%)
  other arithmetic  2.09 us (2%)
    all_to_all x1, waiting for transfers between devices, local(): arrived = lax.all_to_all(placed, 'req', 0, 0, tiled=True)  34.4 us
    all_to_all x1, starting transfers between devices, local(): lax.all_to_all(jnp.broadcast_to(info[None], (group_size, info.shape[0])),...  15.4 us
    all_to_all x1, starting transfers between devices, local(): arrived = lax.all_to_all(placed, 'req', 0, 0, tiled=True)  13.8 us
    pallas_call x1, Pallas kernels, layer_block(): pl.pallas_call(block_kernel, in_specs=[pl.BlockSpec(memory_space=pltpu.SM...  12.5 us
    convert_element_type x1, local copies, waits for them, and re-layouts, local(): placed = lax.dot_general(pick.reshape(group_size, series_here, -1), layer...  2.08 us
  transfers between devices with their start and end apart: 2, of which 1 were waited for; matrix products, arithmetic and copies ran while one was open for 3% of the time, Pallas kernels for 15%

profile of v5, /device:TPU:8, one launch (start us, length us, event | category | flops | bytes accessed | tf_op | source)
XLA Modules:
  0.0 86.0 jit_solution(7150708029876427839)
XLA Ops:
  0.0 0.7 pad_add_fusion
  0.7 0.6 broadcast_in_dim.17
  1.4 15.4 %all-to-all-start = ((s32[128,1,8]{2,1,0:T(1,128)}), s32[128,1,8]{2,1,0:T(1,128)S(1)}, u32[]{:S(2)}, u32[]{:S(2)}) async-start(s32[128,1,8]{2,1,0:T(1,128)} %broadcast_in_dim.17), calls=%async_computation | async-start | bytes 131072 | tf_op jit(solution)/shard_map/all_to_all | solution.py:85
  16.8 0.7 iota_compare_fusion.4
  17.6 0.1 and.66
  17.7 0.1 and.67
  17.8 1.3 %reshape.105.gain_ref = f32[1,1280]{1,0:T(1,128)} reshape(f32[1280]{0:T(1024)} %param.15) | data formatting | bytes 10240 | tf_op jit(solution)/shard_map/reshape | solution.py:75
  19.1 12.5 %shard_map.91 = bf16[128,1280]{1,0:T(8,128)(2,1)} custom-call(s32[4]{0:T(128)} %cache_len_ref.1, bf16[4,32,3840]{2,1,0:T(8,128)(2,1)} %qkv_ref.1, bf16[4,32,2560]{2,1,0:T(8,128)(2,1)} %cache_ref.1, bf16[4,32,1280]{2,1,0:T(8,128)(2,1)} %resid_ref.1, f32[1,1280]{1,0:T(1,128)} %reshape.105.gain_ref, bf16[1280,1280]{1,0:T(8,128)(2,1)} %up_ref.1, ...), custom_call_target="tpu_custom_call" | custom-call | tf_op jit(solution)/shard_map/pallas_call | solution.py:69
  31.6 0.0 all-to-all-done
  31.6 0.1 fusion.12
  31.6 0.1 lt.51
  31.8 0.1 broadcast_in_dim.18
  31.9 0.3 select_reduce_fusion
  32.1 0.1 dynamic_slice.3
  32.3 0.1 copy.16
  32.3 0.1 fusion.10
  32.4 0.1 bitcast_and_fusion
  32.6 1.5 %convolution_convert_fusion = bf16[128,4,1280]{2,0,1:T(8,128)(2,1)S(1)} fusion(pred[128,4,128]{0,2,1:T(32,128)(4,1)S(1)} %bitcast_and_fusion, bf16[128,1280]{1,0:T(8,128)(2,1)} %shard_map.91), kind=kOutput, calls=%fused_computation | convolution fusion | flops 168427520 | bytes 1703936 | tf_op jit(solution)/shard_map/dot_general | solution.py:111
  34.1 2.1 %copy.18 = bf16[128,4,1280]{2,1,0:T(4,128)(2,1)} copy(bf16[128,4,1280]{2,0,1:T(8,128)(2,1)S(1)} %convolution_convert_fusion) | data formatting | bytes 2621440 | tf_op jit(solution)/shard_map/convert_element_type | solution.py:116
  36.2 13.8 %all-to-all-start.1 = ((bf16[128,4,1280]{2,1,0:T(4,128)(2,1)}), bf16[128,4,1280]{2,1,0:T(4,128)(2,1)S(1)}, u32[]{:S(2)}, u32[]{:S(2)}) async-start(bf16[128,4,1280]{2,1,0:T(4,128)(2,1)} %copy.18), calls=%async_computation.1 | async-start | bytes 2621440 | tf_op jit(solution)/shard_map/all_to_all | solution.py:117
  50.0 0.1 reshape.104
  50.1 0.1 fusion.4
  50.2 0.1 eq.54
  50.3 34.4 %all-to-all-done.1 = bf16[128,4,1280]{2,1,0:T(4,128)(2,1)S(1)} async-done(((bf16[128,4,1280]{2,1,0:T(4,128)(2,1)}), bf16[128,4,1280]{2,1,0:T(4,128)(2,1)S(1)}, u32[]{:S(2)}, u32[]{:S(2)}) %all-to-all-start.1) | async-done | bytes 1310752 | tf_op jit(solution)/shard_map/all_to_all | solution.py:117
  84.6 0.3 reshape.106
  84.9 1.1 %convolution_convert_fusion.1 = bf16[128,1280]{1,0:T(8,128)(2,1)} fusion(bf16[512,1280]{1,0:T(8,128)(2,1)S(1)} %reshape.106, s32[512]{0:T(512)S(1)} %eq.54), kind=kOutput, calls=%fused_computation.1 | convolution fusion | flops 168001536 | bytes 1640448 | tf_op jit(solution)/shard_map/dot_general | solution.py:119
  (2 shorter events, 0.0 us)
Async XLA Ops:
  1.4 30.2 %all-to-all-start = ((s32[128,1,8]{2,1,0:T(1,128)}), s32[128,1,8]{2,1,0:T(1,128)S(1)}, u32[]{:S(2)}, u32[]{:S(2)}) async-start(s32[128,1,8]{2,1,0:T(1,128)} %broadcast_in_dim.17), calls=%async_computation | async-start | bytes 131072 | tf_op jit(solution)/shard_map/all_to_all | solution.py:85
  36.2 48.4 %all-to-all-start.1 = ((bf16[128,4,1280]{2,1,0:T(4,128)(2,1)}), bf16[128,4,1280]{2,1,0:T(4,128)(2,1)S(1)}, u32[]{:S(2)}, u32[]{:S(2)}) async-start(bf16[128,4,1280]{2,1,0:T(4,128)(2,1)} %copy.18), calls=%async_computation.1 | async-start | bytes 2621440 | tf_op jit(solution)/shard_map/all_to_all | solution.py:117

commit v6 on v5

--- a/solution.py
+++ b/solution.py
@@ -92,31 +92,75 @@
     all_start = jnp.sum(jnp.where(earlier, all_len[None, :], 0), axis=1)
 
 
+    size_x, size_z = 4, 8
+    size_y = group_size // (size_x * size_z)
+    my_x = me % size_x
+    my_z = (me // size_x) % size_z
+    my_y = me // (size_x * size_z)
+
+    def shift_pairs(step, size, stride):
+        pairs = []
+        for q in range(group_size):
+            c = (q // stride) % size
+            pairs.append((q, q + (((c + step) % size) - c) * stride))
+        return pairs
+
+    per_x = span_slots // size_x
+    xv = (my_x + jnp.arange(size_x, dtype=jnp.int32))[:, None, None] % size_x
+    series_i = jnp.arange(series_here, dtype=jnp.int32)[None, :, None]
+    slot_j = jnp.arange(per_x, dtype=jnp.int32)[None, None, :]
     my_start = lax.dynamic_slice(all_start, (me * series_here,), (series_here,))
-    target = jnp.arange(group_size, dtype=jnp.int32)[None, :, None]
-    slot = jnp.arange(span_slots, dtype=jnp.int32)[None, None, :]
-    my_offset = (target - my_start[:, None, None]) % group_size
-    pick = (my_offset == slot) & (slot < span_len[:, None, None])
-    same = jnp.arange(series_here)[:, None] == jnp.arange(series_here)[None, :]
-    pick = pick.transpose(1, 0, 2)[:, :, None, :] & same[None, :, :, None]
-    pick = pick.reshape(group_size * series_here, series_here * span_slots).astype(jnp.bfloat16)
+    t_x = (xv - my_start[None, :, None]) % size_x + size_x * slot_j
+    live_x = t_x < span_len[None, :, None]
+    col_x = jnp.where(live_x, series_i * span_slots + t_x, -1).reshape(-1)
+    rows_here = series_here * span_slots
+    pick_x = (col_x[:, None] == jnp.arange(rows_here, dtype=jnp.int32)[None, :]).astype(jnp.bfloat16)
+    send_x = jnp.dot(pick_x, layer_out, preferred_element_type=jnp.float32).astype(jnp.bfloat16)
+    send_x = send_x.reshape(size_x, series_here * per_x, width)
+    recv_x = [send_x[0]] + [
+        lax.ppermute(send_x[k], "req", shift_pairs(k, size_x, 1)) for k in range(1, size_x)
+    ]
+    recv_x = jnp.concatenate(recv_x, axis=0)
 
-    src_start = all_start.reshape(group_size, series_here)
-    src_len = all_len.reshape(group_size, series_here)
-    src_t = (me - src_start) % group_size
-    src_row = (src_start + src_t) // group_size
-    src_row = jnp.where(src_t < src_len, src_row, -1)
-    rows_here = series_here * span_slots
-    out_row = jnp.arange(rows_here, dtype=jnp.int32)[:, None]
-    placed = lax.dot_general(
-        pick.reshape(group_size, series_here, -1),
-        layer_out,
-        (((2,), (0,)), ((), ())),
-        preferred_element_type=jnp.float32,
-    ).astype(jnp.bfloat16)
-    arrived = lax.all_to_all(placed, "req", 0, 0, tiled=True)
-    gather = (src_row.reshape(1, -1) == out_row).astype(jnp.bfloat16)
-    result = jnp.dot(gather, arrived.reshape(-1, width), preferred_element_type=jnp.float32)
+    def source_of(src_y, src_z, src_x, i):
+        pos = (src_y * (size_z * size_x) + src_z * size_x + src_x) * series_here + i
+        st = jnp.take(all_start, pos)
+        ln = jnp.take(all_len, pos)
+        t0 = (my_x - st) % size_x
+        base = (st + t0) // size_x
+        return st, ln, t0, base
+
+    kx = jnp.arange(size_x, dtype=jnp.int32)[:, None]
+    ii = jnp.arange(series_here, dtype=jnp.int32)[None, :]
+    _, _, _, base_b = source_of(my_y, my_z, (my_x - kx) % size_x, ii)
+    kz = jnp.arange(size_z, dtype=jnp.int32)[:, None, None]
+    zv = (my_z + kz) % size_z
+    j_b = (zv - base_b[None]) % size_z
+    col_z = (kx[None] * (series_here * per_x) + ii[None] * per_x + j_b).reshape(-1)
+    pick_z = (col_z[:, None] == jnp.arange(rows_here, dtype=jnp.int32)[None, :]).astype(jnp.bfloat16)
+    send_z = jnp.dot(pick_z, recv_x, preferred_element_type=jnp.float32).astype(jnp.bfloat16)
+    send_z = send_z.reshape(size_z, size_x * series_here, width)
+    recv_z = [send_z[0]] + [
+        lax.ppermute(send_z[k], "req", shift_pairs(k, size_z, size_x)) for k in range(1, size_z)
+    ]
+    recv_z = jnp.concatenate(recv_z, axis=0)
+
+    recv_y = [recv_z] + [
+        lax.ppermute(recv_z, "req", shift_pairs(k, size_y, size_x * size_z)) for k in range(1, size_y)
+    ]
+    recv_y = jnp.concatenate(recv_y, axis=0)
+
+    ky = jnp.arange(size_y, dtype=jnp.int32)[:, None, None, None]
+    kz4 = jnp.arange(size_z, dtype=jnp.int32)[None, :, None, None]
+    kx4 = jnp.arange(size_x, dtype=jnp.int32)[None, None, :, None]
+    ii4 = jnp.arange(series_here, dtype=jnp.int32)[None, None, None, :]
+    st, ln, t0, base = source_of((my_y - ky) % size_y, (my_z - kz4) % size_z, (my_x - kx4) % size_x, ii4)
+    t_f = t0 + size_x * ((my_z - base) % size_z)
+    g_f = st + t_f
+    live_f = (t_f < ln) & (g_f % group_size == me)
+    row_f = jnp.where(live_f, g_f // group_size, -1).reshape(-1)
+    gather = (row_f[None, :] == jnp.arange(rows_here, dtype=jnp.int32)[:, None]).astype(jnp.bfloat16)
+    result = jnp.dot(gather, recv_y, preferred_element_type=jnp.float32)
     return result.astype(jnp.bfloat16)
 
 

time: 86.4 us -> 87.4 us (1.012)
  waiting for transfers between devices: 34.4 us -> 16 us
  starting transfers between devices: 29.2 us -> 43.3 us
  local copies, waits for them, and re-layouts: 5.16 us -> 11.1 us
  matrix products: 2.6 us -> 1.64 us
    all_to_all x1 -> x0, waiting for transfers between devices: 34.4 us -> none  [local(): arrived = lax.all_to_all(placed, 'req', 0, 0, tiled=True)]
    ppermute x0 -> x13, starting transfers between devices: none -> 27.9 us  [the longest x7 16.9 us: local(): lax.ppermute(send_z[k], 'req', shift_pairs(k, size_z, size_x))]
    ppermute x0 -> x13, waiting for transfers between devices: none -> 16 us  [the longest x3 10.6 us: local(): lax.ppermute(recv_z, 'req', shift_pairs(k, size_y, size_x * size_z))]
    all_to_all x1 -> x0, starting transfers between devices: 13.8 us -> none  [local(): arrived = lax.all_to_all(placed, 'req', 0, 0, tiled=True)]
    gather x0 -> x6, local copies, waits for them, and re-layouts: none -> 7.99 us  [the longest x4 4.36 us: source_of(): st = jnp.take(all_start, pos)]
    convert_element_type x1 -> x0, local copies, waits for them, and re-layouts: 2.08 us -> none  [local(): placed = lax.dot_general(pick.reshape(group_size, series_here, -1), layer...]
    dot_general x2 -> x3, matrix products: 2.6 us -> 1.64 us  [the longest x1 1.08 us: local(): result = jnp.dot(gather, recv_y, preferred_element_type=jnp.float32)]
  transfers between devices with their start and end apart: 2 -> 14, of which waited for: 1 -> 7; matrix products, arithmetic and copies ran while one was open for 3% -> 11% of each run, Pallas kernels for 15% -> 14%
where the time goes in v6:
time: 87.4 us; the launch traced here: 87.1 us
  starting transfers between devices  43.3 us (50%)
  waiting for transfers between devices  16 us (18%)
  Pallas kernels  12.5 us (14%)
  local copies, waits for them, and re-layouts  11.1 us (13%)
  other arithmetic  2.21 us (3%)
  matrix products  1.64 us (2%)
    ppermute x7, starting transfers between devices, local(): lax.ppermute(send_z[k], 'req', shift_pairs(k, size_z, size_x))  16.9 us
    all_to_all x1, starting transfers between devices, local(): lax.all_to_all(jnp.broadcast_to(info[None], (group_size, info.shape[0])),...  15.4 us
    pallas_call x1, Pallas kernels, layer_block(): pl.pallas_call(block_kernel, in_specs=[pl.BlockSpec(memory_space=pltpu.SM...  12.5 us
    ppermute x3, waiting for transfers between devices, local(): lax.ppermute(recv_z, 'req', shift_pairs(k, size_y, size_x * size_z))  10.6 us
    ppermute x3, starting transfers between devices, local(): lax.ppermute(send_x[k], 'req', shift_pairs(k, size_x, 1))  5.69 us
    ppermute x3, starting transfers between devices, local(): lax.ppermute(recv_z, 'req', shift_pairs(k, size_y, size_x * size_z))  5.29 us
    gather x4, local copies, waits for them, and re-layouts, source_of(): st = jnp.take(all_start, pos)  4.36 us
    gather x2, local copies, waits for them, and re-layouts, source_of(): ln = jnp.take(all_len, pos)  3.63 us
  transfers between devices with their start and end apart: 14, of which 7 were waited for; matrix products, arithmetic and copies ran while one was open for 11% of the time, Pallas kernels for 14%

profile of v6, /device:TPU:8, one launch (start us, length us, event | category | flops | bytes accessed | tf_op | source)
XLA Modules:
  0.0 87.1 jit_solution(17413591411829771640)
XLA Ops:
  0.0 0.7 pad_add_fusion
  0.7 0.7 broadcast_in_dim.27
  1.4 15.4 %all-to-all-start = ((s32[128,1,8]{2,1,0:T(1,128)}), s32[128,1,8]{2,1,0:T(1,128)S(1)}, u32[]{:S(2)}, u32[]{:S(2)}) async-start(s32[128,1,8]{2,1,0:T(1,128)} %broadcast_in_dim.27), calls=%async_computation | async-start | bytes 131072 | tf_op jit(solution)/shard_map/all_to_all | solution.py:85
  17.0 0.1 compare_select_fusion.1
  17.1 0.1 reshape.504
  17.2 0.1 broadcast_add_fusion
  17.2 0.1 broadcast_add_fusion.1
  17.3 0.1 add_multiply_fusion
  17.4 0.1 add.368
  17.5 1.3 %reshape.485.gain_ref = f32[1,1280]{1,0:T(1,128)} reshape(f32[1280]{0:T(1024)} %param.17) | data formatting | bytes 10240 | tf_op jit(solution)/shard_map/reshape | solution.py:75
  18.8 12.5 %shard_map.91 = bf16[128,1280]{1,0:T(8,128)(2,1)} custom-call(s32[4]{0:T(128)} %cache_len_ref.1, bf16[4,32,3840]{2,1,0:T(8,128)(2,1)} %qkv_ref.1, bf16[4,32,2560]{2,1,0:T(8,128)(2,1)} %cache_ref.1, bf16[4,32,1280]{2,1,0:T(8,128)(2,1)} %resid_ref.1, f32[1,1280]{1,0:T(1,128)} %reshape.485.gain_ref, bf16[1280,1280]{1,0:T(8,128)(2,1)} %up_ref.1, ...), custom_call_target="tpu_custom_call" | custom-call | tf_op jit(solution)/shard_map/pallas_call | solution.py:69
  31.3 0.0 all-to-all-done
  31.3 0.1 fusion.43
  31.4 0.1 broadcast_in_dim.28
  31.5 0.1 lt.136
  31.6 0.3 select_reduce_fusion
  31.9 0.7 gather_fusion
  32.5 0.1 reshape.503
  32.6 0.1 add_select_fusion.6
  32.7 0.1 broadcast_subtract_fusion
  32.8 0.1 sub.141
  32.9 0.1 dynamic_slice.3
  33.0 0.1 add_select_fusion.5
  33.1 0.0 copy-done.1
  33.1 0.1 fusion.22
  33.2 0.1 select_n.224
  33.3 0.0 copy-done
  33.3 0.3 convolution_convert_fusion.2
  33.6 1.5 %collective-permute-start = (bf16[32,1280]{1,0:T(8,128)(2,1)S(1)}, bf16[32,1280]{1,0:T(8,128)(2,1)S(1)}, u32[]{:S(2)}, u32[]{:S(2)}) collective-permute-start(bf16[32,1280]{1,0:T(8,128)(2,1)S(1)} %get-tuple-element.18), channel_id=1, source_target_pairs={{0,1},{1,2},{2,3},{3,0},{4,5},{5,6},{6,7},{7,4},{8,9},{9,10},{10,1... | collective-permute-start | bytes 245768 | tf_op jit(solution)/shard_map/ppermute | solution.py:121
  35.1 2.7 %collective-permute-start.1 = (bf16[32,1280]{1,0:T(8,128)(2,1)S(1)}, bf16[32,1280]{1,0:T(8,128)(2,1)S(1)}, u32[]{:S(2)}, u32[]{:S(2)}) collective-permute-start(bf16[32,1280]{1,0:T(8,128)(2,1)S(1)} %get-tuple-element.17), channel_id=1, source_target_pairs={{0,2},{1,3},{2,0},{3,1},{4,6},{5,7},{6,4},{7,5},{8,10},{9,11},{10,... | collective-permute-start | bytes 245768 | tf_op jit(solution)/shard_map/ppermute | solution.py:121
  37.8 1.4 %collective-permute-start.2 = (bf16[32,1280]{1,0:T(8,128)(2,1)S(1)}, bf16[32,1280]{1,0:T(8,128)(2,1)S(1)}, u32[]{:S(2)}, u32[]{:S(2)}) collective-permute-start(bf16[32,1280]{1,0:T(8,128)(2,1)S(1)} %get-tuple-element.16), channel_id=1, source_target_pairs={{0,3},{1,0},{2,1},{3,2},{4,7},{5,4},{6,5},{7,6},{8,11},{9,8},{10,9... | collective-permute-start | bytes 245768 | tf_op jit(solution)/shard_map/ppermute | solution.py:121
  39.3 0.9 %collective-permute-done = bf16[32,1280]{1,0:T(8,128)(2,1)S(1)} collective-permute-done((bf16[32,1280]{1,0:T(8,128)(2,1)S(1)}, bf16[32,1280]{1,0:T(8,128)(2,1)S(1)}, u32[]{:S(2)}, u32[]{:S(2)}) %collective-permute-start) | collective-permute-done | bytes 81952 | tf_op jit(solution)/shard_map/ppermute | solution.py:121
  40.2 1.0 %collective-permute-done.1 = bf16[32,1280]{1,0:T(8,128)(2,1)S(1)} collective-permute-done((bf16[32,1280]{1,0:T(8,128)(2,1)S(1)}, bf16[32,1280]{1,0:T(8,128)(2,1)S(1)}, u32[]{:S(2)}, u32[]{:S(2)}) %collective-permute-start.1) | collective-permute-done | bytes 81952 | tf_op jit(solution)/shard_map/ppermute | solution.py:121
  41.2 1.1 %collective-permute-done.2 = bf16[32,1280]{1,0:T(8,128)(2,1)S(1)} collective-permute-done((bf16[32,1280]{1,0:T(8,128)(2,1)S(1)}, bf16[32,1280]{1,0:T(8,128)(2,1)S(1)}, u32[]{:S(2)}, u32[]{:S(2)}) %collective-permute-start.2) | collective-permute-done | bytes 81952 | tf_op jit(solution)/shard_map/ppermute | solution.py:121
  42.3 0.3 convolution_convert_fusion.1
  42.6 1.5 %collective-permute-start.3 = (bf16[16,1280]{1,0:T(8,128)(2,1)S(1)}, bf16[16,1280]{1,0:T(8,128)(2,1)S(1)}, u32[]{:S(2)}, u32[]{:S(2)}) collective-permute-start(bf16[16,1280]{1,0:T(8,128)(2,1)S(1)} %get-tuple-element.14), channel_id=1, source_target_pairs={{0,4},{1,5},{2,6},{3,7},{4,8},{5,9},{6,10},{7,11},{8,12},{9,13},{1... | collective-permute-start | bytes 122888 | tf_op jit(solution)/shard_map/ppermute | solution.py:144
  44.1 0.1 compare_select_fusion
  44.3 0.1 reshape.515
  44.4 2.5 %collective-permute-start.4 = (bf16[16,1280]{1,0:T(8,128)(2,1)S(1)}, bf16[16,1280]{1,0:T(8,128)(2,1)S(1)}, u32[]{:S(2)}, u32[]{:S(2)}) collective-permute-start(bf16[16,1280]{1,0:T(8,128)(2,1)S(1)} %get-tuple-element.13), channel_id=1, source_target_pairs={{0,8},{1,9},{2,10},{3,11},{4,12},{5,13},{6,14},{7,15},{8,16},{9,17... | collective-permute-start | bytes 122888 | tf_op jit(solution)/shard_map/ppermute | solution.py:144
  46.9 2.7 %collective-permute-start.5 = (bf16[16,1280]{1,0:T(8,128)(2,1)S(1)}, bf16[16,1280]{1,0:T(8,128)(2,1)S(1)}, u32[]{:S(2)}, u32[]{:S(2)}) collective-permute-start(bf16[16,1280]{1,0:T(8,128)(2,1)S(1)} %get-tuple-element.12), channel_id=1, source_target_pairs={{0,12},{1,13},{2,14},{3,15},{4,16},{5,17},{6,18},{7,19},{8,20},{9,... | collective-permute-start | bytes 122888 | tf_op jit(solution)/shard_map/ppermute | solution.py:144
  49.6 2.3 %collective-permute-start.6 = (bf16[16,1280]{1,0:T(8,128)(2,1)S(1)}, bf16[16,1280]{1,0:T(8,128)(2,1)S(1)}, u32[]{:S(2)}, u32[]{:S(2)}) collective-permute-start(bf16[16,1280]{1,0:T(8,128)(2,1)S(1)} %get-tuple-element.11), channel_id=1, source_target_pairs={{0,16},{1,17},{2,18},{3,19},{4,20},{5,21},{6,22},{7,23},{8,24},{9,... | collective-permute-start | bytes 122888 | tf_op jit(solution)/shard_map/ppermute | solution.py:144
  51.9 2.8 %collective-permute-start.7 = (bf16[16,1280]{1,0:T(8,128)(2,1)S(1)}, bf16[16,1280]{1,0:T(8,128)(2,1)S(1)}, u32[]{:S(2)}, u32[]{:S(2)}) collective-permute-start(bf16[16,1280]{1,0:T(8,128)(2,1)S(1)} %get-tuple-element.10), channel_id=1, source_target_pairs={{0,20},{1,21},{2,22},{3,23},{4,24},{5,25},{6,26},{7,27},{8,28},{9,... | collective-permute-start | bytes 122888 | tf_op jit(solution)/shard_map/ppermute | solution.py:144
  54.7 0.0 collective-permute-done.3
  54.7 3.5 %collective-permute-start.8 = (bf16[16,1280]{1,0:T(8,128)(2,1)S(1)}, bf16[16,1280]{1,0:T(8,128)(2,1)S(1)}, u32[]{:S(2)}, u32[]{:S(2)}) collective-permute-start(bf16[16,1280]{1,0:T(8,128)(2,1)S(1)} %get-tuple-element.9), channel_id=1, source_target_pairs={{0,24},{1,25},{2,26},{3,27},{4,28},{5,29},{6,30},{7,31},{8,0},{9,1... | collective-permute-start | bytes 122888 | tf_op jit(solution)/shard_map/ppermute | solution.py:144
  58.2 0.0 collective-permute-done.4
  58.2 1.5 %collective-permute-start.9 = (bf16[16,1280]{1,0:T(8,128)(2,1)S(1)}, bf16[16,1280]{1,0:T(8,128)(2,1)S(1)}, u32[]{:S(2)}, u32[]{:S(2)}) collective-permute-start(bf16[16,1280]{1,0:T(8,128)(2,1)S(1)} %get-tuple-element.8), channel_id=1, source_target_pairs={{0,28},{1,29},{2,30},{3,31},{4,0},{5,1},{6,2},{7,3},{8,4},{9,5},{1... | collective-permute-start | bytes 122888 | tf_op jit(solution)/shard_map/ppermute | solution.py:144
  59.7 0.0 collective-permute-done.5
  59.8 0.0 collective-permute-done.6
  59.8 0.0 collective-permute-done.7
  59.8 0.3 collective-permute-done.8
  60.1 2.2 %collective-permute-done.9 = bf16[16,1280]{1,0:T(8,128)(2,1)S(1)} collective-permute-done((bf16[16,1280]{1,0:T(8,128)(2,1)S(1)}, bf16[16,1280]{1,0:T(8,128)(2,1)S(1)}, u32[]{:S(2)}, u32[]{:S(2)}) %collective-permute-start.9) | collective-permute-done | bytes 40992 | tf_op jit(solution)/shard_map/ppermute | solution.py:144
  62.3 1.7 %collective-permute-start.10 = (bf16[128,1280]{1,0:T(8,128)(2,1)S(1)}, bf16[128,1280]{1,0:T(8,128)(2,1)S(1)}, u32[]{:S(2)}, u32[]{:S(2)}) collective-permute-start(bf16[128,1280]{1,0:T(8,128)(2,1)S(1)} %get-tuple-element.21), channel_id=1, source_target_pairs={{0,32},{1,33},{2,34},{3,35},{4,36},{5,37},{6,38},{7,39},{8,40},{9,... | collective-permute-start | bytes 983048 | tf_op jit(solution)/shard_map/ppermute | solution.py:149
  64.0 3.5 %gather_fusion.1 = s32[512]{0:T(512)S(1)} fusion(s32[512]{0:T(512)S(1)} %select_reduce_fusion, s32[1024]{0:T(1024)S(1)} %pad_clamp_fusion.1), kind=kCustom, calls=%fused_computation.clone | custom fusion | bytes 6144 | tf_op jit(solution)/shard_map/jit(_take)/gather | solution.py:127
  67.5 3.5 %gather_fusion.2 = s32[512]{0:T(512)S(1)} fusion(s32[512]{0:T(512)S(1)} %broadcast_in_dim.28, s32[1024]{0:T(1024)S(1)} %pad_clamp_fusion.1), kind=kCustom, calls=%fused_computation.1.clone | custom fusion | bytes 6144 | tf_op jit(solution)/shard_map/jit(_take)/gather | solution.py:128
  71.0 0.1 reshape.518
  71.1 0.1 reshape.522
  71.3 0.9 %collective-permute-start.11 = (bf16[128,1280]{1,0:T(8,128)(2,1)S(1)}, bf16[128,1280]{1,0:T(8,128)(2,1)S(1)}, u32[]{:S(2)}, u32[]{:S(2)}) collective-permute-start(bf16[128,1280]{1,0:T(8,128)(2,1)S(1)} %get-tuple-element.21), channel_id=1, source_target_pairs={{0,64},{1,65},{2,66},{3,67},{4,68},{5,69},{6,70},{7,71},{8,72},{9,... | collective-permute-start | bytes 983048 | tf_op jit(solution)/shard_map/ppermute | solution.py:149
  72.2 0.4 fusion.15
  72.6 0.1 eq.74
  72.8 2.7 %collective-permute-start.12 = (bf16[128,1280]{1,0:T(8,128)(2,1)S(1)}, bf16[128,1280]{1,0:T(8,128)(2,1)S(1)}, u32[]{:S(2)}, u32[]{:S(2)}) collective-permute-start(bf16[128,1280]{1,0:T(8,128)(2,1)S(1)} %get-tuple-element.21), channel_id=1, source_target_pairs={{0,96},{1,97},{2,98},{3,99},{4,100},{5,101},{6,102},{7,103},{8,104... | collective-permute-start | bytes 983048 | tf_op jit(solution)/shard_map/ppermute | solution.py:149
  75.4 0.0 collective-permute-done.10
  75.5 7.3 %collective-permute-done.11 = bf16[128,1280]{1,0:T(8,128)(2,1)S(1)} collective-permute-done((bf16[128,1280]{1,0:T(8,128)(2,1)S(1)}, bf16[128,1280]{1,0:T(8,128)(2,1)S(1)}, u32[]{:S(2)}, u32[]{:S(2)}) %collective-permute-start.11) | collective-permute-done | bytes 327712 | tf_op jit(solution)/shard_map/ppermute | solution.py:149
  82.7 3.3 %collective-permute-done.12 = bf16[128,1280]{1,0:T(8,128)(2,1)S(1)} collective-permute-done((bf16[128,1280]{1,0:T(8,128)(2,1)S(1)}, bf16[128,1280]{1,0:T(8,128)(2,1)S(1)}, u32[]{:S(2)}, u32[]{:S(2)}) %collective-permute-start.12) | collective-permute-done | bytes 327712 | tf_op jit(solution)/shard_map/ppermute | solution.py:149
  86.1 1.1 %convolution_convert_fusion = bf16[128,1280]{1,0:T(8,128)(2,1)} fusion(bf16[512,1280]{1,0:T(8,128)(2,1)S(1)} %constant_dynamic-update-slice_fusion.8, s32[512]{0:T(512)S(1)} %eq.74), kind=kOutput, calls=%fused_computation.3 | convolution fusion | flops 168001536 | bytes 1640448 | tf_op jit(solution)/shard_map/dot_general | solution.py:163
  (24 shorter events, 0.3 us)
Async XLA Ops:
  1.4 29.9 %all-to-all-start = ((s32[128,1,8]{2,1,0:T(1,128)}), s32[128,1,8]{2,1,0:T(1,128)S(1)}, u32[]{:S(2)}, u32[]{:S(2)}) async-start(s32[128,1,8]{2,1,0:T(1,128)} %broadcast_in_dim.27), calls=%async_computation | async-start | bytes 131072 | tf_op jit(solution)/shard_map/all_to_all | solution.py:85
  31.3 1.8 %copy-start.1 = (s32[4]{0:T(128)S(1)}, s32[4]{0:T(128)}, u32[]{:S(2)}) copy-start(s32[4]{0:T(128)} %param.14) | copy-start | bytes 52
  31.3 2.0 %copy-start = (bf16[128,1280]{1,0:T(8,128)(2,1)S(1)}, bf16[128,1280]{1,0:T(8,128)(2,1)}, u32[]{:S(2)}) copy-start(bf16[128,1280]{1,0:T(8,128)(2,1)} %shard_map.91) | copy-start | bytes 983044
  33.6 6.6 %collective-permute-start = (bf16[32,1280]{1,0:T(8,128)(2,1)S(1)}, bf16[32,1280]{1,0:T(8,128)(2,1)S(1)}, u32[]{:S(2)}, u32[]{:S(2)}) collective-permute-start(bf16[32,1280]{1,0:T(8,128)(2,1)S(1)} %get-tuple-element.18), channel_id=1, source_target_pairs={{0,1},{1,2},{2,3},{3,0},{4,5},{5,6},{6,7},{7,4},{8,9},{9,10},{10,1... | collective-permute-start | bytes 245768 | tf_op jit(solution)/shard_map/ppermute | solution.py:121
  35.1 6.1 %collective-permute-start.1 = (bf16[32,1280]{1,0:T(8,128)(2,1)S(1)}, bf16[32,1280]{1,0:T(8,128)(2,1)S(1)}, u32[]{:S(2)}, u32[]{:S(2)}) collective-permute-start(bf16[32,1280]{1,0:T(8,128)(2,1)S(1)} %get-tuple-element.17), channel_id=1, source_target_pairs={{0,2},{1,3},{2,0},{3,1},{4,6},{5,7},{6,4},{7,5},{8,10},{9,11},{10,... | collective-permute-start | bytes 245768 | tf_op jit(solution)/shard_map/ppermute | solution.py:121
  37.8 4.4 %collective-permute-start.2 = (bf16[32,1280]{1,0:T(8,128)(2,1)S(1)}, bf16[32,1280]{1,0:T(8,128)(2,1)S(1)}, u32[]{:S(2)}, u32[]{:S(2)}) collective-permute-start(bf16[32,1280]{1,0:T(8,128)(2,1)S(1)} %get-tuple-element.16), channel_id=1, source_target_pairs={{0,3},{1,0},{2,1},{3,2},{4,7},{5,4},{6,5},{7,6},{8,11},{9,8},{10,9... | collective-permute-start | bytes 245768 | tf_op jit(solution)/shard_map/ppermute | solution.py:121
  42.6 12.1 %collective-permute-start.3 = (bf16[16,1280]{1,0:T(8,128)(2,1)S(1)}, bf16[16,1280]{1,0:T(8,128)(2,1)S(1)}, u32[]{:S(2)}, u32[]{:S(2)}) collective-permute-start(bf16[16,1280]{1,0:T(8,128)(2,1)S(1)} %get-tuple-element.14), channel_id=1, source_target_pairs={{0,4},{1,5},{2,6},{3,7},{4,8},{5,9},{6,10},{7,11},{8,12},{9,13},{1... | collective-permute-start | bytes 122888 | tf_op jit(solution)/shard_map/ppermute | solution.py:144
  44.4 13.9 %collective-permute-start.4 = (bf16[16,1280]{1,0:T(8,128)(2,1)S(1)}, bf16[16,1280]{1,0:T(8,128)(2,1)S(1)}, u32[]{:S(2)}, u32[]{:S(2)}) collective-permute-start(bf16[16,1280]{1,0:T(8,128)(2,1)S(1)} %get-tuple-element.13), channel_id=1, source_target_pairs={{0,8},{1,9},{2,10},{3,11},{4,12},{5,13},{6,14},{7,15},{8,16},{9,17... | collective-permute-start | bytes 122888 | tf_op jit(solution)/shard_map/ppermute | solution.py:144
  46.9 12.9 %collective-permute-start.5 = (bf16[16,1280]{1,0:T(8,128)(2,1)S(1)}, bf16[16,1280]{1,0:T(8,128)(2,1)S(1)}, u32[]{:S(2)}, u32[]{:S(2)}) collective-permute-start(bf16[16,1280]{1,0:T(8,128)(2,1)S(1)} %get-tuple-element.12), channel_id=1, source_target_pairs={{0,12},{1,13},{2,14},{3,15},{4,16},{5,17},{6,18},{7,19},{8,20},{9,... | collective-permute-start | bytes 122888 | tf_op jit(solution)/shard_map/ppermute | solution.py:144
  49.6 10.1 %collective-permute-start.6 = (bf16[16,1280]{1,0:T(8,128)(2,1)S(1)}, bf16[16,1280]{1,0:T(8,128)(2,1)S(1)}, u32[]{:S(2)}, u32[]{:S(2)}) collective-permute-start(bf16[16,1280]{1,0:T(8,128)(2,1)S(1)} %get-tuple-element.11), channel_id=1, source_target_pairs={{0,16},{1,17},{2,18},{3,19},{4,20},{5,21},{6,22},{7,23},{8,24},{9,... | collective-permute-start | bytes 122888 | tf_op jit(solution)/shard_map/ppermute | solution.py:144
  51.9 7.9 %collective-permute-start.7 = (bf16[16,1280]{1,0:T(8,128)(2,1)S(1)}, bf16[16,1280]{1,0:T(8,128)(2,1)S(1)}, u32[]{:S(2)}, u32[]{:S(2)}) collective-permute-start(bf16[16,1280]{1,0:T(8,128)(2,1)S(1)} %get-tuple-element.10), channel_id=1, source_target_pairs={{0,20},{1,21},{2,22},{3,23},{4,24},{5,25},{6,26},{7,27},{8,28},{9,... | collective-permute-start | bytes 122888 | tf_op jit(solution)/shard_map/ppermute | solution.py:144
  54.7 5.4 %collective-permute-start.8 = (bf16[16,1280]{1,0:T(8,128)(2,1)S(1)}, bf16[16,1280]{1,0:T(8,128)(2,1)S(1)}, u32[]{:S(2)}, u32[]{:S(2)}) collective-permute-start(bf16[16,1280]{1,0:T(8,128)(2,1)S(1)} %get-tuple-element.9), channel_id=1, source_target_pairs={{0,24},{1,25},{2,26},{3,27},{4,28},{5,29},{6,30},{7,31},{8,0},{9,1... | collective-permute-start | bytes 122888 | tf_op jit(solution)/shard_map/ppermute | solution.py:144
  58.2 4.1 %collective-permute-start.9 = (bf16[16,1280]{1,0:T(8,128)(2,1)S(1)}, bf16[16,1280]{1,0:T(8,128)(2,1)S(1)}, u32[]{:S(2)}, u32[]{:S(2)}) collective-permute-start(bf16[16,1280]{1,0:T(8,128)(2,1)S(1)} %get-tuple-element.8), channel_id=1, source_target_pairs={{0,28},{1,29},{2,30},{3,31},{4,0},{5,1},{6,2},{7,3},{8,4},{9,5},{1... | collective-permute-start | bytes 122888 | tf_op jit(solution)/shard_map/ppermute | solution.py:144
  62.3 13.1 %collective-permute-start.10 = (bf16[128,1280]{1,0:T(8,128)(2,1)S(1)}, bf16[128,1280]{1,0:T(8,128)(2,1)S(1)}, u32[]{:S(2)}, u32[]{:S(2)}) collective-permute-start(bf16[128,1280]{1,0:T(8,128)(2,1)S(1)} %get-tuple-element.21), channel_id=1, source_target_pairs={{0,32},{1,33},{2,34},{3,35},{4,36},{5,37},{6,38},{7,39},{8,40},{9,... | collective-permute-start | bytes 983048 | tf_op jit(solution)/shard_map/ppermute | solution.py:149
  71.3 11.5 %collective-permute-start.11 = (bf16[128,1280]{1,0:T(8,128)(2,1)S(1)}, bf16[128,1280]{1,0:T(8,128)(2,1)S(1)}, u32[]{:S(2)}, u32[]{:S(2)}) collective-permute-start(bf16[128,1280]{1,0:T(8,128)(2,1)S(1)} %get-tuple-element.21), channel_id=1, source_target_pairs={{0,64},{1,65},{2,66},{3,67},{4,68},{5,69},{6,70},{7,71},{8,72},{9,... | collective-permute-start | bytes 983048 | tf_op jit(solution)/shard_map/ppermute | solution.py:149
  72.8 13.3 %collective-permute-start.12 = (bf16[128,1280]{1,0:T(8,128)(2,1)S(1)}, bf16[128,1280]{1,0:T(8,128)(2,1)S(1)}, u32[]{:S(2)}, u32[]{:S(2)}) collective-permute-start(bf16[128,1280]{1,0:T(8,128)(2,1)S(1)} %get-tuple-element.21), channel_id=1, source_target_pairs={{0,96},{1,97},{2,98},{3,99},{4,100},{5,101},{6,102},{7,103},{8,104... | collective-permute-start | bytes 983048 | tf_op jit(solution)/shard_map/ppermute | solution.py:149

commit v7 on v6

--- a/solution.py
+++ b/solution.py
@@ -75,15 +75,18 @@
     )(cache_len, new_qkv, cache_kv, resid, ff_gain.reshape(1, width), w_up, w_down)
 
 
+REQ = ("y", "z", "x")
+
+
 def local(new_qkv, cache_kv, resid, span_len, cache_len, series_perm, ff_gain, w_up, w_down):
-    group_size = lax.axis_size("req")
-    me = lax.axis_index("req")
+    group_size = lax.axis_size(REQ)
+    me = lax.axis_index(REQ)
     series_here, span_slots, triple = new_qkv.shape
     width = resid.shape[2]
     layer_out = layer_block(new_qkv, cache_kv, resid, cache_len, ff_gain, w_up, w_down)
     info = jnp.concatenate([span_len, series_perm])
     gathered = lax.all_to_all(
-        jnp.broadcast_to(info[None], (group_size, info.shape[0])), "req", 0, 0, tiled=True
+        jnp.broadcast_to(info[None], (group_size, info.shape[0])), REQ, 0, 0, tiled=True
     )
     all_len = gathered[:, :series_here].reshape(-1)
     all_perm = gathered[:, series_here:].reshape(-1)
@@ -92,18 +95,15 @@
     all_start = jnp.sum(jnp.where(earlier, all_len[None, :], 0), axis=1)
 
 
-    size_x, size_z = 4, 8
-    size_y = group_size // (size_x * size_z)
-    my_x = me % size_x
-    my_z = (me // size_x) % size_z
-    my_y = me // (size_x * size_z)
+    size_x, size_z, size_y = lax.axis_size("x"), lax.axis_size("z"), lax.axis_size("y")
+    my_x = lax.axis_index("x")
+    my_z = lax.axis_index("z")
+    my_y = lax.axis_index("y")
 
-    def shift_pairs(step, size, stride):
-        pairs = []
-        for q in range(group_size):
-            c = (q // stride) % size
-            pairs.append((q, q + (((c + step) % size) - c) * stride))
-        return pairs
+    def rotate(blocks, axis, size, me_here):
+        blocks = jnp.roll(blocks, me_here, axis=0)
+        got = lax.all_to_all(blocks, axis, 0, 0, tiled=True)
+        return jnp.roll(got[::-1], me_here + 1, axis=0)
 
     per_x = span_slots // size_x
     xv = (my_x + jnp.arange(size_x, dtype=jnp.int32))[:, None, None] % size_x
@@ -117,15 +117,14 @@
     pick_x = (col_x[:, None] == jnp.arange(rows_here, dtype=jnp.int32)[None, :]).astype(jnp.bfloat16)
     send_x = jnp.dot(pick_x, layer_out, preferred_element_type=jnp.float32).astype(jnp.bfloat16)
     send_x = send_x.reshape(size_x, series_here * per_x, width)
-    recv_x = [send_x[0]] + [
-        lax.ppermute(send_x[k], "req", shift_pairs(k, size_x, 1)) for k in range(1, size_x)
-    ]
-    recv_x = jnp.concatenate(recv_x, axis=0)
+    recv_x = rotate(send_x, "x", size_x, my_x).reshape(-1, width)
 
     def source_of(src_y, src_z, src_x, i):
         pos = (src_y * (size_z * size_x) + src_z * size_x + src_x) * series_here + i
-        st = jnp.take(all_start, pos)
-        ln = jnp.take(all_len, pos)
+        every = jnp.arange(all_start.shape[0], dtype=jnp.int32)
+        hit = pos[..., None] == every
+        st = jnp.sum(jnp.where(hit, all_start, 0), axis=-1)
+        ln = jnp.sum(jnp.where(hit, all_len, 0), axis=-1)
         t0 = (my_x - st) % size_x
         base = (st + t0) // size_x
         return st, ln, t0, base
@@ -140,15 +139,11 @@
     pick_z = (col_z[:, None] == jnp.arange(rows_here, dtype=jnp.int32)[None, :]).astype(jnp.bfloat16)
     send_z = jnp.dot(pick_z, recv_x, preferred_element_type=jnp.float32).astype(jnp.bfloat16)
     send_z = send_z.reshape(size_z, size_x * series_here, width)
-    recv_z = [send_z[0]] + [
-        lax.ppermute(send_z[k], "req", shift_pairs(k, size_z, size_x)) for k in range(1, size_z)
-    ]
-    recv_z = jnp.concatenate(recv_z, axis=0)
+    recv_z = rotate(send_z, "z", size_z, my_z).reshape(-1, width)
 
-    recv_y = [recv_z] + [
-        lax.ppermute(recv_z, "req", shift_pairs(k, size_y, size_x * size_z)) for k in range(1, size_y)
-    ]
-    recv_y = jnp.concatenate(recv_y, axis=0)
+    recv_y = rotate(
+        jnp.broadcast_to(recv_z[None], (size_y,) + recv_z.shape), "y", size_y, my_y
+    ).reshape(-1, width)
 
     ky = jnp.arange(size_y, dtype=jnp.int32)[:, None, None, None]
     kz4 = jnp.arange(size_z, dtype=jnp.int32)[None, :, None, None]
@@ -165,16 +160,20 @@
 
 
 def solution(mesh):
+    grp = mesh.shape["grp"]
+    req = mesh.shape["req"]
+    fine = jax.sharding.Mesh(mesh.devices.reshape(grp, req // 32, 8, 4), ("grp",) + REQ)
+    rows = ("grp",) + REQ
     in_specs = (
-        P(("grp", "req"), None, None),
-        P(("grp", "req"), None, None),
-        P(("grp", "req"), None, None),
-        P(("grp", "req")),
-        P(("grp", "req")),
-        P(("grp", "req")),
+        P(rows, None, None),
+        P(rows, None, None),
+        P(rows, None, None),
+        P(rows),
+        P(rows),
+        P(rows),
         P(),
         P(),
         P(),
     )
-    out_specs = P(("grp", "req"), None)
-    return jax.shard_map(local, mesh=mesh, in_specs=in_specs, out_specs=out_specs, check_vma=False)
+    out_specs = P(rows, None)
+    return jax.shard_map(local, mesh=fine, in_specs=in_specs, out_specs=out_specs, check_vma=False)

time: 87.4 us -> 87.2 us (level)
  waiting for transfers between devices: 16 us -> 28 us
  starting transfers between devices: 43.3 us -> 31.5 us
  local copies, waits for them, and re-layouts: 11.1 us -> 3.45 us
  other arithmetic: 2.21 us -> 8.38 us
  matrix products: 1.64 us -> 2.62 us
    all_to_all x0 -> x3, waiting for transfers between devices: none -> 28 us  [rotate(): got = lax.all_to_all(blocks, axis, 0, 0, tiled=True)]
    ppermute x13 -> x0, starting transfers between devices: 27.9 us -> none  [the longest x7 16.9 us: local(): lax.ppermute(send_z[k], 'req', shift_pairs(k, size_z, size_x))]
    ppermute x13 -> x0, waiting for transfers between devices: 16 us -> none  [the longest x3 10.6 us: local(): lax.ppermute(recv_z, 'req', shift_pairs(k, size_y, size_x * size_z))]
    all_to_all x0 -> x3, starting transfers between devices: none -> 16 us  [rotate(): got = lax.all_to_all(blocks, axis, 0, 0, tiled=True)]
    gather x6 -> x0, local copies, waits for them, and re-layouts: 7.99 us -> none  [the longest x4 4.36 us: source_of(): st = jnp.take(all_start, pos)]
    concatenate x0 -> x6, other arithmetic: none -> 4.02 us  [the longest x3 3.26 us: rotate(): blocks = jnp.roll(blocks, me_here, axis=0)]
    reduce_sum x0 -> x2, other arithmetic: none -> 2.72 us  [the longest x1 2.5 us: source_of(): ln = jnp.sum(jnp.where(hit, all_len, 0), axis=-1)]
    dot_general x1, matrix products: 0.28 us -> 1.26 us  [local(): jnp.dot(pick_x, layer_out, preferred_element_type=jnp.float32)]
  transfers between devices with their start and end apart: 14 -> 4, of which waited for: 7 -> 3; matrix products, arithmetic and copies ran while one was open for 11% -> 6% of each run, Pallas kernels for 14% -> 14%
where the time goes in v7:
time: 87.2 us; the launch traced here: 86.6 us
  starting transfers between devices  31.5 us (36%)
  waiting for transfers between devices  28 us (32%)
  Pallas kernels  12.5 us (14%)
  other arithmetic  8.38 us (10%)
  local copies, waits for them, and re-layouts  3.45 us (4%)
  matrix products  2.62 us (3%)
    all_to_all x3, waiting for transfers between devices, rotate(): got = lax.all_to_all(blocks, axis, 0, 0, tiled=True)  28 us
    all_to_all x3, starting transfers between devices, rotate(): got = lax.all_to_all(blocks, axis, 0, 0, tiled=True)  16 us
    all_to_all x1, starting transfers between devices, local(): lax.all_to_all(jnp.broadcast_to(info[None], (group_size, info.shape[0])),...  15.4 us
    pallas_call x1, Pallas kernels, layer_block(): pl.pallas_call(block_kernel, in_specs=[pl.BlockSpec(memory_space=pltpu.SM...  12.5 us
    concatenate x3, other arithmetic, rotate(): blocks = jnp.roll(blocks, me_here, axis=0)  3.26 us
    reduce_sum x1, other arithmetic, source_of(): ln = jnp.sum(jnp.where(hit, all_len, 0), axis=-1)  2.5 us
  transfers between devices with their start and end apart: 4, of which 3 were waited for; matrix products, arithmetic and copies ran while one was open for 6% of the time, Pallas kernels for 14%

profile of v7, /device:TPU:8, one launch (start us, length us, event | category | flops | bytes accessed | tf_op | source)
XLA Modules:
  0.0 86.6 jit_solution(14002599040316545347)
XLA Ops:
  0.0 0.7 pad_add_fusion
  0.7 0.7 broadcast_in_dim.46
  1.4 15.4 %all-to-all-start = ((s32[128,1,8]{2,1,0:T(1,128)}), s32[128,1,8]{2,1,0:T(1,128)S(1)}, u32[]{:S(2)}, u32[]{:S(2)}) async-start(s32[128,1,8]{2,1,0:T(1,128)} %broadcast_in_dim.46), calls=%async_computation | async-start | bytes 131072 | tf_op jit(solution)/shard_map/all_to_all | solution.py:88
  16.9 0.1 iota_add_fusion.1
  17.0 0.1 broadcast_add_fusion
  17.1 1.3 %reshape.502.gain_ref = f32[1,1280]{1,0:T(1,128)} reshape(f32[1280]{0:T(1024)} %param.21) | data formatting | bytes 10240 | tf_op jit(solution)/shard_map/reshape | solution.py:75
  18.4 0.1 add.392
  18.5 0.0 copy-start
  18.5 12.5 %shard_map.91 = bf16[128,1280]{1,0:T(8,128)(2,1)} custom-call(s32[4]{0:T(128)} %cache_len_ref.1, bf16[4,32,3840]{2,1,0:T(8,128)(2,1)} %qkv_ref.1, bf16[4,32,2560]{2,1,0:T(8,128)(2,1)} %cache_ref.1, bf16[4,32,1280]{2,1,0:T(8,128)(2,1)} %resid_ref.1, f32[1,1280]{1,0:T(1,128)} %reshape.502.gain_ref, bf16[1280,1280]{1,0:T(8,128)(2,1)} %up_ref.1, ...), custom_call_target="tpu_custom_call" | custom-call | tf_op jit(solution)/shard_map/pallas_call | solution.py:69
  31.0 0.0 all-to-all-done
  31.0 0.1 fusion.36
  31.1 0.1 lt.130
  31.2 0.1 broadcast_in_dim.74
  31.3 0.3 select_reduce_fusion.2
  31.6 0.1 dynamic_slice.12
  31.7 0.2 select_reduce_fusion.3
  31.9 0.1 add_select_fusion
  32.0 0.0 copy-done
  32.0 0.1 fusion.9
  32.0 0.1 select_n.228
  32.1 1.3 %convolution_convert_fusion.2 = bf16[128,1280]{1,0:T(8,128)(2,1)S(1)} fusion(bf16[128,1280]{1,0:T(8,128)(2,1)} %shard_map.91, s32[128]{0:T(128)S(1)} %select_n.228), kind=kOutput, calls=%fused_computation.6 | convolution fusion | flops 42123264 | bytes 655872 | tf_op jit(solution)/shard_map/dot_general | solution.py:118
  33.4 0.9 fusion.5
  34.3 4.3 %all-to-all-start.1 = ((bf16[4,32,1280]{2,1,0:T(8,128)(2,1)}), bf16[4,32,1280]{2,1,0:T(8,128)(2,1)S(1)}, u32[]{:S(2)}, u32[]{:S(2)}) async-start(bf16[4,32,1280]{2,1,0:T(8,128)(2,1)} %fusion.5), calls=%async_computation.1 | async-start | bytes 655360 | tf_op jit(solution)/shard_map/all_to_all | solution.py:105
  38.5 0.1 broadcast_subtract_fusion
  38.6 0.1 sub.149
  38.7 6.8 %all-to-all-done.1 = bf16[4,32,1280]{2,1,0:T(8,128)(2,1)S(1)} async-done(((bf16[4,32,1280]{2,1,0:T(8,128)(2,1)}), bf16[4,32,1280]{2,1,0:T(8,128)(2,1)S(1)}, u32[]{:S(2)}, u32[]{:S(2)}) %all-to-all-start.1) | async-done | bytes 327712 | tf_op jit(solution)/shard_map/all_to_all | solution.py:105
  45.6 0.1 fusion.4
  45.7 0.3 convolution_convert_fusion.1
  46.0 0.9 fusion.3
  46.9 6.8 %all-to-all-start.2 = ((bf16[8,16,1280]{2,1,0:T(8,128)(2,1)}), bf16[8,16,1280]{2,1,0:T(8,128)(2,1)S(1)}, u32[]{:S(2)}, u32[]{:S(2)}) async-start(bf16[8,16,1280]{2,1,0:T(8,128)(2,1)} %fusion.3), calls=%async_computation.2 | async-start | bytes 655360 | tf_op jit(solution)/shard_map/all_to_all | solution.py:105
  53.6 11.3 %all-to-all-done.2 = bf16[8,16,1280]{2,1,0:T(8,128)(2,1)S(1)} async-done(((bf16[8,16,1280]{2,1,0:T(8,128)(2,1)}), bf16[8,16,1280]{2,1,0:T(8,128)(2,1)S(1)}, u32[]{:S(2)}, u32[]{:S(2)}) %all-to-all-start.2) | async-done | bytes 327712 | tf_op jit(solution)/shard_map/all_to_all | solution.py:105
  65.0 0.1 fusion.2
  65.1 0.1 broadcast_in_dim.84
  65.2 1.5 %fusion.1 = bf16[4,128,1280]{2,1,0:T(8,128)(2,1)} fusion(s32[]{:T(128)S(6)} %select_n.244, bf16[4,128,1280]{2,1,0:T(8,128)(2,1)S(1)} %broadcast_in_dim.84), kind=kLoop, calls=%fused_computation.8 | loop fusion | flops 655360 | bytes 2621444 | tf_op jit(solution)/shard_map/jit(_roll_dynamic)/concatenate | solution.py:104
  66.8 5.0 %all-to-all-start.3 = ((bf16[4,128,1280]{2,1,0:T(8,128)(2,1)}), bf16[4,128,1280]{2,1,0:T(8,128)(2,1)S(1)}, u32[]{:S(2)}, u32[]{:S(2)}) async-start(bf16[4,128,1280]{2,1,0:T(8,128)(2,1)} %fusion.1), calls=%async_computation.3 | async-start | bytes 2621440 | tf_op jit(solution)/shard_map/all_to_all | solution.py:105
  71.8 0.1 broadcast_add_fusion.1
  71.8 0.1 add_multiply_fusion
  71.9 2.5 %select_reduce_fusion = (s32[4,8,4,4]{1,3,2,0:T(4,128)S(1)}, s32[4,8,4,4]{1,3,2,0:T(4,128)S(1)}) fusion(s32[512]{0:T(512)S(1)} %broadcast_in_dim.74, s32[4,8,4,4]{1,3,2,0:T(4,128)S(1)} %iota_add_fusion, s32[512]{0:T(512)S(1)} %select_reduce_fusion.2), kind=kLoop, calls=%fused_computation.9 | loop fusion | flops 1309696 | bytes 10240 | tf_op jit(solution)/shard_map/reduce_sum | solution.py:127
  74.4 0.2 copy.11
  74.6 0.1 reduce_sum.44
  74.7 0.2 copy.10
  74.9 0.1 reduce_sum.42
  75.1 9.9 %all-to-all-done.3 = bf16[4,128,1280]{2,1,0:T(8,128)(2,1)S(1)} async-done(((bf16[4,128,1280]{2,1,0:T(8,128)(2,1)}), bf16[4,128,1280]{2,1,0:T(8,128)(2,1)S(1)}, u32[]{:S(2)}, u32[]{:S(2)}) %all-to-all-start.3) | async-done | bytes 1310752 | tf_op jit(solution)/shard_map/all_to_all | solution.py:105
  84.9 0.1 rev.11
  85.0 0.5 fusion
  85.5 1.1 %convolution_convert_fusion = bf16[128,1280]{1,0:T(8,128)(2,1)} fusion(bf16[512,1280]{1,0:T(8,128)(2,1)S(1)} %bitcast.9, s32[512]{0:T(512)S(1)} %fusion.17), kind=kOutput, calls=%fused_computation.4 | convolution fusion | flops 168001536 | bytes 1640448 | tf_op jit(solution)/shard_map/dot_general | solution.py:158
  (12 shorter events, 0.2 us)
Async XLA Ops:
  1.4 29.6 %all-to-all-start = ((s32[128,1,8]{2,1,0:T(1,128)}), s32[128,1,8]{2,1,0:T(1,128)S(1)}, u32[]{:S(2)}, u32[]{:S(2)}) async-start(s32[128,1,8]{2,1,0:T(1,128)} %broadcast_in_dim.46), calls=%async_computation | async-start | bytes 131072 | tf_op jit(solution)/shard_map/all_to_all | solution.py:88
  18.5 13.5 %copy-start = (s32[4]{0:T(128)S(1)}, s32[4]{0:T(128)}, u32[]{:S(2)}) copy-start(s32[4]{0:T(128)} %param.18) | copy-start | bytes 52
  34.3 11.3 %all-to-all-start.1 = ((bf16[4,32,1280]{2,1,0:T(8,128)(2,1)}), bf16[4,32,1280]{2,1,0:T(8,128)(2,1)S(1)}, u32[]{:S(2)}, u32[]{:S(2)}) async-start(bf16[4,32,1280]{2,1,0:T(8,128)(2,1)} %fusion.5), calls=%async_computation.1 | async-start | bytes 655360 | tf_op jit(solution)/shard_map/all_to_all | solution.py:105
  46.9 18.1 %all-to-all-start.2 = ((bf16[8,16,1280]{2,1,0:T(8,128)(2,1)}), bf16[8,16,1280]{2,1,0:T(8,128)(2,1)S(1)}, u32[]{:S(2)}, u32[]{:S(2)}) async-start(bf16[8,16,1280]{2,1,0:T(8,128)(2,1)} %fusion.3), calls=%async_computation.2 | async-start | bytes 655360 | tf_op jit(solution)/shard_map/all_to_all | solution.py:105
  66.8 18.2 %all-to-all-start.3 = ((bf16[4,128,1280]{2,1,0:T(8,128)(2,1)}), bf16[4,128,1280]{2,1,0:T(8,128)(2,1)S(1)}, u32[]{:S(2)}, u32[]{:S(2)}) async-start(bf16[4,128,1280]{2,1,0:T(8,128)(2,1)} %fusion.1), calls=%async_computation.3 | async-start | bytes 2621440 | tf_op jit(solution)/shard_map/all_to_all | solution.py:105

commit v8 on v5

--- a/solution.py
+++ b/solution.py
@@ -8,54 +8,66 @@
 H = 16
 
 
-def block_kernel(cache_len_ref, qkv_ref, cache_ref, resid_ref, gain_ref, up_ref, down_ref, out_ref, hid_ref):
+def block_kernel(cache_len_ref, qkv_ref, cache_ref, resid_ref, gain_ref, up_hbm, down_hbm, out_ref,
+                 hid_ref, up_ref, down_ref, sem):
     series_here, span_slots = qkv_ref.shape[0], qkv_ref.shape[1]
     cache_slots = cache_ref.shape[1]
     width = resid_ref.shape[2]
     head_size = width // H
-    col_head = lax.broadcasted_iota(jnp.int32, (H, 1, width), 2) // head_size
-    head_id = lax.broadcasted_iota(jnp.int32, (H, 1, width), 0)
+    up_copy = pltpu.make_async_copy(up_hbm, up_ref, sem.at[0])
+    down_copy = pltpu.make_async_copy(down_hbm, down_ref, sem.at[1])
+    up_copy.start()
+    down_copy.start()
+    group = 8 if H % 8 == 0 and (8 * head_size) % 128 == 0 else H
+    group_w = group * head_size
+    col_head = lax.broadcasted_iota(jnp.int32, (group, 1, group_w), 2) // head_size
+    head_id = lax.broadcasted_iota(jnp.int32, (group, 1, group_w), 0)
     head_mask = col_head == head_id
     dims = (((1,), (1,)), ((), ()))
     scale = head_size ** (-0.5)
-    rows = H * span_slots
+    rows = group * span_slots
     row_t = lax.broadcasted_iota(jnp.int32, (rows, span_slots), 0) % span_slots
     key_new = lax.broadcasted_iota(jnp.int32, (rows, span_slots), 1)
     key_old = lax.broadcasted_iota(jnp.int32, (rows, cache_slots), 1)
     for i in range(series_here):
-        q = qkv_ref[i, :, 0:width]
-        k_new = qkv_ref[i, :, width : 2 * width]
-        v_new = qkv_ref[i, :, 2 * width : 3 * width]
-        k_old = cache_ref[i, :, 0:width]
-        v_old = cache_ref[i, :, width : 2 * width]
-        q_heads = jnp.where(head_mask, q[None], jnp.zeros((), q.dtype)).reshape(rows, width)
-        s_old = lax.dot_general(q_heads, k_old, dims, preferred_element_type=jnp.float32) * scale
-        s_new = lax.dot_general(q_heads, k_new, dims, preferred_element_type=jnp.float32) * scale
-        s_old = jnp.where(key_old < cache_len_ref[i], s_old, -1e30)
-        s_new = jnp.where(key_new <= row_t, s_new, -1e30)
-        top = jnp.maximum(jnp.max(s_old, axis=1, keepdims=True), jnp.max(s_new, axis=1, keepdims=True))
-        e_old = jnp.exp(s_old - top)
-        e_new = jnp.exp(s_new - top)
-        denom = jnp.sum(e_old, axis=1, keepdims=True) + jnp.sum(e_new, axis=1, keepdims=True)
-        w_old = (e_old / denom).astype(jnp.bfloat16)
-        w_new = (e_new / denom).astype(jnp.bfloat16)
-        mixed = jnp.dot(w_old, v_old, preferred_element_type=jnp.float32) + jnp.dot(
-            w_new, v_new, preferred_element_type=jnp.float32
-        )
-        mixed = mixed.reshape(H, span_slots, width)
-        attended = jnp.sum(jnp.where(head_mask, mixed, 0.0), axis=0)
-        hid_ref[i * span_slots : (i + 1) * span_slots, :] = (
-            resid_ref[i].astype(jnp.float32) + attended
-        ).astype(hid_ref.dtype)
+        old_visible = key_old < cache_len_ref[i]
+        for g in range(H // group):
+            lo = g * group_w
+            q = qkv_ref[i, :, lo : lo + group_w]
+            k_new = qkv_ref[i, :, width + lo : width + lo + group_w]
+            v_new = qkv_ref[i, :, 2 * width + lo : 2 * width + lo + group_w]
+            k_old = cache_ref[i, :, lo : lo + group_w]
+            v_old = cache_ref[i, :, width + lo : width + lo + group_w]
+            q_heads = jnp.where(head_mask, q[None], jnp.zeros((), q.dtype)).reshape(rows, group_w)
+            s_old = lax.dot_general(q_heads, k_old, dims, preferred_element_type=jnp.float32) * scale
+            s_new = lax.dot_general(q_heads, k_new, dims, preferred_element_type=jnp.float32) * scale
+            s_old = jnp.where(old_visible, s_old, -1e30)
+            s_new = jnp.where(key_new <= row_t, s_new, -1e30)
+            top = jnp.maximum(jnp.max(s_old, axis=1, keepdims=True), jnp.max(s_new, axis=1, keepdims=True))
+            e_old = jnp.exp(s_old - top)
+            e_new = jnp.exp(s_new - top)
+            denom = jnp.sum(e_old, axis=1, keepdims=True) + jnp.sum(e_new, axis=1, keepdims=True)
+            w_old = (e_old / denom).astype(jnp.bfloat16)
+            w_new = (e_new / denom).astype(jnp.bfloat16)
+            mixed = jnp.dot(w_old, v_old, preferred_element_type=jnp.float32) + jnp.dot(
+                w_new, v_new, preferred_element_type=jnp.float32
+            )
+            mixed = mixed.reshape(group, span_slots, group_w)
+            attended = jnp.sum(jnp.where(head_mask, mixed, 0.0), axis=0)
+            hid_ref[i * span_slots : (i + 1) * span_slots, lo : lo + group_w] = (
+                resid_ref[i, :, lo : lo + group_w].astype(jnp.float32) + attended
+            ).astype(hid_ref.dtype)
     wide_rows = hid_ref[...].astype(jnp.float32)
     normed = (
         wide_rows
         * lax.rsqrt(jnp.mean(wide_rows * wide_rows, axis=-1, keepdims=True) + 1e-06)
         * gain_ref[...]
     ).astype(jnp.bfloat16)
+    up_copy.wait()
     activated = jax.nn.silu(
         jnp.dot(normed, up_ref[...], preferred_element_type=jnp.float32)
     ).astype(jnp.bfloat16)
+    down_copy.wait()
     out_ref[...] = (
         wide_rows + jnp.dot(activated, down_ref[...], preferred_element_type=jnp.float32)
     ).astype(out_ref.dtype)
@@ -66,12 +78,18 @@
     width = resid.shape[2]
     vmem = pltpu.MemorySpace.VMEM if hasattr(pltpu, "MemorySpace") else pltpu.VMEM
     full = pl.BlockSpec(memory_space=vmem)
+    anywhere = pl.BlockSpec(memory_space=pl.ANY)
     return pl.pallas_call(
         block_kernel,
-        in_specs=[pl.BlockSpec(memory_space=pltpu.SMEM)] + [full] * 6,
+        in_specs=[pl.BlockSpec(memory_space=pltpu.SMEM)] + [full] * 4 + [anywhere] * 2,
         out_specs=full,
         out_shape=jax.ShapeDtypeStruct((series_here * span_slots, width), jnp.bfloat16),
-        scratch_shapes=[pltpu.VMEM((series_here * span_slots, width), jnp.bfloat16)],
+        scratch_shapes=[
+            pltpu.VMEM((series_here * span_slots, width), jnp.bfloat16),
+            pltpu.VMEM(w_up.shape, w_up.dtype),
+            pltpu.VMEM(w_down.shape, w_down.dtype),
+            pltpu.SemaphoreType.DMA((2,)),
+        ],
     )(cache_len, new_qkv, cache_kv, resid, ff_gain.reshape(1, width), w_up, w_down)
 
 

time: 86.4 us -> 82.8 us (0.958)
  Pallas kernels: 12.5 us -> 8.92 us
    pallas_call x1, Pallas kernels: 12.5 us -> 8.92 us  [layer_block(): pl.pallas_call(block_kernel, in_specs=[pl.BlockSpec(memory_space=pltpu.SM...]
  transfers between devices with their start and end apart: 2 -> 2, of which waited for: 1 -> 1; matrix products, arithmetic and copies ran while one was open for 3% -> 3% of each run, Pallas kernels for 15% -> 11%
where the time goes in v8:
time: 82.8 us; the launch traced here: 82.5 us
  waiting for transfers between devices  34.4 us (42%)
  starting transfers between devices  29.2 us (35%)
  Pallas kernels  8.92 us (11%)
  local copies, waits for them, and re-layouts  5.16 us (6%)
  matrix products  2.6 us (3%)
  other arithmetic  2.09 us (3%)
    all_to_all x1, waiting for transfers between devices, local(): arrived = lax.all_to_all(placed, 'req', 0, 0, tiled=True)  34.4 us
    all_to_all x1, starting transfers between devices, local(): lax.all_to_all(jnp.broadcast_to(info[None], (group_size, info.shape[0])),...  15.4 us
    all_to_all x1, starting transfers between devices, local(): arrived = lax.all_to_all(placed, 'req', 0, 0, tiled=True)  13.8 us
    pallas_call x1, Pallas kernels, layer_block(): pl.pallas_call(block_kernel, in_specs=[pl.BlockSpec(memory_space=pltpu.SM...  8.92 us
    convert_element_type x1, local copies, waits for them, and re-layouts, local(): placed = lax.dot_general(pick.reshape(group_size, series_here, -1), layer...  2.08 us
  transfers between devices with their start and end apart: 2, of which 1 were waited for; matrix products, arithmetic and copies ran while one was open for 3% of the time, Pallas kernels for 11%

profile of v8, /device:TPU:8, one launch (start us, length us, event | category | flops | bytes accessed | tf_op | source)
XLA Modules:
  0.0 82.5 jit_solution(10478265627526572658)
XLA Ops:
  0.0 0.7 pad_add_fusion
  0.7 0.6 broadcast_in_dim.17
  1.4 15.4 %all-to-all-start = ((s32[128,1,8]{2,1,0:T(1,128)}), s32[128,1,8]{2,1,0:T(1,128)S(1)}, u32[]{:S(2)}, u32[]{:S(2)}) async-start(s32[128,1,8]{2,1,0:T(1,128)} %broadcast_in_dim.17), calls=%async_computation | async-start | bytes 131072 | tf_op jit(solution)/shard_map/all_to_all | solution.py:103
  16.8 0.7 iota_compare_fusion.4
  17.6 0.1 and.66
  17.7 0.1 and.67
  17.8 1.3 %reshape.105.gain_ref = f32[1,1280]{1,0:T(1,128)} reshape(f32[1280]{0:T(1024)} %param.15) | data formatting | bytes 10240 | tf_op jit(solution)/shard_map/reshape | solution.py:93
  19.1 8.9 %shard_map.91 = bf16[128,1280]{1,0:T(8,128)(2,1)} custom-call(s32[4]{0:T(128)} %cache_len_ref.1, bf16[4,32,3840]{2,1,0:T(8,128)(2,1)} %qkv_ref.1, bf16[4,32,2560]{2,1,0:T(8,128)(2,1)} %cache_ref.1, bf16[4,32,1280]{2,1,0:T(8,128)(2,1)} %resid_ref.1, f32[1,1280]{1,0:T(1,128)} %reshape.105.gain_ref, bf16[1280,1280]{1,0:T(8,128)(2,1)} %up_hbm.1, ...), custom_call_target="tpu_custom_call" | custom-call | tf_op jit(solution)/shard_map/pallas_call | solution.py:82
  28.0 0.0 all-to-all-done
  28.0 0.1 fusion.12
  28.1 0.1 lt.51
  28.2 0.1 broadcast_in_dim.18
  28.3 0.3 select_reduce_fusion
  28.6 0.1 dynamic_slice.3
  28.7 0.1 copy.16
  28.7 0.1 fusion.10
  28.9 0.1 bitcast_and_fusion
  29.0 1.5 %convolution_convert_fusion = bf16[128,4,1280]{2,0,1:T(8,128)(2,1)S(1)} fusion(pred[128,4,128]{0,2,1:T(32,128)(4,1)S(1)} %bitcast_and_fusion, bf16[128,1280]{1,0:T(8,128)(2,1)} %shard_map.91), kind=kOutput, calls=%fused_computation | convolution fusion | flops 168427520 | bytes 1703936 | tf_op jit(solution)/shard_map/dot_general | solution.py:129
  30.5 2.1 %copy.18 = bf16[128,4,1280]{2,1,0:T(4,128)(2,1)} copy(bf16[128,4,1280]{2,0,1:T(8,128)(2,1)S(1)} %convolution_convert_fusion) | data formatting | bytes 2621440 | tf_op jit(solution)/shard_map/convert_element_type | solution.py:134
  32.6 13.8 %all-to-all-start.1 = ((bf16[128,4,1280]{2,1,0:T(4,128)(2,1)}), bf16[128,4,1280]{2,1,0:T(4,128)(2,1)S(1)}, u32[]{:S(2)}, u32[]{:S(2)}) async-start(bf16[128,4,1280]{2,1,0:T(4,128)(2,1)} %copy.18), calls=%async_computation.1 | async-start | bytes 2621440 | tf_op jit(solution)/shard_map/all_to_all | solution.py:135
  46.4 0.1 reshape.104
  46.5 0.1 fusion.4
  46.6 0.1 eq.54
  46.7 34.4 %all-to-all-done.1 = bf16[128,4,1280]{2,1,0:T(4,128)(2,1)S(1)} async-done(((bf16[128,4,1280]{2,1,0:T(4,128)(2,1)}), bf16[128,4,1280]{2,1,0:T(4,128)(2,1)S(1)}, u32[]{:S(2)}, u32[]{:S(2)}) %all-to-all-start.1) | async-done | bytes 1310752 | tf_op jit(solution)/shard_map/all_to_all | solution.py:135
  81.1 0.3 reshape.106
  81.4 1.1 %convolution_convert_fusion.1 = bf16[128,1280]{1,0:T(8,128)(2,1)} fusion(bf16[512,1280]{1,0:T(8,128)(2,1)S(1)} %reshape.106, s32[512]{0:T(512)S(1)} %eq.54), kind=kOutput, calls=%fused_computation.1 | convolution fusion | flops 168001536 | bytes 1640448 | tf_op jit(solution)/shard_map/dot_general | solution.py:137
  (2 shorter events, 0.0 us)
Async XLA Ops:
  1.4 26.6 %all-to-all-start = ((s32[128,1,8]{2,1,0:T(1,128)}), s32[128,1,8]{2,1,0:T(1,128)S(1)}, u32[]{:S(2)}, u32[]{:S(2)}) async-start(s32[128,1,8]{2,1,0:T(1,128)} %broadcast_in_dim.17), calls=%async_computation | async-start | bytes 131072 | tf_op jit(solution)/shard_map/all_to_all | solution.py:103
  32.6 48.5 %all-to-all-start.1 = ((bf16[128,4,1280]{2,1,0:T(4,128)(2,1)}), bf16[128,4,1280]{2,1,0:T(4,128)(2,1)S(1)}, u32[]{:S(2)}, u32[]{:S(2)}) async-start(bf16[128,4,1280]{2,1,0:T(4,128)(2,1)} %copy.18), calls=%async_computation.1 | async-start | bytes 2621440 | tf_op jit(solution)/shard_map/all_to_all | solution.py:135

commit v9 on v8

--- a/solution.py
+++ b/solution.py
@@ -61,7 +61,7 @@
     normed = (
         wide_rows
         * lax.rsqrt(jnp.mean(wide_rows * wide_rows, axis=-1, keepdims=True) + 1e-06)
-        * gain_ref[...]
+        * gain_ref[...].reshape(1, width)
     ).astype(jnp.bfloat16)
     up_copy.wait()
     activated = jax.nn.silu(
@@ -90,7 +90,7 @@
             pltpu.VMEM(w_down.shape, w_down.dtype),
             pltpu.SemaphoreType.DMA((2,)),
         ],
-    )(cache_len, new_qkv, cache_kv, resid, ff_gain.reshape(1, width), w_up, w_down)
+    )(cache_len, new_qkv, cache_kv, resid, ff_gain, w_up, w_down)
 
 
 def local(new_qkv, cache_kv, resid, span_len, cache_len, series_perm, ff_gain, w_up, w_down):
@@ -99,10 +99,11 @@
     series_here, span_slots, triple = new_qkv.shape
     width = resid.shape[2]
     layer_out = layer_block(new_qkv, cache_kv, resid, cache_len, ff_gain, w_up, w_down)
-    info = jnp.concatenate([span_len, series_perm])
-    gathered = lax.all_to_all(
-        jnp.broadcast_to(info[None], (group_size, info.shape[0])), "req", 0, 0, tiled=True
+    info = jnp.concatenate(
+        [jnp.broadcast_to(span_len[None], (group_size, series_here)),
+         jnp.broadcast_to(series_perm[None], (group_size, series_here))], axis=1
     )
+    gathered = lax.all_to_all(info, "req", 0, 0, tiled=True)
     all_len = gathered[:, :series_here].reshape(-1)
     all_perm = gathered[:, series_here:].reshape(-1)
     series_total = all_len.shape[0]
@@ -115,26 +116,39 @@
     slot = jnp.arange(span_slots, dtype=jnp.int32)[None, None, :]
     my_offset = (target - my_start[:, None, None]) % group_size
     pick = (my_offset == slot) & (slot < span_len[:, None, None])
+    half = width // 2
     same = jnp.arange(series_here)[:, None] == jnp.arange(series_here)[None, :]
     pick = pick.transpose(1, 0, 2)[:, :, None, :] & same[None, :, :, None]
-    pick = pick.reshape(group_size * series_here, series_here * span_slots).astype(jnp.bfloat16)
+    pick = pick.reshape(group_size, series_here, 1, series_here * span_slots)
+    halves = jnp.arange(2)[None, None, :, None]
+    rows_here = series_here * span_slots
+    placed = 0
+    for h in range(2):
+        pick_h = (pick & (halves == h)).reshape(-1, rows_here).astype(jnp.bfloat16)
+        placed = placed + jnp.dot(
+            pick_h, layer_out[:, h * half : (h + 1) * half], preferred_element_type=jnp.float32
+        )
+    placed = placed.astype(jnp.bfloat16)
+    arrived = lax.all_to_all(placed, "req", 0, 0, tiled=True)
 
     src_start = all_start.reshape(group_size, series_here)
     src_len = all_len.reshape(group_size, series_here)
     src_t = (me - src_start) % group_size
     src_row = (src_start + src_t) // group_size
     src_row = jnp.where(src_t < src_len, src_row, -1)
-    rows_here = series_here * span_slots
-    out_row = jnp.arange(rows_here, dtype=jnp.int32)[:, None]
-    placed = lax.dot_general(
-        pick.reshape(group_size, series_here, -1),
-        layer_out,
-        (((2,), (0,)), ((), ())),
-        preferred_element_type=jnp.float32,
-    ).astype(jnp.bfloat16)
-    arrived = lax.all_to_all(placed, "req", 0, 0, tiled=True)
-    gather = (src_row.reshape(1, -1) == out_row).astype(jnp.bfloat16)
-    result = jnp.dot(gather, arrived.reshape(-1, width), preferred_element_type=jnp.float32)
+    out_row = jnp.arange(rows_here, dtype=jnp.int32)[:, None, None, None]
+    hit = src_row[None, :, :, None] == out_row
+    result = jnp.concatenate(
+        [
+            jnp.dot(
+                (hit & (halves.reshape(1, 1, 1, 2) == h)).reshape(rows_here, -1).astype(jnp.bfloat16),
+                arrived,
+                preferred_element_type=jnp.float32,
+            )
+            for h in range(2)
+        ],
+        axis=1,
+    )
     return result.astype(jnp.bfloat16)
 
 

time: 82.8 us -> 81.4 us (0.983)
  local copies, waits for them, and re-layouts: 5.16 us -> 3.14 us
  other arithmetic: 2.09 us -> 3.65 us
    convert_element_type x1 -> x0, local copies, waits for them, and re-layouts: 2.08 us -> none  [local(): placed = lax.dot_general(pick.reshape(group_size, series_here, -1), layer...]
    and x0 -> x8, local copies, waits for them, and re-layouts: none -> 1.65 us  [the longest x6 1.02 us: local(): pick_h = (pick & (halves == h)).reshape(-1, rows_here).astype(jnp.bfloat16)]
    reshape x2 -> x0, local copies, waits for them, and re-layouts: 1.63 us -> none  [the longest x1 1.3 us: layer_block(): ff_gain.reshape(1, width)]
    all_to_all x1, waiting for transfers between devices: 34.4 us -> 33 us  [local(): arrived = lax.all_to_all(placed, 'req', 0, 0, tiled=True)]
    dot_general x2 -> x4, matrix products: 2.6 us -> 3.04 us  [the longest x2 2.19 us: local(): jnp.dot(pick_h, layer_out[:, h * half:(h + 1) * half], preferred_element_...]
  transfers between devices with their start and end apart: 2 -> 2, of which waited for: 1 -> 2; matrix products, arithmetic and copies ran while one was open for 3% -> 4% of each run, Pallas kernels for 11% -> 11%
where the time goes in v9:
time: 81.4 us; the launch traced here: 81.2 us
  waiting for transfers between devices  33.6 us (41%)
  starting transfers between devices  28.6 us (35%)
  Pallas kernels  8.93 us (11%)
  other arithmetic  3.65 us (4%)
  local copies, waits for them, and re-layouts  3.14 us (4%)
  matrix products  3.04 us (4%)
    all_to_all x1, waiting for transfers between devices, local(): arrived = lax.all_to_all(placed, 'req', 0, 0, tiled=True)  33 us
    all_to_all x1, starting transfers between devices, local(): gathered = lax.all_to_all(info, 'req', 0, 0, tiled=True)  15.4 us
    all_to_all x1, starting transfers between devices, local(): arrived = lax.all_to_all(placed, 'req', 0, 0, tiled=True)  13.2 us
    pallas_call x1, Pallas kernels, layer_block(): pl.pallas_call(block_kernel, in_specs=[pl.BlockSpec(memory_space=pltpu.SM...  8.93 us
    dot_general x2, matrix products, local(): jnp.dot(pick_h, layer_out[:, h * half:(h + 1) * half], preferred_element_...  2.19 us
  transfers between devices with their start and end apart: 2, of which 2 were waited for; matrix products, arithmetic and copies ran while one was open for 4% of the time, Pallas kernels for 11%

profile of v9, /device:TPU:8, one launch (start us, length us, event | category | flops | bytes accessed | tf_op | source)
XLA Modules:
  0.0 81.2 jit_solution(5077228798092502774)
XLA Ops:
  0.0 0.7 pad_add_fusion
  0.7 0.6 broadcast.204.clone
  1.4 15.4 %all-to-all-start = ((s32[128,1,8]{2,1,0:T(1,128)}), s32[128,1,8]{2,1,0:T(1,128)S(1)}, u32[]{:S(2)}, u32[]{:S(2)}) async-start(s32[128,1,8]{2,1,0:T(1,128)} %bitcast), calls=%async_computation | async-start | bytes 131072 | tf_op jit(solution)/shard_map/all_to_all | solution.py:106
  16.8 0.7 iota_compare_fusion.3
  17.6 0.1 and.153
  17.6 0.1 and.154
  17.8 0.2 and.160
  18.0 0.2 and.164
  18.2 8.9 %shard_map.91 = bf16[128,1280]{1,0:T(8,128)(2,1)} custom-call(s32[4]{0:T(128)} %cache_len_ref.1, bf16[4,32,3840]{2,1,0:T(8,128)(2,1)} %qkv_ref.1, bf16[4,32,2560]{2,1,0:T(8,128)(2,1)} %cache_ref.1, bf16[4,32,1280]{2,1,0:T(8,128)(2,1)} %resid_ref.1, f32[1280]{0:T(1024)} %gain_ref.1, bf16[1280,1280]{1,0:T(8,128)(2,1)} %up_hbm.1, bf16[1280,1280]{1,0:T(8,128)(2,1)} %down_hbm.1), custom_call_target="tpu_custom_call" | custom-call | tf_op jit(solution)/shard_map/pallas_call | solution.py:82
  27.1 0.0 copy-start
  27.1 0.6 all-to-all-done
  27.8 0.1 fusion.28
  27.8 0.1 broadcast_in_dim.21
  27.9 0.1 lt.51
  28.1 0.3 select_reduce_fusion
  28.3 0.1 dynamic_slice.3
  28.4 0.1 copy.16
  28.5 0.1 fusion.26
  28.6 0.1 bitcast_and_fusion
  28.7 0.2 copy.17
  28.9 0.3 and.157
  29.2 0.3 and.158
  29.5 0.0 copy-done
  29.5 0.6 fusion.12
  30.1 1.6 %fusion = bf16[128,8,640]{2,1,0:T(8,128)(2,1)} fusion(f32[1024,640]{1,0:T(8,128)S(1)} %fusion.12, pred[1024,128]{1,0:T(32,128)(4,1)S(1)} %and.158, pred[1024]{0:T(1024)(128)(4,1)S(1)} %and.164, bf16[128,1280]{1,0:T(8,128)(2,1)S(1)} %copy-done), kind=kOutput, calls=%fused_computation.1 | convolution fusion | flops 169213952 | bytes 4228096 | tf_op jit(solution)/shard_map/dot_general | solution.py:128
  31.7 13.2 %all-to-all-start.1 = ((bf16[128,8,640]{2,1,0:T(8,128)(2,1)}), bf16[128,8,640]{2,1,0:T(8,128)(2,1)S(1)}, u32[]{:S(2)}, u32[]{:S(2)}) async-start(bf16[128,8,640]{2,1,0:T(8,128)(2,1)} %fusion), calls=%async_computation.1 | async-start | bytes 2621440 | tf_op jit(solution)/shard_map/all_to_all | solution.py:132
  44.9 0.1 reshape.200
  45.0 0.1 fusion.20
  45.1 0.2 iota_compare_fusion
  45.3 0.6 broadcast_and_fusion.1
  45.9 0.3 and.147
  46.2 0.3 and.169
  46.5 33.0 %all-to-all-done.1 = bf16[128,8,640]{2,1,0:T(8,128)(2,1)S(1)} async-done(((bf16[128,8,640]{2,1,0:T(8,128)(2,1)}), bf16[128,8,640]{2,1,0:T(8,128)(2,1)S(1)}, u32[]{:S(2)}, u32[]{:S(2)}) %all-to-all-start.1) | async-done | bytes 1310752 | tf_op jit(solution)/shard_map/all_to_all | solution.py:132
  79.6 0.4 fusion.5
  80.0 0.4 fusion.8
  80.4 0.8 pad_maximum_fusion
  (5 shorter events, 0.1 us)
Async XLA Ops:
  1.4 26.4 %all-to-all-start = ((s32[128,1,8]{2,1,0:T(1,128)}), s32[128,1,8]{2,1,0:T(1,128)S(1)}, u32[]{:S(2)}, u32[]{:S(2)}) async-start(s32[128,1,8]{2,1,0:T(1,128)} %bitcast), calls=%async_computation | async-start | bytes 131072 | tf_op jit(solution)/shard_map/all_to_all | solution.py:106
  27.1 2.4 %copy-start = (bf16[128,1280]{1,0:T(8,128)(2,1)S(1)}, bf16[128,1280]{1,0:T(8,128)(2,1)}, u32[]{:S(2)}) copy-start(bf16[128,1280]{1,0:T(8,128)(2,1)} %shard_map.91) | copy-start | bytes 983044
  31.7 47.8 %all-to-all-start.1 = ((bf16[128,8,640]{2,1,0:T(8,128)(2,1)}), bf16[128,8,640]{2,1,0:T(8,128)(2,1)S(1)}, u32[]{:S(2)}, u32[]{:S(2)}) async-start(bf16[128,8,640]{2,1,0:T(8,128)(2,1)} %fusion), calls=%async_computation.1 | async-start | bytes 2621440 | tf_op jit(solution)/shard_map/all_to_all | solution.py:132

commit v10 on v9

--- a/solution.py
+++ b/solution.py
@@ -93,42 +93,66 @@
     )(cache_len, new_qkv, cache_kv, resid, ff_gain, w_up, w_down)
 
 
+def send_kernel(start_ref, len_ref, rows_ref, out_ref):
+    rows, cols = out_ref.shape[0], rows_ref.shape[0]
+    series_here = start_ref.shape[0]
+    span_slots = cols // series_here
+    half = out_ref.shape[1]
+    targets = rows // (2 * series_here)
+    r = lax.broadcasted_iota(jnp.int32, (rows, cols), 0)
+    c = lax.broadcasted_iota(jnp.int32, (rows, cols), 1)
+    d = r // (2 * series_here)
+    i = (r // 2) % series_here
+    h = r % 2
+    start_i = jnp.zeros((rows, cols), jnp.int32)
+    len_i = jnp.zeros((rows, cols), jnp.int32)
+    for k in range(series_here):
+        start_i = jnp.where(i == k, start_ref[k], start_i)
+        len_i = jnp.where(i == k, len_ref[k], len_i)
+    t = c % span_slots
+    hit = (c // span_slots == i) & (t == (d - start_i) % targets) & (t < len_i)
+    acc = jnp.zeros((rows, half), jnp.float32)
+    for k in range(2):
+        pick = jnp.where(hit & (h == k), 1.0, 0.0).astype(jnp.bfloat16)
+        acc = acc + jnp.dot(pick, rows_ref[:, k * half : (k + 1) * half], preferred_element_type=jnp.float32)
+    out_ref[...] = acc.astype(out_ref.dtype)
+
+
+def send_block(my_start, span_len, layer_out, targets):
+    series_here = my_start.shape[0]
+    width = layer_out.shape[1]
+    smem = pl.BlockSpec(memory_space=pltpu.SMEM)
+    vmem = pltpu.MemorySpace.VMEM if hasattr(pltpu, "MemorySpace") else pltpu.VMEM
+    full = pl.BlockSpec(memory_space=vmem)
+    return pl.pallas_call(
+        send_kernel,
+        in_specs=[smem, smem, full],
+        out_specs=full,
+        out_shape=jax.ShapeDtypeStruct((targets * series_here * 2, width // 2), layer_out.dtype),
+    )(my_start, span_len, layer_out)
+
+
 def local(new_qkv, cache_kv, resid, span_len, cache_len, series_perm, ff_gain, w_up, w_down):
     group_size = lax.axis_size("req")
     me = lax.axis_index("req")
     series_here, span_slots, triple = new_qkv.shape
     width = resid.shape[2]
     layer_out = layer_block(new_qkv, cache_kv, resid, cache_len, ff_gain, w_up, w_down)
-    info = jnp.concatenate(
-        [jnp.broadcast_to(span_len[None], (group_size, series_here)),
-         jnp.broadcast_to(series_perm[None], (group_size, series_here))], axis=1
-    )
-    gathered = lax.all_to_all(info, "req", 0, 0, tiled=True)
-    all_len = gathered[:, :series_here].reshape(-1)
-    all_perm = gathered[:, series_here:].reshape(-1)
+    pack = 2 * span_slots
+    info = jnp.broadcast_to((series_perm * pack + span_len)[None], (group_size, series_here))
+    gathered = lax.all_to_all(info, "req", 0, 0, tiled=True).reshape(-1)
+    all_len = gathered % pack
+    all_perm = gathered // pack
     series_total = all_len.shape[0]
     earlier = all_perm[None, :] < all_perm[:, None]
     all_start = jnp.sum(jnp.where(earlier, all_len[None, :], 0), axis=1)
 
 
     my_start = lax.dynamic_slice(all_start, (me * series_here,), (series_here,))
-    target = jnp.arange(group_size, dtype=jnp.int32)[None, :, None]
-    slot = jnp.arange(span_slots, dtype=jnp.int32)[None, None, :]
-    my_offset = (target - my_start[:, None, None]) % group_size
-    pick = (my_offset == slot) & (slot < span_len[:, None, None])
+    rows_here = series_here * span_slots
     half = width // 2
-    same = jnp.arange(series_here)[:, None] == jnp.arange(series_here)[None, :]
-    pick = pick.transpose(1, 0, 2)[:, :, None, :] & same[None, :, :, None]
-    pick = pick.reshape(group_size, series_here, 1, series_here * span_slots)
     halves = jnp.arange(2)[None, None, :, None]
-    rows_here = series_here * span_slots
-    placed = 0
-    for h in range(2):
-        pick_h = (pick & (halves == h)).reshape(-1, rows_here).astype(jnp.bfloat16)
-        placed = placed + jnp.dot(
-            pick_h, layer_out[:, h * half : (h + 1) * half], preferred_element_type=jnp.float32
-        )
-    placed = placed.astype(jnp.bfloat16)
+    placed = send_block(my_start, span_len, layer_out, group_size)
     arrived = lax.all_to_all(placed, "req", 0, 0, tiled=True)
 
     src_start = all_start.reshape(group_size, series_here)

time: 81.4 us -> 81.8 us (level)
  Pallas kernels: 8.93 us -> 12.3 us
  matrix products: 3.04 us -> 0.84 us
  starting transfers between devices: 28.6 us -> 27.3 us
  waiting for transfers between devices: 33.6 us -> 34.9 us
    pallas_call x0 -> x1, Pallas kernels: none -> 3.39 us  [send_block(): pl.pallas_call(send_kernel, in_specs=[smem, smem, full], out_specs=full,...]
    dot_general x2 -> x0, matrix products: 2.19 us -> none  [local(): jnp.dot(pick_h, layer_out[:, h * half:(h + 1) * half], preferred_element_...]
    all_to_all x1, waiting for transfers between devices: 0.61 us -> 1.96 us  [local(): gathered = lax.all_to_all(info, 'req', 0, 0, tiled=True).reshape(-1)]
    and x9 -> x0, local copies, waits for them, and re-layouts: 1.35 us -> none  [the longest x6 1.02 us: local(): pick_h = (pick & (halves == h)).reshape(-1, rows_here).astype(jnp.bfloat16)]
    all_to_all x1, starting transfers between devices: 13.2 us -> 11.9 us  [local(): arrived = lax.all_to_all(placed, 'req', 0, 0, tiled=True)]
  transfers between devices with their start and end apart: 2 -> 2, of which waited for: 2 -> 2; matrix products, arithmetic and copies ran while one was open for 4% -> 2% of each run, Pallas kernels for 11% -> 11%
where the time goes in v10:
time: 81.8 us; the launch traced here: 81.5 us
  waiting for transfers between devices  34.9 us (43%)
  starting transfers between devices  27.3 us (33%)
  Pallas kernels  12.3 us (15%)
  other arithmetic  3.39 us (4%)
  local copies, waits for them, and re-layouts  2.67 us (3%)
  matrix products  0.84 us (1%)
    all_to_all x1, waiting for transfers between devices, local(): arrived = lax.all_to_all(placed, 'req', 0, 0, tiled=True)  33 us
    all_to_all x1, starting transfers between devices, local(): gathered = lax.all_to_all(info, 'req', 0, 0, tiled=True).reshape(-1)  15.4 us
    all_to_all x1, starting transfers between devices, local(): arrived = lax.all_to_all(placed, 'req', 0, 0, tiled=True)  11.9 us
    pallas_call x1, Pallas kernels, layer_block(): pl.pallas_call(block_kernel, in_specs=[pl.BlockSpec(memory_space=pltpu.SM...  8.92 us
    pallas_call x1, Pallas kernels, send_block(): pl.pallas_call(send_kernel, in_specs=[smem, smem, full], out_specs=full,...  3.39 us
    all_to_all x1, waiting for transfers between devices, local(): gathered = lax.all_to_all(info, 'req', 0, 0, tiled=True).reshape(-1)  1.96 us
  transfers between devices with their start and end apart: 2, of which 2 were waited for; matrix products, arithmetic and copies ran while one was open for 2% of the time, Pallas kernels for 11%

profile of v10, /device:TPU:8, one launch (start us, length us, event | category | flops | bytes accessed | tf_op | source)
XLA Modules:
  0.0 81.5 jit_solution(6257435388897421827)
XLA Ops:
  0.0 0.7 multiply_add_fusion
  0.7 0.6 broadcast_in_dim.15
  1.3 15.4 %all-to-all-start = ((s32[128,1,4]{2,1,0:T(1,128)}), s32[128,1,4]{2,1,0:T(1,128)S(1)}, u32[]{:S(2)}, u32[]{:S(2)}) async-start(s32[128,1,4]{2,1,0:T(1,128)} %broadcast_in_dim.15), calls=%async_computation | async-start | bytes 131072 | tf_op jit(solution)/shard_map/all_to_all | solution.py:143
  16.8 8.9 %shard_map.91.rows_ref = bf16[128,1280]{1,0:T(8,128)(2,1)} custom-call(s32[4]{0:T(128)} %cache_len_ref.1, bf16[4,32,3840]{2,1,0:T(8,128)(2,1)} %qkv_ref.1, bf16[4,32,2560]{2,1,0:T(8,128)(2,1)} %cache_ref.1, bf16[4,32,1280]{2,1,0:T(8,128)(2,1)} %resid_ref.1, f32[1280]{0:T(1024)} %gain_ref.1, bf16[1280,1280]{1,0:T(8,128)(2,1)} %up_hbm.1, ...), custom_call_target="tpu_custom_call" | custom-call | tf_op jit(solution)/shard_map/pallas_call | solution.py:82
  25.7 2.0 %all-to-all-done = s32[128,1,4]{2,1,0:T(1,128)S(1)} async-done(((s32[128,1,4]{2,1,0:T(1,128)}), s32[128,1,4]{2,1,0:T(1,128)S(1)}, u32[]{:S(2)}, u32[]{:S(2)}) %all-to-all-start) | async-done | bytes 2080 | tf_op jit(solution)/shard_map/all_to_all | solution.py:143
  27.7 0.5 broadcast.287
  28.2 0.8 reduce.3
  29.0 0.1 reshape.236
  29.1 0.3 select_reduce_fusion
  29.4 0.7 dynamic_slice.3.start_ref
  30.0 3.4 %shard_map.92 = bf16[1024,640]{1,0:T(8,128)(2,1)} custom-call(s32[4]{0:T(128)} %dynamic_slice.3.start_ref, s32[4]{0:T(128)} %len_ref.1, bf16[128,1280]{1,0:T(8,128)(2,1)} %shard_map.91.rows_ref), custom_call_target="tpu_custom_call" | custom-call | tf_op jit(solution)/shard_map/pallas_call | solution.py:127
  33.4 11.9 %all-to-all-start.1 = ((bf16[128,8,640]{2,1,0:T(8,128)(2,1)}), bf16[128,8,640]{2,1,0:T(8,128)(2,1)S(1)}, u32[]{:S(2)}, u32[]{:S(2)}) async-start(bf16[128,8,640]{2,1,0:T(8,128)(2,1)} %bitcast.17), calls=%async_computation.1 | async-start | bytes 2621440 | tf_op jit(solution)/shard_map/all_to_all | solution.py:156
  45.3 0.1 reshape.237
  45.4 0.1 fusion.14
  45.5 0.2 iota_compare_fusion
  45.7 0.6 broadcast_and_fusion.1
  46.3 0.3 and.122
  46.7 0.3 and.125
  47.0 33.0 %all-to-all-done.1 = bf16[128,8,640]{2,1,0:T(8,128)(2,1)S(1)} async-done(((bf16[128,8,640]{2,1,0:T(8,128)(2,1)}), bf16[128,8,640]{2,1,0:T(8,128)(2,1)S(1)}, u32[]{:S(2)}, u32[]{:S(2)}) %all-to-all-start.1) | async-done | bytes 1310752 | tf_op jit(solution)/shard_map/all_to_all | solution.py:156
  79.9 0.4 fusion.4
  80.4 0.4 fusion.7
  80.8 0.8 pad_maximum_fusion
  (2 shorter events, 0.0 us)
Async XLA Ops:
  1.3 26.3 %all-to-all-start = ((s32[128,1,4]{2,1,0:T(1,128)}), s32[128,1,4]{2,1,0:T(1,128)S(1)}, u32[]{:S(2)}, u32[]{:S(2)}) async-start(s32[128,1,4]{2,1,0:T(1,128)} %broadcast_in_dim.15), calls=%async_computation | async-start | bytes 131072 | tf_op jit(solution)/shard_map/all_to_all | solution.py:143
  33.4 46.5 %all-to-all-start.1 = ((bf16[128,8,640]{2,1,0:T(8,128)(2,1)}), bf16[128,8,640]{2,1,0:T(8,128)(2,1)S(1)}, u32[]{:S(2)}, u32[]{:S(2)}) async-start(bf16[128,8,640]{2,1,0:T(8,128)(2,1)} %bitcast.17), calls=%async_computation.1 | async-start | bytes 2621440 | tf_op jit(solution)/shard_map/all_to_all | solution.py:156

commit v11 on v9

--- a/solution.py
+++ b/solution.py
@@ -99,13 +99,19 @@
     series_here, span_slots, triple = new_qkv.shape
     width = resid.shape[2]
     layer_out = layer_block(new_qkv, cache_kv, resid, cache_len, ff_gain, w_up, w_down)
-    info = jnp.concatenate(
-        [jnp.broadcast_to(span_len[None], (group_size, series_here)),
-         jnp.broadcast_to(series_perm[None], (group_size, series_here))], axis=1
+    pack = 2 * span_slots
+    everyone = ("grp", "req")
+    code = (series_perm * pack + span_len).astype(jnp.float32)
+    lanes = 128
+    own_row = jnp.zeros((lax.axis_size(everyone), lanes), jnp.float32)
+    own_row = lax.dynamic_update_slice(
+        own_row, jnp.pad(code, (0, lanes - series_here))[None], (lax.axis_index(everyone), 0)
     )
-    gathered = lax.all_to_all(info, "req", 0, 0, tiled=True)
-    all_len = gathered[:, :series_here].reshape(-1)
-    all_perm = gathered[:, series_here:].reshape(-1)
+    summed = lax.psum(own_row, everyone)
+    summed = lax.dynamic_slice_in_dim(summed, lax.axis_index("grp") * group_size, group_size, 0)
+    gathered = summed[:, :series_here].astype(jnp.int32).reshape(-1)
+    all_len = gathered % pack
+    all_perm = gathered // pack
     series_total = all_len.shape[0]
     earlier = all_perm[None, :] < all_perm[:, None]
     all_start = jnp.sum(jnp.where(earlier, all_len[None, :], 0), axis=1)

time: 81.4 us -> 320 us (3.93)
  waiting for transfers between devices: 33.6 us -> 277 us
  starting transfers between devices: 28.6 us -> 8.99 us
  between operations: 0.16 us -> 13.6 us
    psum x0 -> x1, waiting for transfers between devices: none -> 243 us  [local(): summed = lax.psum(own_row, everyone)]
    all_to_all x1 -> x0, starting transfers between devices: 15.4 us -> none  [local(): gathered = lax.all_to_all(info, 'req', 0, 0, tiled=True)]
    all_to_all x1, starting transfers between devices: 13.2 us -> 8.99 us  [local(): arrived = lax.all_to_all(placed, 'req', 0, 0, tiled=True)]
  transfers between devices with their start and end apart: 2 -> 2, of which waited for: 2 -> 2; matrix products, arithmetic and copies ran while one was open for 4% -> 1% of each run, Pallas kernels for 11% -> 3%
where the time goes in v11:
time: 320 us; the launch traced here: 319 us
  waiting for transfers between devices  277 us (87%)
  between operations  13.6 us (4%)
  starting transfers between devices  8.99 us (3%)
  Pallas kernels  8.92 us (3%)
  other arithmetic  4.47 us (1%)
    psum x1, waiting for transfers between devices, local(): summed = lax.psum(own_row, everyone)  243 us
    all_to_all x1, waiting for transfers between devices, local(): arrived = lax.all_to_all(placed, 'req', 0, 0, tiled=True)  33.8 us
    all_to_all x1, starting transfers between devices, local(): arrived = lax.all_to_all(placed, 'req', 0, 0, tiled=True)  8.99 us
    pallas_call x1, Pallas kernels, layer_block(): pl.pallas_call(block_kernel, in_specs=[pl.BlockSpec(memory_space=pltpu.SM...  8.92 us
  transfers between devices with their start and end apart: 2, of which 2 were waited for; matrix products, arithmetic and copies ran while one was open for 1% of the time, Pallas kernels for 3%

profile of v11, /device:TPU:8, one launch (start us, length us, event | category | flops | bytes accessed | tf_op | source)
XLA Modules:
  0.0 319.0 jit_solution(13953137054333318619)
XLA Ops:
  6.5 0.0 all-reduce.3.cloned.1.call-start
  6.5 0.7 add_convert_fusion.1
  7.3 0.0 copy-start.1
  7.3 0.6 copy-done.1
  7.9 0.0 all-reduce.3.cloned.1.call-update
  7.9 0.7 iota_compare_fusion.3
  8.7 0.1 and.194
  8.8 0.1 and.195
  8.9 0.2 and.201
  9.1 0.2 and.205
  9.3 8.9 %shard_map.91 = bf16[128,1280]{1,0:T(8,128)(2,1)} custom-call(s32[4]{0:T(128)} %cache_len_ref.1, bf16[4,32,3840]{2,1,0:T(8,128)(2,1)} %qkv_ref.1, bf16[4,32,2560]{2,1,0:T(8,128)(2,1)} %cache_ref.1, bf16[4,32,1280]{2,1,0:T(8,128)(2,1)} %resid_ref.1, f32[1280]{0:T(1024)} %gain_ref.1, bf16[1280,1280]{1,0:T(8,128)(2,1)} %up_hbm.1, bf16[1280,1280]{1,0:T(8,128)(2,1)} %down_hbm.1), custom_call_target="tpu_custom_call" | custom-call | tf_op jit(solution)/shard_map/pallas_call | solution.py:82
  18.2 0.0 copy-start
  18.3 243.2 %all-reduce.3.cloned.1.call-done = f32[256,128]{1,0:T(8,128)} async-done(((f32[256,128]{1,0:T(8,128)}), f32[256,128]{1,0:T(8,128)}) %all-reduce.3.cloned.1.call-update) | async-done | bytes 131088 | tf_op jit(solution)/shard_map/psum | solution.py:110
  261.5 0.8 dynamic-slice_convert_fusion
  262.3 0.1 reshape.274
  262.5 0.3 select_reduce_fusion
  262.7 0.1 dynamic_slice.7
  262.8 0.1 copy.12
  262.9 0.1 fusion.28
  263.0 0.1 bitcast_and_fusion
  263.2 0.2 copy.13
  263.3 0.3 and.198
  263.6 0.3 and.199
  263.9 0.0 copy-done
  263.9 0.6 fusion.12
  264.5 1.6 fusion
  266.1 0.0 copy-start.2
  266.1 9.0 %all-to-all-start = ((bf16[128,8,640]{2,1,0:T(8,128)(2,1)}), bf16[128,8,640]{2,1,0:T(8,128)(2,1)S(1)}, u32[]{:S(2)}, u32[]{:S(2)}) async-start(bf16[128,8,640]{2,1,0:T(8,128)(2,1)} %fusion), calls=%async_computation | async-start | bytes 2621440 | tf_op jit(solution)/shard_map/all_to_all | solution.py:138
  275.1 0.1 reshape.275
  275.2 0.0 copy-done.2
  275.2 0.1 fusion.22
  275.4 0.2 iota_compare_fusion
  275.6 0.6 broadcast_and_fusion.1
  276.2 0.3 and.188
  276.5 0.3 and.210
  276.8 33.8 %all-to-all-done = bf16[128,8,640]{2,1,0:T(8,128)(2,1)S(1)} async-done(((bf16[128,8,640]{2,1,0:T(8,128)(2,1)}), bf16[128,8,640]{2,1,0:T(8,128)(2,1)S(1)}, u32[]{:S(2)}, u32[]{:S(2)}) %all-to-all-start) | async-done | bytes 1310752 | tf_op jit(solution)/shard_map/all_to_all | solution.py:138
  310.6 0.4 fusion.5
  311.0 0.4 fusion.8
  311.4 0.8 pad_maximum_fusion
  (9 shorter events, 0.2 us)
Async XLA Ops:
  6.5 255.0 %all-reduce.3.cloned.1.call-start = ((), (), s32[]{:S(2)}) async-start(), calls=%async_computation.1 | async-start | bytes 262144 | tf_op jit(solution)/shard_map/psum | solution.py:110
  7.3 0.6 copy-start.1
  18.2 245.7 %copy-start = (bf16[128,1280]{1,0:T(8,128)(2,1)S(1)}, bf16[128,1280]{1,0:T(8,128)(2,1)}, u32[]{:S(2)}) copy-start(bf16[128,1280]{1,0:T(8,128)(2,1)} %shard_map.91) | copy-start | bytes 983044
  266.1 9.1 %copy-start.2 = (f32[256,128]{1,0:T(8,128)S(1)}, f32[256,128]{1,0:T(8,128)}, u32[]{:S(2)}) copy-start(f32[256,128]{1,0:T(8,128)} %all-reduce.3.cloned.1.call-done) | copy-start | bytes 393220
  266.1 44.5 %all-to-all-start = ((bf16[128,8,640]{2,1,0:T(8,128)(2,1)}), bf16[128,8,640]{2,1,0:T(8,128)(2,1)S(1)}, u32[]{:S(2)}, u32[]{:S(2)}) async-start(bf16[128,8,640]{2,1,0:T(8,128)(2,1)} %fusion), calls=%async_computation | async-start | bytes 2621440 | tf_op jit(solution)/shard_map/all_to_all | solution.py:138
Sparse Core Ops, SparseCore 0:
  12.8 248.6 all-reduce.2

commit v12 on v9

--- a/solution.py
+++ b/solution.py
@@ -93,9 +93,14 @@
     )(cache_len, new_qkv, cache_kv, resid, ff_gain, w_up, w_down)
 
 
+REQ = ("y", "z", "x")
+PLANE = ("z", "x")
+
+
 def local(new_qkv, cache_kv, resid, span_len, cache_len, series_perm, ff_gain, w_up, w_down):
-    group_size = lax.axis_size("req")
-    me = lax.axis_index("req")
+    group_size = lax.axis_size(REQ)
+    me = lax.axis_index(REQ)
+    plane = lax.axis_size(PLANE)
     series_here, span_slots, triple = new_qkv.shape
     width = resid.shape[2]
     layer_out = layer_block(new_qkv, cache_kv, resid, cache_len, ff_gain, w_up, w_down)
@@ -103,7 +108,7 @@
         [jnp.broadcast_to(span_len[None], (group_size, series_here)),
          jnp.broadcast_to(series_perm[None], (group_size, series_here))], axis=1
     )
-    gathered = lax.all_to_all(info, "req", 0, 0, tiled=True)
+    gathered = lax.all_to_all(info, REQ, 0, 0, tiled=True)
     all_len = gathered[:, :series_here].reshape(-1)
     all_perm = gathered[:, series_here:].reshape(-1)
     series_total = all_len.shape[0]
@@ -112,14 +117,14 @@
 
 
     my_start = lax.dynamic_slice(all_start, (me * series_here,), (series_here,))
-    target = jnp.arange(group_size, dtype=jnp.int32)[None, :, None]
+    target = jnp.arange(plane, dtype=jnp.int32)[None, :, None]
     slot = jnp.arange(span_slots, dtype=jnp.int32)[None, None, :]
-    my_offset = (target - my_start[:, None, None]) % group_size
+    my_offset = (target - my_start[:, None, None]) % plane
     pick = (my_offset == slot) & (slot < span_len[:, None, None])
     half = width // 2
     same = jnp.arange(series_here)[:, None] == jnp.arange(series_here)[None, :]
     pick = pick.transpose(1, 0, 2)[:, :, None, :] & same[None, :, :, None]
-    pick = pick.reshape(group_size, series_here, 1, series_here * span_slots)
+    pick = pick.reshape(plane, series_here, 1, series_here * span_slots)
     halves = jnp.arange(2)[None, None, :, None]
     rows_here = series_here * span_slots
     placed = 0
@@ -129,7 +134,11 @@
             pick_h, layer_out[:, h * half : (h + 1) * half], preferred_element_type=jnp.float32
         )
     placed = placed.astype(jnp.bfloat16)
-    arrived = lax.all_to_all(placed, "req", 0, 0, tiled=True)
+    in_plane = lax.all_to_all(placed, PLANE, 0, 0, tiled=True)
+    ys = group_size // plane
+    arrived = lax.all_to_all(
+        jnp.broadcast_to(in_plane[None], (ys,) + in_plane.shape), "y", 0, 0, tiled=True
+    ).reshape(-1, in_plane.shape[1])
 
     src_start = all_start.reshape(group_size, series_here)
     src_len = all_len.reshape(group_size, series_here)
@@ -153,16 +162,20 @@
 
 
 def solution(mesh):
+    grp = mesh.shape["grp"]
+    req = mesh.shape["req"]
+    fine = jax.sharding.Mesh(mesh.devices.reshape(grp, req // 32, 8, 4), ("grp",) + REQ)
+    rows = ("grp",) + REQ
     in_specs = (
-        P(("grp", "req"), None, None),
-        P(("grp", "req"), None, None),
-        P(("grp", "req"), None, None),
-        P(("grp", "req")),
-        P(("grp", "req")),
-        P(("grp", "req")),
+        P(rows, None, None),
+        P(rows, None, None),
+        P(rows, None, None),
+        P(rows),
+        P(rows),
+        P(rows),
         P(),
         P(),
         P(),
     )
-    out_specs = P(("grp", "req"), None)
-    return jax.shard_map(local, mesh=mesh, in_specs=in_specs, out_specs=out_specs, check_vma=False)
+    out_specs = P(rows, None)
+    return jax.shard_map(local, mesh=fine, in_specs=in_specs, out_specs=out_specs, check_vma=False)

time: 81.4 us -> 75 us (0.921)
  blocking collectives: 0 us -> 22 us
  waiting for transfers between devices: 33.6 us -> 13.2 us
  starting transfers between devices: 28.6 us -> 20.5 us
    all_to_all x0 -> x1, blocking collectives: none -> 22 us  [local(): in_plane = lax.all_to_all(placed, PLANE, 0, 0, tiled=True)]
    all_to_all x2, waiting for transfers between devices: 33.6 us -> 13.2 us  [the longest x1 12.4 us: local(): lax.all_to_all(jnp.broadcast_to(in_plane[None], (ys,) + in_plane.shape),...]
    all_to_all x2, starting transfers between devices: 28.6 us -> 20.5 us  [the longest x1 15.4 us: local(): gathered = lax.all_to_all(info, REQ, 0, 0, tiled=True)]
    broadcast_in_dim x0 -> x1, local copies, waits for them, and re-layouts: none -> 1.17 us  [local(): jnp.broadcast_to(in_plane[None], (ys,) + in_plane.shape)]
  transfers between devices with their start and end apart: 2 -> 2, of which waited for: 2 -> 2; matrix products, arithmetic and copies ran while one was open for 4% -> 4% of each run, Pallas kernels for 11% -> 12%
where the time goes in v12:
time: 75 us; the launch traced here: 74.4 us
  blocking collectives  22 us (29%)
  starting transfers between devices  20.5 us (27%)
  waiting for transfers between devices  13.2 us (18%)
  Pallas kernels  8.93 us (12%)
  local copies, waits for them, and re-layouts  3.74 us (5%)
  other arithmetic  3.51 us (5%)
  matrix products  2.34 us (3%)
    all_to_all x1, blocking collectives, local(): in_plane = lax.all_to_all(placed, PLANE, 0, 0, tiled=True)  22 us
    all_to_all x1, starting transfers between devices, local(): gathered = lax.all_to_all(info, REQ, 0, 0, tiled=True)  15.4 us
    all_to_all x1, waiting for transfers between devices, local(): lax.all_to_all(jnp.broadcast_to(in_plane[None], (ys,) + in_plane.shape),...  12.4 us
    pallas_call x1, Pallas kernels, layer_block(): pl.pallas_call(block_kernel, in_specs=[pl.BlockSpec(memory_space=pltpu.SM...  8.93 us
    all_to_all x1, starting transfers between devices, local(): lax.all_to_all(jnp.broadcast_to(in_plane[None], (ys,) + in_plane.shape),...  5.01 us
  transfers between devices with their start and end apart: 2, of which 2 were waited for; matrix products, arithmetic and copies ran while one was open for 4% of the time, Pallas kernels for 12%

profile of v12, /device:TPU:8, one launch (start us, length us, event | category | flops | bytes accessed | tf_op | source)
XLA Modules:
  0.0 74.4 jit_solution(7184698466098563609)
XLA Ops:
  0.0 0.7 %pad_add_fusion = s32[8]{0:T(128)S(1)} fusion(s32[4]{0:T(128)} %param.14, s32[4]{0:T(128)} %param.12), kind=kLoop, calls=%fused_computation.42 | loop fusion | flops 8 | bytes 64 | tf_op jit(solution)/shard_map/concatenate | solution.py:107
  0.7 0.6 broadcast.207.clone
  1.4 15.4 %all-to-all-start = ((s32[128,1,8]{2,1,0:T(1,128)}), s32[128,1,8]{2,1,0:T(1,128)S(1)}, u32[]{:S(2)}, u32[]{:S(2)}) async-start(s32[128,1,8]{2,1,0:T(1,128)} %bitcast), calls=%async_computation | async-start | bytes 131072 | tf_op jit(solution)/shard_map/all_to_all | solution.py:111
  16.8 0.7 iota_compare_fusion.3
  17.6 0.1 and.155
  17.6 0.1 and.156
  17.8 0.1 and.162
  17.9 0.1 and.166
  18.1 8.9 %shard_map.91 = bf16[128,1280]{1,0:T(8,128)(2,1)} custom-call(s32[4]{0:T(128)} %cache_len_ref.1, bf16[4,32,3840]{2,1,0:T(8,128)(2,1)} %qkv_ref.1, bf16[4,32,2560]{2,1,0:T(8,128)(2,1)} %cache_ref.1, bf16[4,32,1280]{2,1,0:T(8,128)(2,1)} %resid_ref.1, f32[1280]{0:T(1024)} %gain_ref.1, bf16[1280,1280]{1,0:T(8,128)(2,1)} %up_hbm.1, bf16[1280,1280]{1,0:T(8,128)(2,1)} %down_hbm.1), custom_call_target="tpu_custom_call" | custom-call | tf_op jit(solution)/shard_map/pallas_call | solution.py:82
  27.0 0.0 copy-start
  27.0 0.7 all-to-all-done
  27.8 0.1 fusion.19
  27.8 0.1 broadcast_in_dim.25
  27.9 0.1 lt.51
  28.1 0.3 select_reduce_fusion
  28.3 0.1 dynamic_slice.3
  28.4 0.1 fusion.13
  28.5 0.1 and.153
  28.6 0.1 and.154
  28.8 0.1 and.159
  28.8 0.1 and.160
  28.9 1.2 %fusion.3 = f32[256,640]{1,0:T(8,128)S(1)} fusion(bf16[128,1280]{1,0:T(8,128)(2,1)} %shard_map.91, pred[256,128]{1,0:T(32,128)(4,1)S(1)} %and.160, pred[256]{0:T(512)(128)(4,1)S(1)} %and.162), kind=kOutput, calls=%fused_computation.11 | convolution fusion | flops 41975808 | bytes 852224 | tf_op jit(solution)/shard_map/dot_general | solution.py:133
  30.1 0.0 copy-done
  30.2 0.3 fusion.1
  30.4 22.0 %all_to_all.26 = bf16[32,8,640]{2,1,0:T(8,128)(2,1)S(1)} all-to-all(bf16[32,8,640]{2,1,0:T(8,128)(2,1)S(1)} %fusion.1), channel_id=1, replica_groups=mesh['grp'=2,'y'=4,'z'=8,'x'=4] {'z','x'}, dimensions={0} | all-to-all | bytes 655360 | tf_op jit(solution)/shard_map/all_to_all | solution.py:137
  52.5 1.2 %broadcast_in_dim.29 = bf16[4,256,640]{2,1,0:T(8,128)(2,1)} broadcast(bf16[256,640]{1,0:T(8,128)(2,1)S(1)} %bitcast.19), dimensions={1,2} | broadcast | bytes 1638400 | tf_op jit(solution)/shard_map/broadcast_in_dim | solution.py:140
  53.7 5.0 %all-to-all-start.2 = ((bf16[4,256,640]{2,1,0:T(8,128)(2,1)}), bf16[4,256,640]{2,1,0:T(8,128)(2,1)S(1)}, u32[]{:S(2)}, u32[]{:S(2)}) async-start(bf16[4,256,640]{2,1,0:T(8,128)(2,1)} %broadcast_in_dim.29), calls=%async_computation.2 | async-start | bytes 2621440 | tf_op jit(solution)/shard_map/all_to_all | solution.py:139
  58.7 0.1 reshape.205
  58.8 0.1 fusion.9
  58.9 0.2 iota_compare_fusion
  59.1 0.6 broadcast_and_fusion.1
  59.7 0.3 and.149
  60.0 0.3 and.171
  60.3 12.4 %all-to-all-done.2 = bf16[4,256,640]{2,1,0:T(8,128)(2,1)S(1)} async-done(((bf16[4,256,640]{2,1,0:T(8,128)(2,1)}), bf16[4,256,640]{2,1,0:T(8,128)(2,1)S(1)}, u32[]{:S(2)}, u32[]{:S(2)}) %all-to-all-start.2) | async-done | bytes 1310752 | tf_op jit(solution)/shard_map/all_to_all | solution.py:139
  72.8 0.4 convolution_convert_fusion.1
  73.2 0.4 convolution_convert_fusion
  73.6 0.8 %pad_maximum_fusion = bf16[128,1280]{1,0:T(8,128)(2,1)} fusion(bf16[128,640]{1,0:T(8,128)(2,1)S(1)} %convolution_convert_fusion, bf16[128,640]{1,0:T(8,128)(2,1)S(1)} %convolution_convert_fusion.1), kind=kLoop, calls=%fused_computation.8 | loop fusion | flops 655360 | bytes 655360 | tf_op jit(solution)/shard_map/concatenate | solution.py:150
  (7 shorter events, 0.1 us)
Async XLA Ops:
  1.4 26.4 %all-to-all-start = ((s32[128,1,8]{2,1,0:T(1,128)}), s32[128,1,8]{2,1,0:T(1,128)S(1)}, u32[]{:S(2)}, u32[]{:S(2)}) async-start(s32[128,1,8]{2,1,0:T(1,128)} %bitcast), calls=%async_computation | async-start | bytes 131072 | tf_op jit(solution)/shard_map/all_to_all | solution.py:111
  27.0 3.1 %copy-start = (bf16[128,1280]{1,0:T(8,128)(2,1)S(1)}, bf16[128,1280]{1,0:T(8,128)(2,1)}, u32[]{:S(2)}) copy-start(bf16[128,1280]{1,0:T(8,128)(2,1)} %shard_map.91) | copy-start | bytes 983044
  53.7 19.1 %all-to-all-start.2 = ((bf16[4,256,640]{2,1,0:T(8,128)(2,1)}), bf16[4,256,640]{2,1,0:T(8,128)(2,1)S(1)}, u32[]{:S(2)}, u32[]{:S(2)}) async-start(bf16[4,256,640]{2,1,0:T(8,128)(2,1)} %broadcast_in_dim.29), calls=%async_computation.2 | async-start | bytes 2621440 | tf_op jit(solution)/shard_map/all_to_all | solution.py:139

commit v13 on v12

--- a/solution.py
+++ b/solution.py
@@ -136,15 +136,19 @@
     placed = placed.astype(jnp.bfloat16)
     in_plane = lax.all_to_all(placed, PLANE, 0, 0, tiled=True)
     ys = group_size // plane
-    arrived = lax.all_to_all(
-        jnp.broadcast_to(in_plane[None], (ys,) + in_plane.shape), "y", 0, 0, tiled=True
-    ).reshape(-1, in_plane.shape[1])
+    arrived = jnp.concatenate(
+        [in_plane]
+        + [lax.ppermute(in_plane, "y", [(j, (j + k) % ys) for j in range(ys)]) for k in range(1, ys)],
+        axis=0,
+    )
 
     src_start = all_start.reshape(group_size, series_here)
     src_len = all_len.reshape(group_size, series_here)
     src_t = (me - src_start) % group_size
     src_row = (src_start + src_t) // group_size
     src_row = jnp.where(src_t < src_len, src_row, -1)
+    src_row = src_row.reshape(ys, plane, series_here)[::-1]
+    src_row = jnp.roll(src_row, lax.axis_index("y") + 1, axis=0).reshape(group_size, series_here)
     out_row = jnp.arange(rows_here, dtype=jnp.int32)[:, None, None, None]
     hit = src_row[None, :, :, None] == out_row
     result = jnp.concatenate(

time: 75 us -> 75.8 us (1.011)
  the two profiles are of different devices: /device:TPU:8 before, /device:TPU:1 now
where the time goes in v13:
time: 75.8 us; the launch traced here: 75.5 us
  starting transfers between devices  28.5 us (38%)
  waiting for transfers between devices  27.2 us (36%)
  Pallas kernels  8.93 us (12%)
  matrix products  4.55 us (6%)
  local copies, waits for them, and re-layouts  3.2 us (4%)
  other arithmetic  2.93 us (4%)
    all_to_all x1, starting transfers between devices, local(): gathered = lax.all_to_all(info, REQ, 0, 0, tiled=True)  16.3 us
    ppermute x3, waiting for transfers between devices, local(): lax.ppermute(in_plane, 'y', [(j, (j + k) % ys) for j in range(ys)])  15.7 us
    all_to_all x1, waiting for transfers between devices, local(): in_plane = lax.all_to_all(placed, PLANE, 0, 0, tiled=True)  11.1 us
    pallas_call x1, Pallas kernels, layer_block(): pl.pallas_call(block_kernel, in_specs=[pl.BlockSpec(memory_space=pltpu.SM...  8.93 us
    all_to_all x1, starting transfers between devices, local(): in_plane = lax.all_to_all(placed, PLANE, 0, 0, tiled=True)  8.15 us
    ppermute x3, starting transfers between devices, local(): lax.ppermute(in_plane, 'y', [(j, (j + k) % ys) for j in range(ys)])  4.01 us
    dot_general x2, matrix products, local(): jnp.dot(pick_h, layer_out[:, h * half:(h + 1) * half], preferred_element_...  3.14 us
  transfers between devices with their start and end apart: 5, of which 5 were waited for; matrix products, arithmetic and copies ran while one was open for 4% of the time, Pallas kernels for 12%

profile of v13, /device:TPU:1, one launch (start us, length us, event | category | flops | bytes accessed | tf_op | source)
XLA Modules:
  0.0 75.5 jit_solution(9182459936701533997)
XLA Ops:
  0.0 0.7 pad_add_fusion
  0.7 0.6 broadcast.157.clone
  1.4 16.3 %all-to-all-start = ((s32[128,1,8]{2,1,0:T(1,128)}), s32[128,1,8]{2,1,0:T(1,128)S(1)}, u32[]{:S(2)}, u32[]{:S(2)}) async-start(s32[128,1,8]{2,1,0:T(1,128)} %bitcast), calls=%async_computation | async-start | bytes 131072 | tf_op jit(solution)/shard_map/all_to_all | solution.py:111
  17.7 0.7 iota_compare_fusion.3
  18.5 0.1 and.156
  18.5 0.1 and.157
  18.6 0.1 and.167
  18.8 0.1 and.163
  19.0 8.9 %shard_map.91 = bf16[128,1280]{1,0:T(8,128)(2,1)} custom-call(s32[4]{0:T(128)} %cache_len_ref.1, bf16[4,32,3840]{2,1,0:T(8,128)(2,1)} %qkv_ref.1, bf16[4,32,2560]{2,1,0:T(8,128)(2,1)} %cache_ref.1, bf16[4,32,1280]{2,1,0:T(8,128)(2,1)} %resid_ref.1, f32[1280]{0:T(1024)} %gain_ref.1, bf16[1280,1280]{1,0:T(8,128)(2,1)} %up_hbm.1, bf16[1280,1280]{1,0:T(8,128)(2,1)} %down_hbm.1), custom_call_target="tpu_custom_call" | custom-call | tf_op jit(solution)/shard_map/pallas_call | solution.py:82
  27.9 0.4 all-to-all-done
  28.3 0.1 fusion.26
  28.4 0.1 lt.63
  28.5 0.1 broadcast_in_dim.21
  28.6 0.3 select_reduce_fusion
  28.9 0.1 dynamic_slice.8
  29.0 0.1 fusion.17
  29.1 0.1 and.154
  29.2 0.1 and.155
  29.3 0.1 and.160
  29.4 0.1 and.161
  29.5 1.2 %fusion.7 = f32[256,640]{1,0:T(8,128)S(1)} fusion(bf16[128,1280]{1,0:T(8,128)(2,1)} %shard_map.91, pred[256,128]{1,0:T(32,128)(4,1)S(1)} %and.161, pred[256]{0:T(512)(128)(4,1)S(1)} %and.163), kind=kOutput, calls=%fused_computation.14 | convolution fusion | flops 41975808 | bytes 852224 | tf_op jit(solution)/shard_map/dot_general | solution.py:133
  30.7 1.9 %fusion.1 = bf16[32,8,640]{2,1,0:T(8,128)(2,1)} fusion(f32[256,640]{1,0:T(8,128)S(1)} %fusion.7, bf16[128,1280]{1,0:T(8,128)(2,1)} %shard_map.91, pred[256,128]{1,0:T(32,128)(4,1)S(1)} %and.161, pred[256]{0:T(512)(128)(4,1)S(1)} %and.167), kind=kOutput, calls=%fused_computation.3 | convolution fusion | flops 42303488 | bytes 1179904 | tf_op jit(solution)/shard_map/dot_general | solution.py:133
  32.6 8.2 %all-to-all-start.1 = ((bf16[32,8,640]{2,1,0:T(8,128)(2,1)}), bf16[32,8,640]{2,1,0:T(8,128)(2,1)S(1)}, u32[]{:S(2)}, u32[]{:S(2)}) async-start(bf16[32,8,640]{2,1,0:T(8,128)(2,1)} %fusion.1), calls=%async_computation.1 | async-start | bytes 655360 | tf_op jit(solution)/shard_map/all_to_all | solution.py:137
  40.9 0.2 and.148
  41.1 0.2 and.171
  41.3 0.1 reshape.143
  41.4 0.1 fusion.13
  41.5 0.1 copy.16
  41.6 11.1 %all-to-all-done.1 = bf16[32,8,640]{2,1,0:T(8,128)(2,1)S(1)} async-done(((bf16[32,8,640]{2,1,0:T(8,128)(2,1)}), bf16[32,8,640]{2,1,0:T(8,128)(2,1)S(1)}, u32[]{:S(2)}, u32[]{:S(2)}) %all-to-all-start.1) | async-done | bytes 327712 | tf_op jit(solution)/shard_map/all_to_all | solution.py:137
  52.7 3.1 %collective-permute-start.2 = (bf16[256,640]{1,0:T(8,128)(2,1)S(1)}, bf16[256,640]{1,0:T(8,128)(2,1)S(1)}, u32[]{:S(2)}, u32[]{:S(2)}) collective-permute-start(bf16[256,640]{1,0:T(8,128)(2,1)S(1)} %bitcast.14), channel_id=1, source_target_pairs={{0,96},{32,0},{64,32},{96,64},{1,97},{33,1},{65,33},{97,65},{2,98}... | collective-permute-start | bytes 983048 | tf_op jit(solution)/shard_map/ppermute | solution.py:141
  55.7 0.1 collective-permute-start.1
  55.8 0.8 %collective-permute-start = (bf16[256,640]{1,0:T(8,128)(2,1)S(1)}, bf16[256,640]{1,0:T(8,128)(2,1)S(1)}, u32[]{:S(2)}, u32[]{:S(2)}) collective-permute-start(bf16[256,640]{1,0:T(8,128)(2,1)S(1)} %bitcast.16), channel_id=1, source_target_pairs={{0,32},{32,64},{64,96},{96,0},{1,33},{33,65},{65,97},{97,1},{2,34}... | collective-permute-start | bytes 983048 | tf_op jit(solution)/shard_map/ppermute | solution.py:141
  56.7 0.1 copy.18
  56.8 0.2 iota_compare_fusion
  57.0 0.3 and.145
  57.3 0.3 and.146
  57.6 5.4 %collective-permute-done.2 = bf16[256,640]{1,0:T(8,128)(2,1)S(1)} collective-permute-done((bf16[256,640]{1,0:T(8,128)(2,1)S(1)}, bf16[256,640]{1,0:T(8,128)(2,1)S(1)}, u32[]{:S(2)}, u32[]{:S(2)}) %collective-permute-start.2) | collective-permute-done | bytes 327712 | tf_op jit(solution)/shard_map/ppermute | solution.py:141
  63.0 0.3 collective-permute-done.1
  63.2 10.1 %collective-permute-done = bf16[256,640]{1,0:T(8,128)(2,1)S(1)} collective-permute-done((bf16[256,640]{1,0:T(8,128)(2,1)S(1)}, bf16[256,640]{1,0:T(8,128)(2,1)S(1)}, u32[]{:S(2)}, u32[]{:S(2)}) %collective-permute-start) | collective-permute-done | bytes 327712 | tf_op jit(solution)/shard_map/ppermute | solution.py:141
  73.3 0.7 convolution_convert_fusion
  74.0 0.7 convolution_convert_fusion.1
  74.7 0.8 pad_maximum_fusion.1
  (12 shorter events, 0.2 us)
Async XLA Ops:
  1.4 26.9 %all-to-all-start = ((s32[128,1,8]{2,1,0:T(1,128)}), s32[128,1,8]{2,1,0:T(1,128)S(1)}, u32[]{:S(2)}, u32[]{:S(2)}) async-start(s32[128,1,8]{2,1,0:T(1,128)} %bitcast), calls=%async_computation | async-start | bytes 131072 | tf_op jit(solution)/shard_map/all_to_all | solution.py:111
  32.6 20.0 %all-to-all-start.1 = ((bf16[32,8,640]{2,1,0:T(8,128)(2,1)}), bf16[32,8,640]{2,1,0:T(8,128)(2,1)S(1)}, u32[]{:S(2)}, u32[]{:S(2)}) async-start(bf16[32,8,640]{2,1,0:T(8,128)(2,1)} %fusion.1), calls=%async_computation.1 | async-start | bytes 655360 | tf_op jit(solution)/shard_map/all_to_all | solution.py:137
  52.7 10.3 %collective-permute-start.2 = (bf16[256,640]{1,0:T(8,128)(2,1)S(1)}, bf16[256,640]{1,0:T(8,128)(2,1)S(1)}, u32[]{:S(2)}, u32[]{:S(2)}) collective-permute-start(bf16[256,640]{1,0:T(8,128)(2,1)S(1)} %bitcast.14), channel_id=1, source_target_pairs={{0,96},{32,0},{64,32},{96,64},{1,97},{33,1},{65,33},{97,65},{2,98}... | collective-permute-start | bytes 983048 | tf_op jit(solution)/shard_map/ppermute | solution.py:141
  55.7 7.5 %collective-permute-start.1 = (bf16[256,640]{1,0:T(8,128)(2,1)S(1)}, bf16[256,640]{1,0:T(8,128)(2,1)S(1)}, u32[]{:S(2)}, u32[]{:S(2)}) collective-permute-start(bf16[256,640]{1,0:T(8,128)(2,1)S(1)} %bitcast.15), channel_id=1, source_target_pairs={{0,64},{32,96},{64,0},{96,32},{1,65},{33,97},{65,1},{97,33},{2,66}... | collective-permute-start | bytes 983048 | tf_op jit(solution)/shard_map/ppermute | solution.py:141
  55.8 17.5 %collective-permute-start = (bf16[256,640]{1,0:T(8,128)(2,1)S(1)}, bf16[256,640]{1,0:T(8,128)(2,1)S(1)}, u32[]{:S(2)}, u32[]{:S(2)}) collective-permute-start(bf16[256,640]{1,0:T(8,128)(2,1)S(1)} %bitcast.16), channel_id=1, source_target_pairs={{0,32},{32,64},{64,96},{96,0},{1,33},{33,65},{65,97},{97,1},{2,34}... | collective-permute-start | bytes 983048 | tf_op jit(solution)/shard_map/ppermute | solution.py:141

commit v14 on v12

--- a/solution.py
+++ b/solution.py
@@ -136,9 +136,7 @@
     placed = placed.astype(jnp.bfloat16)
     in_plane = lax.all_to_all(placed, PLANE, 0, 0, tiled=True)
     ys = group_size // plane
-    arrived = lax.all_to_all(
-        jnp.broadcast_to(in_plane[None], (ys,) + in_plane.shape), "y", 0, 0, tiled=True
-    ).reshape(-1, in_plane.shape[1])
+    arrived = lax.all_gather(in_plane, "y", axis=0, tiled=True)
 
     src_start = all_start.reshape(group_size, series_here)
     src_len = all_len.reshape(group_size, series_here)

time: 75 us -> 93.4 us (1.25)
  between operations: 0.18 us -> 13.6 us
  waiting for transfers between devices: 13.2 us -> 21.9 us
  starting transfers between devices: 20.5 us -> 15.5 us
  matrix products: 2.34 us -> 4.32 us
    all_gather x0 -> x1, waiting for transfers between devices: none -> 21.2 us  [local(): arrived = lax.all_gather(in_plane, 'y', axis=0, tiled=True)]
    all_to_all x1 -> x0, waiting for transfers between devices: 12.4 us -> none  [local(): lax.all_to_all(jnp.broadcast_to(in_plane[None], (ys,) + in_plane.shape),...]
    all_to_all x1 -> x0, starting transfers between devices: 5.01 us -> none  [local(): lax.all_to_all(jnp.broadcast_to(in_plane[None], (ys,) + in_plane.shape),...]
    dot_general x2, matrix products: 0.85 us -> 2.83 us  [local(): jnp.dot((hit & (halves.reshape(1, 1, 1, 2) == h)).reshape(rows_here, -1)....]
    broadcast_in_dim x1 -> x0, local copies, waits for them, and re-layouts: 1.17 us -> none  [local(): jnp.broadcast_to(in_plane[None], (ys,) + in_plane.shape)]
  transfers between devices with their start and end apart: 2 -> 2, of which waited for: 2 -> 2; matrix products, arithmetic and copies ran while one was open for 4% -> 3% of each run, Pallas kernels for 12% -> 10%
where the time goes in v14:
time: 93.4 us; the launch traced here: 92.3 us
  blocking collectives  22.2 us (24%)
  waiting for transfers between devices  21.9 us (23%)
  starting transfers between devices  15.5 us (17%)
  between operations  13.6 us (15%)
  Pallas kernels  8.92 us (10%)
  matrix products  4.32 us (5%)
  local copies, waits for them, and re-layouts  2.98 us (3%)
  other arithmetic  2.91 us (3%)
    all_to_all x1, blocking collectives, local(): in_plane = lax.all_to_all(placed, PLANE, 0, 0, tiled=True)  22.2 us
    all_gather x1, waiting for transfers between devices, local(): arrived = lax.all_gather(in_plane, 'y', axis=0, tiled=True)  21.2 us
    all_to_all x1, starting transfers between devices, local(): gathered = lax.all_to_all(info, REQ, 0, 0, tiled=True)  15.4 us
    pallas_call x1, Pallas kernels, layer_block(): pl.pallas_call(block_kernel, in_specs=[pl.BlockSpec(memory_space=pltpu.SM...  8.92 us
    dot_general x2, matrix products, local(): jnp.dot((hit & (halves.reshape(1, 1, 1, 2) == h)).reshape(rows_here, -1)....  2.83 us
  transfers between devices with their start and end apart: 2, of which 2 were waited for; matrix products, arithmetic and copies ran while one was open for 3% of the time, Pallas kernels for 10%

profile of v14, /device:TPU:8, one launch (start us, length us, event | category | flops | bytes accessed | tf_op | source)
XLA Modules:
  0.0 92.3 jit_solution(11252953752129302341)
XLA Ops:
  6.5 0.7 pad_add_fusion
  7.3 0.6 broadcast.157.clone
  7.9 15.4 %all-to-all-start = ((s32[128,1,8]{2,1,0:T(1,128)}), s32[128,1,8]{2,1,0:T(1,128)S(1)}, u32[]{:S(2)}, u32[]{:S(2)}) async-start(s32[128,1,8]{2,1,0:T(1,128)} %bitcast), calls=%async_computation | async-start | bytes 131072 | tf_op jit(solution)/shard_map/all_to_all | solution.py:111
  23.4 0.0 all-gather.2.cloned.1.call-start
  23.4 0.7 iota_compare_fusion.3
  24.2 0.1 and.149
  24.2 0.1 and.150
  24.3 0.1 and.156
  24.5 0.1 and.160
  24.7 8.9 %shard_map.91 = bf16[128,1280]{1,0:T(8,128)(2,1)} custom-call(s32[4]{0:T(128)} %cache_len_ref.1, bf16[4,32,3840]{2,1,0:T(8,128)(2,1)} %qkv_ref.1, bf16[4,32,2560]{2,1,0:T(8,128)(2,1)} %cache_ref.1, bf16[4,32,1280]{2,1,0:T(8,128)(2,1)} %resid_ref.1, f32[1280]{0:T(1024)} %gain_ref.1, bf16[1280,1280]{1,0:T(8,128)(2,1)} %up_hbm.1, bf16[1280,1280]{1,0:T(8,128)(2,1)} %down_hbm.1), custom_call_target="tpu_custom_call" | custom-call | tf_op jit(solution)/shard_map/pallas_call | solution.py:82
  33.6 0.0 copy-start.1
  33.6 0.7 all-to-all-done
  34.3 0.1 fusion.23
  34.4 0.1 broadcast_in_dim.21
  34.5 0.1 lt.51
  34.6 0.3 select_reduce_fusion
  34.8 0.1 dynamic_slice.3
  34.9 0.1 fusion.17
  35.1 0.1 and.147
  35.1 0.1 and.148
  35.3 0.1 and.153
  35.4 0.1 and.154
  35.5 1.2 %fusion.7 = f32[256,640]{1,0:T(8,128)S(1)} fusion(bf16[128,1280]{1,0:T(8,128)(2,1)} %shard_map.91, pred[256,128]{1,0:T(32,128)(4,1)S(1)} %and.154, pred[256]{0:T(512)(128)(4,1)S(1)} %and.156), kind=kOutput, calls=%fused_computation.13 | convolution fusion | flops 41975808 | bytes 852224 | tf_op jit(solution)/shard_map/dot_general | solution.py:133
  36.7 0.0 copy-done.1
  36.7 0.3 fusion.1
  37.0 22.2 %all_to_all.24 = bf16[32,8,640]{2,1,0:T(8,128)(2,1)} all-to-all(bf16[32,8,640]{2,1,0:T(8,128)(2,1)S(1)} %fusion.1), channel_id=1, replica_groups=mesh['grp'=2,'y'=4,'z'=8,'x'=4] {'z','x'}, dimensions={0} | all-to-all | bytes 655360 | tf_op jit(solution)/shard_map/all_to_all | solution.py:137
  59.2 0.0 all-gather.2.cloned.1.call-update
  59.2 0.2 and.141
  59.5 0.2 and.164
  59.7 0.1 reshape.140
  59.8 0.1 fusion.13
  59.9 0.2 iota_compare_fusion
  60.1 0.3 and.138
  60.3 0.3 and.139
  60.7 21.2 %all-gather.2.cloned.1.call-done = bf16[1024,640]{1,0:T(8,128)(2,1)} async-done(((bf16[256,640]{1,0:T(8,128)(2,1)}), bf16[1024,640]{1,0:T(8,128)(2,1)}) %all-gather.2.cloned.1.call-update) | async-done | bytes 1310736 | tf_op jit(solution)/shard_map/all_gather | solution.py:139
  81.8 0.0 copy-start
  81.8 2.1 %convolution_convert_fusion.1 = bf16[128,640]{1,0:T(8,128)(2,1)S(1)} fusion(bf16[1024,640]{1,0:T(8,128)(2,1)} %all-gather.2.cloned.1.call-done, pred[128,1024]{0,1:T(32,128)(4,1)S(1)} %and.139, pred[1024]{0:T(1024)(128)(4,1)S(1)} %and.141), kind=kOutput, calls=%fused_computation.4 | convolution fusion | flops 167985152 | bytes 1606656 | tf_op jit(solution)/shard_map/dot_general | solution.py:150
  84.0 0.0 copy-done
  84.0 0.7 convolution_convert_fusion
  84.7 0.8 pad_maximum_fusion
  (10 shorter events, 0.2 us)
Async XLA Ops:
  7.9 26.4 %all-to-all-start = ((s32[128,1,8]{2,1,0:T(1,128)}), s32[128,1,8]{2,1,0:T(1,128)S(1)}, u32[]{:S(2)}, u32[]{:S(2)}) async-start(s32[128,1,8]{2,1,0:T(1,128)} %bitcast), calls=%async_computation | async-start | bytes 131072 | tf_op jit(solution)/shard_map/all_to_all | solution.py:111
  23.4 58.5 %all-gather.2.cloned.1.call-start = ((), (), s32[]{:S(2)}) async-start(), calls=%async_computation.2 | async-start | bytes 1638400 | tf_op jit(solution)/shard_map/all_gather | solution.py:139
  33.6 3.1 %copy-start.1 = (bf16[128,1280]{1,0:T(8,128)(2,1)S(1)}, bf16[128,1280]{1,0:T(8,128)(2,1)}, u32[]{:S(2)}) copy-start(bf16[128,1280]{1,0:T(8,128)(2,1)} %shard_map.91) | copy-start | bytes 983044
  81.8 2.1 %copy-start = (bf16[1024,640]{1,0:T(8,128)(2,1)S(1)}, bf16[1024,640]{1,0:T(8,128)(2,1)}, u32[]{:S(2)}) copy-start(bf16[1024,640]{1,0:T(8,128)(2,1)} %all-gather.2.cloned.1.call-done) | copy-start | bytes 3932164
Sparse Core Ops, SparseCore 0:
  59.3 22.4 all-gather.1

commit v15 on v12

--- a/solution.py
+++ b/solution.py
@@ -108,7 +108,11 @@
         [jnp.broadcast_to(span_len[None], (group_size, series_here)),
          jnp.broadcast_to(series_perm[None], (group_size, series_here))], axis=1
     )
-    gathered = lax.all_to_all(info, REQ, 0, 0, tiled=True)
+    ys = group_size // plane
+    in_plane_info = lax.all_to_all(info[:plane], PLANE, 0, 0, tiled=True)
+    gathered = lax.all_to_all(
+        jnp.broadcast_to(in_plane_info[None], (ys,) + in_plane_info.shape), "y", 0, 0, tiled=True
+    ).reshape(group_size, -1)
     all_len = gathered[:, :series_here].reshape(-1)
     all_perm = gathered[:, series_here:].reshape(-1)
     series_total = all_len.shape[0]

time: 75 us -> 78.2 us (1.043)
  waiting for transfers between devices: 13.2 us -> 20.2 us
  blocking collectives: 22 us -> 15.7 us
  local copies, waits for them, and re-layouts: 3.74 us -> 5.18 us
    all_to_all x1 -> x2, waiting for transfers between devices: 0.73 us -> 8.95 us  [the longest x1 8.95 us: local(): in_plane_info = lax.all_to_all(info[:plane], PLANE, 0, 0, tiled=True)]
    all_to_all x1, blocking collectives: 22 us -> 15.7 us  [local(): in_plane = lax.all_to_all(placed, PLANE, 0, 0, tiled=True)]
    all_to_all x1, waiting for transfers between devices: 12.4 us -> 11.3 us  [local(): lax.all_to_all(jnp.broadcast_to(in_plane[None], (ys,) + in_plane.shape),...]
    all_to_all x1 -> x2, starting transfers between devices: 15.4 us -> 16.2 us  [the longest x1 11.3 us: local(): in_plane_info = lax.all_to_all(info[:plane], PLANE, 0, 0, tiled=True)]
  transfers between devices with their start and end apart: 2 -> 3, of which waited for: 2 -> 2; matrix products, arithmetic and copies ran while one was open for 4% -> 4% of each run, Pallas kernels for 12% -> 11%
where the time goes in v15:
time: 78.2 us; the launch traced here: 77.7 us
  starting transfers between devices  21 us (27%)
  waiting for transfers between devices  20.2 us (26%)
  blocking collectives  15.7 us (20%)
  Pallas kernels  8.93 us (11%)
  local copies, waits for them, and re-layouts  5.18 us (7%)
  other arithmetic  4.14 us (5%)
  matrix products  2.33 us (3%)
    all_to_all x1, blocking collectives, local(): in_plane = lax.all_to_all(placed, PLANE, 0, 0, tiled=True)  15.7 us
    all_to_all x1, starting transfers between devices, local(): in_plane_info = lax.all_to_all(info[:plane], PLANE, 0, 0, tiled=True)  11.3 us
    all_to_all x1, waiting for transfers between devices, local(): lax.all_to_all(jnp.broadcast_to(in_plane[None], (ys,) + in_plane.shape),...  11.3 us
    all_to_all x1, waiting for transfers between devices, local(): in_plane_info = lax.all_to_all(info[:plane], PLANE, 0, 0, tiled=True)  8.95 us
    pallas_call x1, Pallas kernels, layer_block(): pl.pallas_call(block_kernel, in_specs=[pl.BlockSpec(memory_space=pltpu.SM...  8.93 us
    all_to_all x1, starting transfers between devices, local(): lax.all_to_all(jnp.broadcast_to(in_plane_info[None], (ys,) + in_plane_inf...  4.91 us
    all_to_all x1, starting transfers between devices, local(): lax.all_to_all(jnp.broadcast_to(in_plane[None], (ys,) + in_plane.shape),...  4.8 us
  transfers between devices with their start and end apart: 3, of which 2 were waited for; matrix products, arithmetic and copies ran while one was open for 4% of the time, Pallas kernels for 11%

profile of v15, /device:TPU:8, one launch (start us, length us, event | category | flops | bytes accessed | tf_op | source)
XLA Modules:
  0.0 77.7 jit_solution(15625908985217985785)
XLA Ops:
  0.0 0.7 pad_add_fusion
  0.7 0.6 broadcast.208.clone
  1.4 11.3 %all-to-all-start = ((s32[32,1,8]{2,1,0:T(1,128)}), s32[32,1,8]{2,1,0:T(1,128)S(1)}, u32[]{:S(2)}, u32[]{:S(2)}) async-start(s32[32,1,8]{2,1,0:T(1,128)} %bitcast), calls=%async_computation | async-start | bytes 32768 | tf_op jit(solution)/shard_map/all_to_all | solution.py:112
  12.7 0.7 iota_compare_fusion.3
  13.4 8.9 %all-to-all-done = s32[32,1,8]{2,1,0:T(1,128)S(1)} async-done(((s32[32,1,8]{2,1,0:T(1,128)}), s32[32,1,8]{2,1,0:T(1,128)S(1)}, u32[]{:S(2)}, u32[]{:S(2)}) %all-to-all-start) | async-done | bytes 1056 | tf_op jit(solution)/shard_map/all_to_all | solution.py:112
  22.4 0.1 copy.14
  22.4 0.7 reshape.215
  23.1 4.9 %all-to-all-start.1 = ((s32[4,1,256]{2,1,0:T(1,128)}), s32[4,1,256]{2,1,0:T(1,128)S(1)}, u32[]{:S(2)}, u32[]{:S(2)}) async-start(s32[4,1,256]{2,1,0:T(1,128)} %reshape.215), calls=%async_computation.1 | async-start | bytes 8192 | tf_op jit(solution)/shard_map/all_to_all | solution.py:113
  28.0 0.1 and.155
  28.1 0.1 and.156
  28.2 0.1 and.162
  28.4 0.1 and.166
  28.5 8.9 %shard_map.91 = bf16[128,1280]{1,0:T(8,128)(2,1)} custom-call(s32[4]{0:T(128)} %cache_len_ref.1, bf16[4,32,3840]{2,1,0:T(8,128)(2,1)} %qkv_ref.1, bf16[4,32,2560]{2,1,0:T(8,128)(2,1)} %cache_ref.1, bf16[4,32,1280]{2,1,0:T(8,128)(2,1)} %resid_ref.1, f32[1280]{0:T(1024)} %gain_ref.1, bf16[1280,1280]{1,0:T(8,128)(2,1)} %up_hbm.1, bf16[1280,1280]{1,0:T(8,128)(2,1)} %down_hbm.1), custom_call_target="tpu_custom_call" | custom-call | tf_op jit(solution)/shard_map/pallas_call | solution.py:82
  37.5 0.0 copy-start
  37.5 0.0 all-to-all-done.1
  37.5 0.5 broadcast.215
  38.0 0.6 reduce
  38.7 0.1 reshape.216
  38.7 0.1 copy.15
  38.8 0.1 fusion.19
  38.9 0.1 broadcast_in_dim.31
  39.0 0.1 lt.51
  39.1 0.3 select_reduce_fusion
  39.4 0.1 dynamic_slice.3
  39.5 0.1 fusion.13
  39.6 0.1 and.153
  39.7 0.1 and.154
  39.8 0.1 and.159
  39.9 0.1 and.160
  40.0 1.2 %fusion.3 = f32[256,640]{1,0:T(8,128)S(1)} fusion(bf16[128,1280]{1,0:T(8,128)(2,1)} %shard_map.91, pred[256,128]{1,0:T(32,128)(4,1)S(1)} %and.160, pred[256]{0:T(512)(128)(4,1)S(1)} %and.162), kind=kOutput, calls=%fused_computation.11 | convolution fusion | flops 41975808 | bytes 852224 | tf_op jit(solution)/shard_map/dot_general | solution.py:137
  41.2 0.0 copy-done
  41.2 0.3 fusion.1
  41.5 15.7 %all_to_all.28 = bf16[32,8,640]{2,1,0:T(8,128)(2,1)S(1)} all-to-all(bf16[32,8,640]{2,1,0:T(8,128)(2,1)S(1)} %fusion.1), channel_id=1, replica_groups=mesh['grp'=2,'y'=4,'z'=8,'x'=4] {'z','x'}, dimensions={0} | all-to-all | bytes 655360 | tf_op jit(solution)/shard_map/all_to_all | solution.py:141
  57.2 1.2 %broadcast_in_dim.36 = bf16[4,256,640]{2,1,0:T(8,128)(2,1)} broadcast(bf16[256,640]{1,0:T(8,128)(2,1)S(1)} %bitcast.23), dimensions={1,2} | broadcast | bytes 1638400 | tf_op jit(solution)/shard_map/broadcast_in_dim | solution.py:144
  58.4 4.8 %all-to-all-start.3 = ((bf16[4,256,640]{2,1,0:T(8,128)(2,1)}), bf16[4,256,640]{2,1,0:T(8,128)(2,1)S(1)}, u32[]{:S(2)}, u32[]{:S(2)}) async-start(bf16[4,256,640]{2,1,0:T(8,128)(2,1)} %broadcast_in_dim.36), calls=%async_computation.3 | async-start | bytes 2621440 | tf_op jit(solution)/shard_map/all_to_all | solution.py:143
  63.2 0.1 reshape.211
  63.3 0.1 fusion.9
  63.4 0.2 iota_compare_fusion
  63.6 0.6 broadcast_and_fusion.1
  64.2 0.3 and.149
  64.5 0.3 and.171
  64.8 11.3 %all-to-all-done.3 = bf16[4,256,640]{2,1,0:T(8,128)(2,1)S(1)} async-done(((bf16[4,256,640]{2,1,0:T(8,128)(2,1)}), bf16[4,256,640]{2,1,0:T(8,128)(2,1)S(1)}, u32[]{:S(2)}, u32[]{:S(2)}) %all-to-all-start.3) | async-done | bytes 1310752 | tf_op jit(solution)/shard_map/all_to_all | solution.py:143
  76.1 0.4 convolution_convert_fusion.1
  76.5 0.4 convolution_convert_fusion
  77.0 0.8 pad_maximum_fusion
  (8 shorter events, 0.1 us)
Async XLA Ops:
  1.4 21.0 %all-to-all-start = ((s32[32,1,8]{2,1,0:T(1,128)}), s32[32,1,8]{2,1,0:T(1,128)S(1)}, u32[]{:S(2)}, u32[]{:S(2)}) async-start(s32[32,1,8]{2,1,0:T(1,128)} %bitcast), calls=%async_computation | async-start | bytes 32768 | tf_op jit(solution)/shard_map/all_to_all | solution.py:112
  23.1 14.4 %all-to-all-start.1 = ((s32[4,1,256]{2,1,0:T(1,128)}), s32[4,1,256]{2,1,0:T(1,128)S(1)}, u32[]{:S(2)}, u32[]{:S(2)}) async-start(s32[4,1,256]{2,1,0:T(1,128)} %reshape.215), calls=%async_computation.1 | async-start | bytes 8192 | tf_op jit(solution)/shard_map/all_to_all | solution.py:113
  37.5 3.7 %copy-start = (bf16[128,1280]{1,0:T(8,128)(2,1)S(1)}, bf16[128,1280]{1,0:T(8,128)(2,1)}, u32[]{:S(2)}) copy-start(bf16[128,1280]{1,0:T(8,128)(2,1)} %shard_map.91) | copy-start | bytes 983044
  58.4 17.7 %all-to-all-start.3 = ((bf16[4,256,640]{2,1,0:T(8,128)(2,1)}), bf16[4,256,640]{2,1,0:T(8,128)(2,1)S(1)}, u32[]{:S(2)}, u32[]{:S(2)}) async-start(bf16[4,256,640]{2,1,0:T(8,128)(2,1)} %broadcast_in_dim.36), calls=%async_computation.3 | async-start | bytes 2621440 | tf_op jit(solution)/shard_map/all_to_all | solution.py:143

commit v16 on v12

--- a/solution.py
+++ b/solution.py
@@ -136,28 +136,19 @@
     placed = placed.astype(jnp.bfloat16)
     in_plane = lax.all_to_all(placed, PLANE, 0, 0, tiled=True)
     ys = group_size // plane
+    in_plane = in_plane.reshape(-1, width)
     arrived = lax.all_to_all(
         jnp.broadcast_to(in_plane[None], (ys,) + in_plane.shape), "y", 0, 0, tiled=True
-    ).reshape(-1, in_plane.shape[1])
+    ).reshape(-1, width)
 
     src_start = all_start.reshape(group_size, series_here)
     src_len = all_len.reshape(group_size, series_here)
     src_t = (me - src_start) % group_size
     src_row = (src_start + src_t) // group_size
     src_row = jnp.where(src_t < src_len, src_row, -1)
-    out_row = jnp.arange(rows_here, dtype=jnp.int32)[:, None, None, None]
-    hit = src_row[None, :, :, None] == out_row
-    result = jnp.concatenate(
-        [
-            jnp.dot(
-                (hit & (halves.reshape(1, 1, 1, 2) == h)).reshape(rows_here, -1).astype(jnp.bfloat16),
-                arrived,
-                preferred_element_type=jnp.float32,
-            )
-            for h in range(2)
-        ],
-        axis=1,
-    )
+    out_row = jnp.arange(rows_here, dtype=jnp.int32)[:, None]
+    gather = (src_row.reshape(1, -1) == out_row).astype(jnp.bfloat16)
+    result = jnp.dot(gather, arrived, preferred_element_type=jnp.float32)
     return result.astype(jnp.bfloat16)
 
 

time: 75 us -> 74.5 us (level)
  other arithmetic: 3.51 us -> 1.95 us
  waiting for transfers between devices: 13.2 us -> 14.5 us
    all_to_all x1, waiting for transfers between devices: 12.4 us -> 13.8 us  [local(): lax.all_to_all(jnp.broadcast_to(in_plane[None], (ys,) + in_plane.shape),...]
    concatenate x1 -> x0, other arithmetic: 0.75 us -> none  [local(): jnp.concatenate([jnp.dot((hit & (halves.reshape(1, 1, 1, 2) == h)).reshap...]
  transfers between devices with their start and end apart: 2 -> 2, of which waited for: 2 -> 2; matrix products, arithmetic and copies ran while one was open for 4% -> 2% of each run, Pallas kernels for 12% -> 12%
where the time goes in v16:
time: 74.5 us; the launch traced here: 73.9 us
  blocking collectives  22.1 us (30%)
  starting transfers between devices  20.5 us (28%)
  waiting for transfers between devices  14.5 us (19%)
  Pallas kernels  8.93 us (12%)
  local copies, waits for them, and re-layouts  3.31 us (4%)
  matrix products  2.57 us (3%)
  other arithmetic  1.95 us (3%)
    all_to_all x1, blocking collectives, local(): in_plane = lax.all_to_all(placed, PLANE, 0, 0, tiled=True)  22.1 us
    all_to_all x1, starting transfers between devices, local(): gathered = lax.all_to_all(info, REQ, 0, 0, tiled=True)  15.4 us
    all_to_all x1, waiting for transfers between devices, local(): lax.all_to_all(jnp.broadcast_to(in_plane[None], (ys,) + in_plane.shape),...  13.8 us
    pallas_call x1, Pallas kernels, layer_block(): pl.pallas_call(block_kernel, in_specs=[pl.BlockSpec(memory_space=pltpu.SM...  8.93 us
    all_to_all x1, starting transfers between devices, local(): lax.all_to_all(jnp.broadcast_to(in_plane[None], (ys,) + in_plane.shape),...  5.01 us
    dot_general x2, matrix products, local(): jnp.dot(pick_h, layer_out[:, h * half:(h + 1) * half], preferred_element_...  1.49 us
  transfers between devices with their start and end apart: 2, of which 2 were waited for; matrix products, arithmetic and copies ran while one was open for 2% of the time, Pallas kernels for 12%

profile of v16, /device:TPU:8, one launch (start us, length us, event | category | flops | bytes accessed | tf_op | source)
XLA Modules:
  0.0 73.9 jit_solution(17363909163473837788)
XLA Ops:
  0.0 0.7 %pad_add_fusion = s32[8]{0:T(128)S(1)} fusion(s32[4]{0:T(128)} %param.14, s32[4]{0:T(128)} %param.12), kind=kLoop, calls=%fused_computation.39 | loop fusion | flops 8 | bytes 64 | tf_op jit(solution)/shard_map/concatenate | solution.py:107
  0.7 0.6 broadcast.129.clone
  1.4 15.4 %all-to-all-start = ((s32[128,1,8]{2,1,0:T(1,128)}), s32[128,1,8]{2,1,0:T(1,128)S(1)}, u32[]{:S(2)}, u32[]{:S(2)}) async-start(s32[128,1,8]{2,1,0:T(1,128)} %bitcast), calls=%async_computation | async-start | bytes 131072 | tf_op jit(solution)/shard_map/all_to_all | solution.py:111
  16.8 0.7 iota_compare_fusion.4
  17.6 0.1 and.107
  17.7 0.1 and.108
  17.8 0.1 and.118
  17.9 0.1 and.114
  18.1 8.9 %shard_map.91 = bf16[128,1280]{1,0:T(8,128)(2,1)} custom-call(s32[4]{0:T(128)} %cache_len_ref.1, bf16[4,32,3840]{2,1,0:T(8,128)(2,1)} %qkv_ref.1, bf16[4,32,2560]{2,1,0:T(8,128)(2,1)} %cache_ref.1, bf16[4,32,1280]{2,1,0:T(8,128)(2,1)} %resid_ref.1, f32[1280]{0:T(1024)} %gain_ref.1, bf16[1280,1280]{1,0:T(8,128)(2,1)} %up_hbm.1, bf16[1280,1280]{1,0:T(8,128)(2,1)} %down_hbm.1), custom_call_target="tpu_custom_call" | custom-call | tf_op jit(solution)/shard_map/pallas_call | solution.py:82
  27.0 0.0 copy-start
  27.0 0.7 all-to-all-done
  27.7 0.1 fusion.20
  27.8 0.1 lt.51
  27.9 0.1 broadcast_in_dim.25
  28.0 0.3 select_reduce_fusion
  28.3 0.1 dynamic_slice.3
  28.4 0.1 fusion.14
  28.5 0.1 and.105
  28.6 0.1 and.106
  28.7 0.1 and.111
  28.8 0.1 and.112
  28.9 1.2 %fusion.3 = f32[256,640]{1,0:T(8,128)S(1)} fusion(bf16[128,1280]{1,0:T(8,128)(2,1)} %shard_map.91, pred[256,128]{1,0:T(32,128)(4,1)S(1)} %and.112, pred[256]{0:T(512)(128)(4,1)S(1)} %and.114), kind=kOutput, calls=%fused_computation.7 | convolution fusion | flops 41975808 | bytes 852224 | tf_op jit(solution)/shard_map/dot_general | solution.py:133
  30.1 0.0 copy-done
  30.1 0.3 fusion.1
  30.4 22.1 %all_to_all.26 = bf16[32,8,640]{2,1,0:T(8,128)(2,1)S(1)} all-to-all(bf16[32,8,640]{2,1,0:T(8,128)(2,1)S(1)} %fusion.1), channel_id=1, replica_groups=mesh['grp'=2,'y'=4,'z'=8,'x'=4] {'z','x'}, dimensions={0} | all-to-all | bytes 655360 | tf_op jit(solution)/shard_map/all_to_all | solution.py:137
  52.5 0.1 broadcast_in_dim.28
  52.6 1.1 %broadcast_in_dim.30 = bf16[4,128,1280]{2,1,0:T(8,128)(2,1)} broadcast(bf16[128,1280]{1,0:T(8,128)(2,1)S(1)} %broadcast_in_dim.28), dimensions={1,2} | broadcast | bytes 1638400 | tf_op jit(solution)/shard_map/broadcast_in_dim | solution.py:141
  53.8 5.0 %all-to-all-start.2 = ((bf16[4,128,1280]{2,1,0:T(8,128)(2,1)}), bf16[4,128,1280]{2,1,0:T(8,128)(2,1)S(1)}, u32[]{:S(2)}, u32[]{:S(2)}) async-start(bf16[4,128,1280]{2,1,0:T(8,128)(2,1)} %broadcast_in_dim.30), calls=%async_computation.2 | async-start | bytes 2621440 | tf_op jit(solution)/shard_map/all_to_all | solution.py:140
  58.8 0.1 reshape.123
  58.9 0.1 fusion.10
  59.0 0.1 eq.70
  59.1 13.8 %all-to-all-done.2 = bf16[4,128,1280]{2,1,0:T(8,128)(2,1)S(1)} async-done(((bf16[4,128,1280]{2,1,0:T(8,128)(2,1)}), bf16[4,128,1280]{2,1,0:T(8,128)(2,1)S(1)}, u32[]{:S(2)}, u32[]{:S(2)}) %all-to-all-start.2) | async-done | bytes 1310752 | tf_op jit(solution)/shard_map/all_to_all | solution.py:140
  72.8 1.1 %convolution_convert_fusion = bf16[128,1280]{1,0:T(8,128)(2,1)} fusion(bf16[512,1280]{1,0:T(8,128)(2,1)S(1)} %bitcast.9, s32[512]{0:T(512)S(1)} %eq.70), kind=kOutput, calls=%fused_computation | convolution fusion | flops 168001536 | bytes 1640448 | tf_op jit(solution)/shard_map/dot_general | solution.py:151
  (8 shorter events, 0.1 us)
Async XLA Ops:
  1.4 26.3 %all-to-all-start = ((s32[128,1,8]{2,1,0:T(1,128)}), s32[128,1,8]{2,1,0:T(1,128)S(1)}, u32[]{:S(2)}, u32[]{:S(2)}) async-start(s32[128,1,8]{2,1,0:T(1,128)} %bitcast), calls=%async_computation | async-start | bytes 131072 | tf_op jit(solution)/shard_map/all_to_all | solution.py:111
  27.0 3.1 %copy-start = (bf16[128,1280]{1,0:T(8,128)(2,1)S(1)}, bf16[128,1280]{1,0:T(8,128)(2,1)}, u32[]{:S(2)}) copy-start(bf16[128,1280]{1,0:T(8,128)(2,1)} %shard_map.91) | copy-start | bytes 983044
  53.8 19.1 %all-to-all-start.2 = ((bf16[4,128,1280]{2,1,0:T(8,128)(2,1)}), bf16[4,128,1280]{2,1,0:T(8,128)(2,1)S(1)}, u32[]{:S(2)}, u32[]{:S(2)}) async-start(bf16[4,128,1280]{2,1,0:T(8,128)(2,1)} %broadcast_in_dim.30), calls=%async_computation.2 | async-start | bytes 2621440 | tf_op jit(solution)/shard_map/all_to_all | solution.py:140
